TPU v7x, 768 devices: a whole 4x8x12 slice. The times are simulated.
768 devices in a mesh: lat: 16 (over x_hi, y), lon: 24 (over z, core), pipe: 2 (over x_lo).
Axes of the slice: x: 4 (x_hi: 2, x_lo: 2; x = x_hi * 2 + x_lo), y: 8, z: 12, core: 2. Of those that a mesh axis runs over, the one named last changes fastest.
Arguments:
- queries_keys: bfloat16 [2, 2, 256, 192, 1536], P('pipe', None, 'lat', 'lon'), may hold values from -30 to 30
- values: bfloat16 [2, 256, 192, 1536], P('pipe', 'lat', 'lon'), may hold values from -6 to 6
- cotangent: bfloat16 [256, 192, 1536], P('lat', 'lon'), may hold values from -6 to 6
Outputs:
- activations: bfloat16 [2, 256, 192, 1536], P('pipe', 'lat', 'lon')
- grad_queries_keys: bfloat16 [2, 2, 256, 192, 1536], P('pipe', None, 'lat', 'lon')
- grad_values: bfloat16 [2, 256, 192, 1536], P('pipe', 'lat', 'lon')
All inputs are finite; a program needn't handle non-finite values.
Results may differ from a plain program's by a relative error of at most 0.0063.
Values may be sent and summed in bfloat16 or wider, within the bound.
No kernel may reach another device: no remote copies, remote signals or barrier semaphores. Data moves between devices by JAX's collectives and lax.ppermute only.
A program may use at most 64 MiB of HBM per device.

v0:
```python
import math

import jax
import jax.numpy as jnp
from jax import lax
from jax.sharding import PartitionSpec as P

HEADS = 12
MARGIN = 2


NEGATIVE = -1e30


def padded(shard, sides, width):
    for axis, dim in sides:
        peers, length = (lax.axis_size(axis), shard.shape[dim])
        up = [(i, (i + 1) % peers) for i in range(peers)]
        down = [(j, i) for i, j in up]
        last = lax.slice_in_dim(shard, length - width, length, axis=dim)
        initial = lax.slice_in_dim(shard, 0, width, axis=dim)
        before = lax.ppermute(last, axis, up)
        after = lax.ppermute(initial, axis, down)
        shard = jnp.concatenate([before, shard, after], axis=dim)
    return shard


def shifted(value, axis, steps):
    count = lax.axis_size(axis)
    initial, last = (max(0, -steps), min(count, count - steps))
    return lax.ppermute(value, axis, [(source, source + steps) for source in range(initial, last)])


def softmax_rows(query_head, key_head, allowed, scaling):
    scores = jnp.dot(query_head, key_head.T, preferred_element_type=jnp.float32) * scaling
    scores = jnp.where(allowed[None, :], scores, NEGATIVE)
    highest = jnp.max(scores, axis=1, keepdims=True)
    weights = jnp.exp(scores - highest)
    return weights / jnp.sum(weights, axis=1, keepdims=True)


def head_forward(query_head, key_head, value_head, allowed, scaling):
    weights = softmax_rows(query_head, key_head, allowed, scaling)
    return jnp.dot(
        weights.astype(jnp.bfloat16), value_head, preferred_element_type=jnp.float32
    ).astype(jnp.bfloat16)


def head_backward(query_head, key_head, value_head, upstream_head, allowed, scaling):
    weights = softmax_rows(query_head, key_head, allowed, scaling)
    weights_low = weights.astype(jnp.bfloat16)
    dweights = jnp.dot(upstream_head, value_head.T, preferred_element_type=jnp.float32)
    inner = jnp.sum(weights * dweights, axis=1, keepdims=True)
    dscore = (weights * (dweights - inner) * scaling).astype(jnp.bfloat16)
    grad_query = jnp.dot(dscore, key_head, preferred_element_type=jnp.float32).astype(jnp.bfloat16)
    grad_key = jnp.dot(dscore.T, query_head, preferred_element_type=jnp.float32)
    grad_value = jnp.dot(weights_low.T, upstream_head, preferred_element_type=jnp.float32)
    return (grad_query, grad_key, grad_value)


def split_heads(field, heads):
    return field.reshape(field.shape[0], heads, -1).transpose(1, 0, 2)


def join_heads(field):
    return field.transpose(1, 0, 2).reshape(field.shape[1], -1)


def tile_forward(queries, keys_ext, values_ext, allowed, heads):
    scaling = 1.0 / math.sqrt(queries.shape[1] // heads)

    def one_head(operands):
        return head_forward(operands[0], operands[1], operands[2], allowed, scaling)

    result = lax.map(
        one_head,
        (split_heads(queries, heads), split_heads(keys_ext, heads), split_heads(values_ext, heads)),
    )
    return join_heads(result)


def tile_backward(queries, keys_ext, values_ext, upstream, allowed, heads):
    scaling = 1.0 / math.sqrt(queries.shape[1] // heads)

    def one_head(operands):
        return head_backward(operands[0], operands[1], operands[2], operands[3], allowed, scaling)

    result = lax.map(
        one_head,
        (
            split_heads(queries, heads),
            split_heads(keys_ext, heads),
            split_heads(values_ext, heads),
            split_heads(upstream, heads),
        ),
    )
    return (join_heads(result[0]), join_heads(result[1]), join_heads(result[2]))


def gather_margin(stacked):
    return padded(stacked, (("lat", 0), ("lon", 1)), MARGIN)


def return_margin(ext):
    margin = MARGIN
    rows_ext = ext.shape[0]
    cols_ext = ext.shape[1]
    tile_rows = rows_ext - 2 * margin
    tile_cols = cols_ext - 2 * margin
    sent = ext.astype(jnp.bfloat16)
    own = ext[margin : margin + tile_rows, margin : margin + tile_cols]
    got = padded(sent, (("lat", 0), ("lon", 1)), margin)
    upper = got[:margin].astype(jnp.float32)
    lower = got[tile_rows + 3 * margin :].astype(jnp.float32)
    middle = got[2 * margin : 2 * margin + tile_rows].astype(jnp.float32)
    tail = upper.shape[2:]
    gap_cols = jnp.zeros((margin, tile_cols - 2 * margin) + tail, jnp.float32)
    upper_band = upper[:, 2 * margin : 2 * margin + tile_cols] + jnp.concatenate(
        [upper[:, :margin], gap_cols, upper[:, tile_cols + 3 * margin :]], axis=1
    )
    lower_band = lower[:, 2 * margin : 2 * margin + tile_cols] + jnp.concatenate(
        [lower[:, :margin], gap_cols, lower[:, tile_cols + 3 * margin :]], axis=1
    )
    gap_rows = jnp.zeros((tile_rows - 2 * margin, tile_cols) + tail, jnp.float32)
    side_gap = jnp.zeros((tile_rows, tile_cols - 2 * margin) + tail, jnp.float32)
    row_term = jnp.concatenate([upper_band, gap_rows, lower_band], axis=0)
    col_term = jnp.concatenate(
        [middle[:, :margin], side_gap, middle[:, tile_cols + 3 * margin :]], axis=1
    )
    return own + row_term + col_term


def body(queries_keys, values, cotangent):
    section_count = lax.axis_size("pipe")
    section_index = lax.axis_index("pipe")
    tile_rows, tile_cols, features = cotangent.shape
    margin = MARGIN
    rows_ext = tile_rows + 2 * margin
    cols_ext = tile_cols + 2 * margin
    window_size = rows_ext * cols_ext
    token_count = tile_rows * tile_cols
    queries = queries_keys[0, 0].reshape(token_count, features)
    key_tile = queries_keys[0, 1]
    value_tile = values[0]
    lat_rows = lax.axis_index("lat") * tile_rows - margin + jnp.arange(rows_ext, dtype=jnp.int32)
    inside = (lat_rows >= 0) & (lat_rows < tile_rows * lax.axis_size("lat"))
    allowed = jnp.broadcast_to(inside[:, None], (rows_ext, cols_ext)).reshape(window_size)

    def run_forward(window):
        keys_ext = window[:, :, 0].reshape(window_size, features)
        values_ext = window[:, :, 1].reshape(window_size, features)
        return tile_forward(queries, keys_ext, values_ext, allowed, HEADS).reshape(
            tile_rows, tile_cols, features
        )

    def skip_forward(window):
        return jnp.zeros((tile_rows, tile_cols, features), jnp.bfloat16)

    def run_backward(operands):
        window, upstream = operands
        keys_ext = window[:, :, 0].reshape(window_size, features)
        values_ext = window[:, :, 1].reshape(window_size, features)
        return tile_backward(
            queries, keys_ext, values_ext, upstream.reshape(token_count, features), allowed, HEADS
        )

    def skip_backward(operands):
        return (
            jnp.zeros((token_count, features), jnp.bfloat16),
            jnp.zeros((window_size, features), jnp.float32),
            jnp.zeros((window_size, features), jnp.float32),
        )

    received = jnp.zeros_like(value_tile)
    outputs = jnp.zeros_like(value_tile)
    stored = jnp.zeros((rows_ext, cols_ext, 2, features), jnp.bfloat16)
    for turn_index in range(section_count):
        inputs = (value_tile.astype(jnp.float32) + received.astype(jnp.float32)).astype(
            jnp.bfloat16
        )
        window = gather_margin(jnp.stack([key_tile, inputs], axis=2))
        active = section_index == turn_index
        context = lax.cond(active, run_forward, skip_forward, window)
        outputs = jnp.where(active, context, outputs)
        stored = jnp.where(active, window, stored)
        if turn_index + 1 < section_count:
            received = shifted(context, "pipe", 1)
    grad_query = jnp.zeros_like(value_tile)
    grad_key = jnp.zeros_like(value_tile)
    grad_value = jnp.zeros_like(value_tile)
    returned = cotangent
    for turn_index in reversed(range(section_count)):
        active = section_index == turn_index
        incoming = cotangent if turn_index == section_count - 1 else returned
        query_term, key_term, value_term = lax.cond(
            active, run_backward, skip_backward, (stored, incoming)
        )
        ext = jnp.stack(
            [
                key_term.reshape(rows_ext, cols_ext, features),
                value_term.reshape(rows_ext, cols_ext, features),
            ],
            axis=2,
        )
        owned = return_margin(ext).astype(jnp.bfloat16)
        grad_query = jnp.where(
            active, query_term.reshape(tile_rows, tile_cols, features), grad_query
        )
        grad_key = jnp.where(active, owned[:, :, 0], grad_key)
        grad_value = jnp.where(active, owned[:, :, 1], grad_value)
        if turn_index > 0:
            returned = shifted(owned[:, :, 1], "pipe", -1)
    return (outputs[None], jnp.stack([grad_query, grad_key], axis=0)[None], grad_value[None])


def solution(mesh):
    in_specs = (
        P("pipe", None, "lat", "lon", None),
        P("pipe", "lat", "lon", None),
        P("lat", "lon", None),
    )
    out_specs = (
        P("pipe", "lat", "lon", None),
        P("pipe", None, "lat", "lon", None),
        P("pipe", "lat", "lon", None),
    )
    return jax.shard_map(body, mesh=mesh, in_specs=in_specs, out_specs=out_specs, check_vma=False)
```

profile of v0, /device:TPU:60, one launch (start us, length us, event | category | flops | bytes accessed | tf_op | source)
XLA Modules:
  0.0 360.2 jit_solution(14425323020179400021)
XLA Ops:
  3.3 3.2 collective-permute-start.1
  6.6 9.3 %collective-permute-start = (bf16[2,8,2,1536]{3,1,0,2:T(8,128)(2,1)S(1)}, bf16[2,8,2,1536]{3,1,0,2:T(8,128)(2,1)S(1)}, u32[]{:S(2)}, u32[]{:S(2)}) collective-permute-start(bf16[2,8,2,1536]{3,1,0,2:T(8,128)(2,1)S(1)} %get-tuple-element.379), channel_id=1, source_target_pairs={{0,48},{48,96},{96,144},{144,192},{192,240},{240,288},{288,336},{3... | collective-permute-start | bytes 294920 | tf_op jit(solution)/shard_map/ppermute | solution.py:22
  18.7 7.9 %collective-permute-start.3 = (bf16[20,2,2,1536]{3,1,0,2:T(2,128)(2,1)S(1)}, bf16[20,2,2,1536]{3,1,0,2:T(2,128)(2,1)}, u32[]{:S(2)}, u32[]{:S(2)}) collective-permute-start(bf16[20,2,2,1536]{3,1,0,2:T(2,128)(2,1)S(1)} %get-tuple-element.374), channel_id=1, source_target_pairs={{2,0},{4,2},{6,4},{8,6},{10,8},{12,10},{14,12},{16,14},{18,16},{20... | collective-permute-start | bytes 737288 | tf_op jit(solution)/shard_map/ppermute | solution.py:23
  26.6 3.9 %collective-permute-done.2 = bf16[20,2,2,1536]{3,1,0,2:T(2,128)(2,1)S(1)} collective-permute-done((bf16[20,2,2,1536]{3,1,0,2:T(2,128)(2,1)S(1)}, bf16[20,2,2,1536]{3,1,0,2:T(2,128)(2,1)S(1)}, u32[]{:S(2)}, u32[]{:S(2)}) %collective-permute-start.2) | collective-permute-done | bytes 245792 | tf_op jit(solution)/shard_map/ppermute | solution.py:22
  30.5 2.4 fusion.89
  33.6 33.0 %conditional.4 = (bf16[16,8,1536]{2,1,0:T(8,128)(2,1)S(1)}) conditional(s32[]{:T(128)} %convert_element_type.89, () %tuple.65, (bf16[1,1,16,8,1536]{4,3,2,1,0:T(8,128)(2,1)S(1)}, bf16[20,12,2,1536]{3,1,0,2:T(8,128)(2,1)S(1)}, pred[20,12]{1,0:T(8,128)(4,1)}) %tuple.66), branch_computations={%region_0.0_spmd, %region_1.6_spmd} | conditional | flops 15990530 | bytes 15505065 | solution.py:183
  41.7 23.3 %while.48 = (s32[]{:T(128)}, bf16[12,128,128]{2,1,0:T(8,128)(2,1)}, pred[20,12]{1,0:T(8,128)(4,1)}, bf16[12,128,128]{2,1,0:T(8,128)(2,1)S(1)}, bf16[12,240,128]{...) while((s32[]{:T(128)}, bf16[12,128,128]{2,1,0:T(8,128)(2,1)}, ...), condition=%wide.wide.region_5.5_spmd, body=%wide.wide.region_2.4_spmd.sunk | while | flops 15990530 | bytes 562269 | solution.py:75
  67.9 5.2 %collective-permute-done.4 = bf16[16,8,1536]{2,1,0:T(8,128)(2,1)S(1)} collective-permute-done((bf16[16,8,1536]{2,1,0:T(8,128)(2,1)S(1)}, bf16[16,8,1536]{2,1,0:T(8,128)(2,1)S(1)}, u32[]{:S(2)}, u32[]{:S(2)}) %collective-permute-start.4) | collective-permute-done | bytes 393248 | tf_op jit(solution)/shard_map/ppermute | solution.py:31
  74.1 8.7 %collective-permute-start.5 = (bf16[2,8,2,1536]{3,1,0,2:T(8,128)(2,1)S(1)}, bf16[2,8,2,1536]{3,1,0,2:T(8,128)(2,1)S(1)}, u32[]{:S(2)}, u32[]{:S(2)}) collective-permute-start(bf16[2,8,2,1536]{3,1,0,2:T(8,128)(2,1)S(1)} %get-tuple-element.377), channel_id=1, source_target_pairs={{0,48},{48,96},{96,144},{144,192},{192,240},{240,288},{288,336},{3... | collective-permute-start | bytes 294920 | tf_op jit(solution)/shard_map/ppermute | solution.py:22
  82.8 1.9 collective-permute-start.6
  85.0 7.9 %collective-permute-done.6 = bf16[2,8,2,1536]{3,1,0,2:T(8,128)(2,1)S(1)} collective-permute-done((bf16[2,8,2,1536]{3,1,0,2:T(8,128)(2,1)S(1)}, bf16[2,8,2,1536]{3,1,0,2:T(8,128)(2,1)S(1)}, u32[]{:S(2)}, u32[]{:S(2)}) %collective-permute-start.6) | collective-permute-done | bytes 98336 | tf_op jit(solution)/shard_map/ppermute | solution.py:23
  93.6 3.1 collective-permute-start.8
  96.7 3.9 %collective-permute-done.7 = bf16[20,2,2,1536]{3,1,0,2:T(2,128)(2,1)S(1)} collective-permute-done((bf16[20,2,2,1536]{3,1,0,2:T(2,128)(2,1)S(1)}, bf16[20,2,2,1536]{3,1,0,2:T(2,128)(2,1)S(1)}, u32[]{:S(2)}, u32[]{:S(2)}) %collective-permute-start.7) | collective-permute-done | bytes 245792 | tf_op jit(solution)/shard_map/ppermute | solution.py:22
  101.2 4.9 %select_select_fusion = (bf16[20,12,2,1536]{3,1,0,2:T(8,128)(2,1)S(1)}, bf16[20,12,2,1536]{3,1,0,2:T(8,128)(2,1)}) fusion(pred[]{:T(512)S(6)} %eq.9, pred[]{:T(512)S(6)} %eq.8, bf16[20,2,2,1536]{3,1,0,2:T(2,128)(2,1)} %collective-permute-done.8, bf16[2,8,2,1536]{3,1,0,2:T(8,128)(2,1)} %copy-done.12, bf16[16,8,1,1536]{3,1,0,2:T(8,128)(2,1)S(1)} %fusion.103, ...), kind=kLoop, calls=%fused_computation.116 | loop fusion | flops 18432000 | bytes 5505026 | tf_op jit(solution)/shard_map/jit(_where)/select_n | solution.py:185
  106.2 3.9 %conditional.6 = (bf16[1,16,8,1536]{3,2,1,0:T(8,128)(2,1)}, f32[20,12,1,1536]{3,1,0,2:T(8,128)}, f32[20,12,1,1536]{3,1,0,2:T(8,128)}) conditional(s32[]{:T(128)} %convert_element_type.86, () %tuple.69, (bf16[1,1,16,8,1536]{4,3,2,1,0:T(8,128)(2,1)S(1)}, bf16[20,12,2,1536]{3,1,0,2:T(8,128)(2,1)S(1)}, bf16[16,8,1536]{2,1,0:T(8,128)(2,1)}, ...), branch_computations={%region_12.13_spmd, %region_13.19_spmd} | conditional | flops 39890560 | bytes 28585432 | solution.py:195
  113.9 1.9 collective-permute-start.9
  115.8 3.9 %collective-permute-start.10 = (bf16[2,12,2,1536]{3,1,0,2:T(8,128)(2,1)S(1)}, bf16[2,12,2,1536]{3,1,0,2:T(8,128)(2,1)S(1)}, u32[]{:S(2)}, u32[]{:S(2)}) collective-permute-start(bf16[2,12,2,1536]{3,1,0,2:T(8,128)(2,1)S(1)} %get-tuple-element.366), channel_id=1, source_target_pairs={{48,0},{96,48},{144,96},{192,144},{240,192},{288,240},{336,288},{3... | collective-permute-start | bytes 442376 | tf_op jit(solution)/shard_map/ppermute | solution.py:23
  121.4 5.5 %collective-permute-done.10 = bf16[2,12,2,1536]{3,1,0,2:T(8,128)(2,1)S(1)} collective-permute-done((bf16[2,12,2,1536]{3,1,0,2:T(8,128)(2,1)S(1)}, bf16[2,12,2,1536]{3,1,0,2:T(8,128)(2,1)S(1)}, u32[]{:S(2)}, u32[]{:S(2)}) %collective-permute-start.10) | collective-permute-done | bytes 147488 | tf_op jit(solution)/shard_map/ppermute | solution.py:23
  127.5 2.9 collective-permute-start.12
  130.6 4.2 %collective-permute-done.11 = bf16[24,2,2,1536]{3,1,0,2:T(2,128)(2,1)S(1)} collective-permute-done((bf16[24,2,2,1536]{3,1,0,2:T(2,128)(2,1)S(1)}, bf16[24,2,2,1536]{3,1,0,2:T(2,128)(2,1)S(1)}, u32[]{:S(2)}, u32[]{:S(2)}) %collective-permute-start.11) | collective-permute-done | bytes 294944 | tf_op jit(solution)/shard_map/ppermute | solution.py:22
  139.1 113.9 %collective-permute-done.13 = bf16[16,8,1536]{2,1,0:T(8,128)(2,1)} collective-permute-done((bf16[16,8,1536]{2,1,0:T(8,128)(2,1)}, bf16[16,8,1536]{2,1,0:T(8,128)(2,1)}, u32[]{:S(2)}, u32[]{:S(2)}) %collective-permute-start.13) | collective-permute-done | bytes 393248 | tf_op jit(solution)/shard_map/ppermute | solution.py:31
  253.0 75.9 %conditional.7 = (bf16[1,16,8,1536]{3,2,1,0:T(8,128)(2,1)S(1)}, f32[20,12,1,1536]{3,1,0,2:T(8,128)}, f32[20,12,1,1536]{3,1,0,2:T(8,128)}) conditional(s32[]{:T(128)} %convert_element_type.89, () %tuple.68, (bf16[1,1,16,8,1536]{4,3,2,1,0:T(8,128)(2,1)S(1)}, bf16[20,12,2,1536]{3,1,0,2:T(8,128)(2,1)S(1)}, bf16[16,8,1536]{2,1,0:T(8,128)(2,1)}, ...), branch_computations={%region_19.20_spmd, %region_20.26_spmd} | conditional | flops 39890560 | bytes 29961960 | solution.py:195
  256.0 2.1 reshape.118
  258.1 1.9 copy.36
  265.2 55.3 %while.51 = (s32[]{:T(128)}, bf16[12,128,128]{2,1,0:T(8,128)(2,1)}, f32[12,240,128]{2,1,0:T(8,128)}, f32[12,240,128]{2,1,0:T(8,128)}, pred[20,12]{1,0:T(8,128)(4...) while((s32[]{:T(128)}, bf16[12,128,128]{2,1,0:T(8,128)(2,1)}, ...), condition=%wide.wide.region_25.25_spmd, body=%wide.wide.region_21.24_spmd.sunk | while | flops 39890560 | bytes 1649781 | solution.py:88
  322.0 1.9 copy.40
  325.5 1.9 copy.39
  332.8 1.9 collective-permute-start.14
  334.7 4.2 %collective-permute-start.15 = (bf16[2,12,2,1536]{3,1,0,2:T(8,128)(2,1)S(1)}, bf16[2,12,2,1536]{3,1,0,2:T(8,128)(2,1)S(1)}, u32[]{:S(2)}, u32[]{:S(2)}) collective-permute-start(bf16[2,12,2,1536]{3,1,0,2:T(8,128)(2,1)S(1)} %get-tuple-element.364), channel_id=1, source_target_pairs={{48,0},{96,48},{144,96},{192,144},{240,192},{288,240},{336,288},{3... | collective-permute-start | bytes 442376 | tf_op jit(solution)/shard_map/ppermute | solution.py:23
  340.3 5.5 %collective-permute-done.15 = bf16[2,12,2,1536]{3,1,0,2:T(8,128)(2,1)S(1)} collective-permute-done((bf16[2,12,2,1536]{3,1,0,2:T(8,128)(2,1)S(1)}, bf16[2,12,2,1536]{3,1,0,2:T(8,128)(2,1)S(1)}, u32[]{:S(2)}, u32[]{:S(2)}) %collective-permute-start.15) | collective-permute-done | bytes 147488 | tf_op jit(solution)/shard_map/ppermute | solution.py:23
  346.4 5.7 %collective-permute-start.17 = (bf16[24,2,2,1536]{3,1,0,2:T(2,128)(2,1)S(1)}, bf16[24,2,2,1536]{3,1,0,2:T(2,128)(2,1)S(1)}, u32[]{:S(2)}, u32[]{:S(2)}) collective-permute-start(bf16[24,2,2,1536]{3,1,0,2:T(2,128)(2,1)S(1)} %get-tuple-element.360), channel_id=1, source_target_pairs={{2,0},{4,2},{6,4},{8,6},{10,8},{12,10},{14,12},{16,14},{18,16},{20... | collective-permute-start | bytes 884744 | tf_op jit(solution)/shard_map/ppermute | solution.py:23
  352.2 4.3 %collective-permute-done.16 = bf16[24,2,2,1536]{3,1,0,2:T(2,128)(2,1)S(1)} collective-permute-done((bf16[24,2,2,1536]{3,1,0,2:T(2,128)(2,1)S(1)}, bf16[24,2,2,1536]{3,1,0,2:T(2,128)(2,1)S(1)}, u32[]{:S(2)}, u32[]{:S(2)}) %collective-permute-start.16) | collective-permute-done | bytes 294944 | tf_op jit(solution)/shard_map/ppermute | solution.py:22
  (233 shorter events, 134.8 us)
Async XLA Ops:
  0.6 17.4 %copy-start = (bf16[1,16,8,1536]{3,2,1,0:T(8,128)(2,1)S(1)}, bf16[1,16,8,1536]{3,2,1,0:T(8,128)(2,1)}, u32[]{:S(2)}) copy-start(bf16[1,16,8,1536]{3,2,1,0:T(8,128)(2,1)} %param.20) | copy-start | bytes 1179652
  3.3 13.2 %collective-permute-start.1 = (bf16[2,8,2,1536]{3,1,0,2:T(8,128)(2,1)S(1)}, bf16[2,8,2,1536]{3,1,0,2:T(8,128)(2,1)S(1)}, u32[]{:S(2)}, u32[]{:S(2)}) collective-permute-start(bf16[2,8,2,1536]{3,1,0,2:T(8,128)(2,1)S(1)} %get-tuple-element.323), channel_id=1, source_target_pairs={{48,0},{96,48},{144,96},{192,144},{240,192},{288,240},{336,288},{3... | collective-permute-start | bytes 294920 | tf_op jit(solution)/shard_map/ppermute | solution.py:23
  6.6 11.5 %collective-permute-start = (bf16[2,8,2,1536]{3,1,0,2:T(8,128)(2,1)S(1)}, bf16[2,8,2,1536]{3,1,0,2:T(8,128)(2,1)S(1)}, u32[]{:S(2)}, u32[]{:S(2)}) collective-permute-start(bf16[2,8,2,1536]{3,1,0,2:T(8,128)(2,1)S(1)} %get-tuple-element.379), channel_id=1, source_target_pairs={{0,48},{48,96},{96,144},{144,192},{192,240},{240,288},{288,336},{3... | collective-permute-start | bytes 294920 | tf_op jit(solution)/shard_map/ppermute | solution.py:22
  16.5 16.4 %copy-start.8 = (bf16[2,8,2,1536]{3,1,0,2:T(8,128)(2,1)}, bf16[2,8,2,1536]{3,1,0,2:T(8,128)(2,1)S(1)}, u32[]{:S(2)}) copy-start(bf16[2,8,2,1536]{3,1,0,2:T(8,128)(2,1)S(1)} %collective-permute-done.1) | copy-start | bytes 294916
  18.1 0.6 copy-start.9
  18.7 11.8 %collective-permute-start.2 = (bf16[20,2,2,1536]{3,1,0,2:T(2,128)(2,1)S(1)}, bf16[20,2,2,1536]{3,1,0,2:T(2,128)(2,1)S(1)}, u32[]{:S(2)}, u32[]{:S(2)}) collective-permute-start(bf16[20,2,2,1536]{3,1,0,2:T(2,128)(2,1)S(1)} %get-tuple-element.373), channel_id=1, source_target_pairs={{0,2},{2,4},{4,6},{6,8},{8,10},{10,12},{12,14},{14,16},{16,18},{18... | collective-permute-start | bytes 737288 | tf_op jit(solution)/shard_map/ppermute | solution.py:22
  18.7 11.8 %collective-permute-start.3 = (bf16[20,2,2,1536]{3,1,0,2:T(2,128)(2,1)S(1)}, bf16[20,2,2,1536]{3,1,0,2:T(2,128)(2,1)}, u32[]{:S(2)}, u32[]{:S(2)}) collective-permute-start(bf16[20,2,2,1536]{3,1,0,2:T(2,128)(2,1)S(1)} %get-tuple-element.374), channel_id=1, source_target_pairs={{2,0},{4,2},{6,4},{8,6},{10,8},{12,10},{14,12},{16,14},{18,16},{20... | collective-permute-start | bytes 737288 | tf_op jit(solution)/shard_map/ppermute | solution.py:23
  30.5 3.1 copy-start.7
  38.0 2.9 copy-start.1
  66.5 1.3 copy-start.3
  66.5 6.6 %collective-permute-start.4 = (bf16[16,8,1536]{2,1,0:T(8,128)(2,1)S(1)}, bf16[16,8,1536]{2,1,0:T(8,128)(2,1)S(1)}, u32[]{:S(2)}, u32[]{:S(2)}) collective-permute-start(bf16[16,8,1536]{2,1,0:T(8,128)(2,1)S(1)} %get-tuple-element.874), channel_id=1, source_target_pairs={{0,1},{2,3},{4,5},{6,7},{8,9},{10,11},{12,13},{14,15},{16,17},{18,... | collective-permute-start | bytes 1179656 | tf_op jit(solution)/shard_map/ppermute | solution.py:31
  74.1 10.9 %collective-permute-start.5 = (bf16[2,8,2,1536]{3,1,0,2:T(8,128)(2,1)S(1)}, bf16[2,8,2,1536]{3,1,0,2:T(8,128)(2,1)S(1)}, u32[]{:S(2)}, u32[]{:S(2)}) collective-permute-start(bf16[2,8,2,1536]{3,1,0,2:T(8,128)(2,1)S(1)} %get-tuple-element.377), channel_id=1, source_target_pairs={{0,48},{48,96},{96,144},{144,192},{192,240},{240,288},{288,336},{3... | collective-permute-start | bytes 294920 | tf_op jit(solution)/shard_map/ppermute | solution.py:22
  82.8 10.1 %collective-permute-start.6 = (bf16[2,8,2,1536]{3,1,0,2:T(8,128)(2,1)S(1)}, bf16[2,8,2,1536]{3,1,0,2:T(8,128)(2,1)S(1)}, u32[]{:S(2)}, u32[]{:S(2)}) collective-permute-start(bf16[2,8,2,1536]{3,1,0,2:T(8,128)(2,1)S(1)} %get-tuple-element.378), channel_id=1, source_target_pairs={{48,0},{96,48},{144,96},{192,144},{240,192},{288,240},{336,288},{3... | collective-permute-start | bytes 294920 | tf_op jit(solution)/shard_map/ppermute | solution.py:23
  85.0 8.4 %copy-start.11 = (bf16[2,8,2,1536]{3,1,0,2:T(8,128)(2,1)}, bf16[2,8,2,1536]{3,1,0,2:T(8,128)(2,1)S(1)}, u32[]{:S(2)}) copy-start(bf16[2,8,2,1536]{3,1,0,2:T(8,128)(2,1)S(1)} %collective-permute-done.5) | copy-start | bytes 294916
  93.0 0.6 copy-start.12
  93.6 6.9 %collective-permute-start.7 = (bf16[20,2,2,1536]{3,1,0,2:T(2,128)(2,1)S(1)}, bf16[20,2,2,1536]{3,1,0,2:T(2,128)(2,1)S(1)}, u32[]{:S(2)}, u32[]{:S(2)}) collective-permute-start(bf16[20,2,2,1536]{3,1,0,2:T(2,128)(2,1)S(1)} %get-tuple-element.371), channel_id=1, source_target_pairs={{0,2},{2,4},{4,6},{6,8},{8,10},{10,12},{12,14},{14,16},{16,18},{18... | collective-permute-start | bytes 737288 | tf_op jit(solution)/shard_map/ppermute | solution.py:22
  93.6 7.6 %collective-permute-start.8 = (bf16[20,2,2,1536]{3,1,0,2:T(2,128)(2,1)S(1)}, bf16[20,2,2,1536]{3,1,0,2:T(2,128)(2,1)}, u32[]{:S(2)}, u32[]{:S(2)}) collective-permute-start(bf16[20,2,2,1536]{3,1,0,2:T(2,128)(2,1)S(1)} %get-tuple-element.372), channel_id=1, source_target_pairs={{2,0},{4,2},{6,4},{8,6},{10,8},{12,10},{14,12},{16,14},{18,16},{20... | collective-permute-start | bytes 737288 | tf_op jit(solution)/shard_map/ppermute | solution.py:23
  100.5 0.7 copy-start.13
  113.9 7.6 %collective-permute-start.9 = (bf16[2,12,2,1536]{3,1,0,2:T(8,128)(2,1)S(1)}, bf16[2,12,2,1536]{3,1,0,2:T(8,128)(2,1)S(1)}, u32[]{:S(2)}, u32[]{:S(2)}) collective-permute-start(bf16[2,12,2,1536]{3,1,0,2:T(8,128)(2,1)S(1)} %get-tuple-element.365), channel_id=1, source_target_pairs={{0,48},{48,96},{96,144},{144,192},{192,240},{240,288},{288,336},{3... | collective-permute-start | bytes 442376 | tf_op jit(solution)/shard_map/ppermute | solution.py:22
  115.8 11.2 %collective-permute-start.10 = (bf16[2,12,2,1536]{3,1,0,2:T(8,128)(2,1)S(1)}, bf16[2,12,2,1536]{3,1,0,2:T(8,128)(2,1)S(1)}, u32[]{:S(2)}, u32[]{:S(2)}) collective-permute-start(bf16[2,12,2,1536]{3,1,0,2:T(8,128)(2,1)S(1)} %get-tuple-element.366), channel_id=1, source_target_pairs={{48,0},{96,48},{144,96},{192,144},{240,192},{288,240},{336,288},{3... | collective-permute-start | bytes 442376 | tf_op jit(solution)/shard_map/ppermute | solution.py:23
  127.5 7.4 %collective-permute-start.11 = (bf16[24,2,2,1536]{3,1,0,2:T(2,128)(2,1)S(1)}, bf16[24,2,2,1536]{3,1,0,2:T(2,128)(2,1)S(1)}, u32[]{:S(2)}, u32[]{:S(2)}) collective-permute-start(bf16[24,2,2,1536]{3,1,0,2:T(2,128)(2,1)S(1)} %get-tuple-element.361), channel_id=1, source_target_pairs={{0,2},{2,4},{4,6},{6,8},{8,10},{10,12},{12,14},{14,16},{16,18},{18... | collective-permute-start | bytes 884744 | tf_op jit(solution)/shard_map/ppermute | solution.py:22
  127.5 7.3 %collective-permute-start.12 = (bf16[24,2,2,1536]{3,1,0,2:T(2,128)(2,1)S(1)}, bf16[24,2,2,1536]{3,1,0,2:T(2,128)(2,1)S(1)}, u32[]{:S(2)}, u32[]{:S(2)}) collective-permute-start(bf16[24,2,2,1536]{3,1,0,2:T(2,128)(2,1)S(1)} %get-tuple-element.362), channel_id=1, source_target_pairs={{2,0},{4,2},{6,4},{8,6},{10,8},{12,10},{14,12},{16,14},{18,16},{20... | collective-permute-start | bytes 884744 | tf_op jit(solution)/shard_map/ppermute | solution.py:23
  137.5 115.5 %collective-permute-start.13 = (bf16[16,8,1536]{2,1,0:T(8,128)(2,1)}, bf16[16,8,1536]{2,1,0:T(8,128)(2,1)}, u32[]{:S(2)}, u32[]{:S(2)}) collective-permute-start(bf16[16,8,1536]{2,1,0:T(8,128)(2,1)} %slice_bitcast_fusion.1), channel_id=1, source_target_pairs={{1,0},{3,2},{5,4},{7,6},{9,8},{11,10},{13,12},{15,14},{17,16},{19,... | collective-permute-start | bytes 1179656 | tf_op jit(solution)/shard_map/ppermute | solution.py:31
  139.1 113.9 %copy-start.5 = (bf16[16,8,1536]{2,1,0:T(8,128)(2,1)}, bf16[16,8,1536]{2,1,0:T(8,128)(2,1)S(1)}, u32[]{:S(2)}) copy-start(bf16[16,8,1536]{2,1,0:T(8,128)(2,1)S(1)} %get-tuple-element.875) | copy-start | bytes 1179652
  261.4 2.9 copy-start.2
  332.4 6.5 %copy-start.4 = (bf16[16,8,1536]{2,1,0:T(8,128)(2,1)S(1)}, bf16[16,8,1536]{2,1,0:T(8,128)(2,1)}, u32[]{:S(2)}) copy-start(bf16[16,8,1536]{2,1,0:T(8,128)(2,1)} %copy-done.3) | copy-start | bytes 1179652
  332.4 6.5 %copy-start.6 = (bf16[16,8,1536]{2,1,0:T(8,128)(2,1)S(1)}, bf16[16,8,1536]{2,1,0:T(8,128)(2,1)}, u32[]{:S(2)}) copy-start(bf16[16,8,1536]{2,1,0:T(8,128)(2,1)} %copy-done.5) | copy-start | bytes 1179652
  332.8 7.6 %collective-permute-start.14 = (bf16[2,12,2,1536]{3,1,0,2:T(8,128)(2,1)S(1)}, bf16[2,12,2,1536]{3,1,0,2:T(8,128)(2,1)S(1)}, u32[]{:S(2)}, u32[]{:S(2)}) collective-permute-start(bf16[2,12,2,1536]{3,1,0,2:T(8,128)(2,1)S(1)} %get-tuple-element.363), channel_id=1, source_target_pairs={{0,48},{48,96},{96,144},{144,192},{192,240},{240,288},{288,336},{3... | collective-permute-start | bytes 442376 | tf_op jit(solution)/shard_map/ppermute | solution.py:22
  334.7 11.2 %collective-permute-start.15 = (bf16[2,12,2,1536]{3,1,0,2:T(8,128)(2,1)S(1)}, bf16[2,12,2,1536]{3,1,0,2:T(8,128)(2,1)S(1)}, u32[]{:S(2)}, u32[]{:S(2)}) collective-permute-start(bf16[2,12,2,1536]{3,1,0,2:T(8,128)(2,1)S(1)} %get-tuple-element.364), channel_id=1, source_target_pairs={{48,0},{96,48},{144,96},{192,144},{240,192},{288,240},{336,288},{3... | collective-permute-start | bytes 442376 | tf_op jit(solution)/shard_map/ppermute | solution.py:23
  346.4 10.1 %collective-permute-start.16 = (bf16[24,2,2,1536]{3,1,0,2:T(2,128)(2,1)S(1)}, bf16[24,2,2,1536]{3,1,0,2:T(2,128)(2,1)S(1)}, u32[]{:S(2)}, u32[]{:S(2)}) collective-permute-start(bf16[24,2,2,1536]{3,1,0,2:T(2,128)(2,1)S(1)} %get-tuple-element.359), channel_id=1, source_target_pairs={{0,2},{2,4},{4,6},{6,8},{8,10},{10,12},{12,14},{14,16},{16,18},{18... | collective-permute-start | bytes 884744 | tf_op jit(solution)/shard_map/ppermute | solution.py:22
  346.4 10.1 %collective-permute-start.17 = (bf16[24,2,2,1536]{3,1,0,2:T(2,128)(2,1)S(1)}, bf16[24,2,2,1536]{3,1,0,2:T(2,128)(2,1)S(1)}, u32[]{:S(2)}, u32[]{:S(2)}) collective-permute-start(bf16[24,2,2,1536]{3,1,0,2:T(2,128)(2,1)S(1)} %get-tuple-element.360), channel_id=1, source_target_pairs={{2,0},{4,2},{6,4},{8,6},{10,8},{12,10},{14,12},{16,14},{18,16},{20... | collective-permute-start | bytes 884744 | tf_op jit(solution)/shard_map/ppermute | solution.py:23
where the time goes:
time: 366 us; the launch traced here: 360 us
  waiting for transfers between devices  159 us (43%)
  matrix products  76.4 us (21%)
  starting transfers between devices  57.3 us (16%)
  local copies, waits for them, and re-layouts  45.6 us (12%)
  other arithmetic  20 us (5%)
    ppermute x2, waiting for transfers between devices, shifted(): lax.ppermute(value, axis, [(source, source + steps) for source in range(i...  119 us
    ppermute x8, starting transfers between devices, padded(): after = lax.ppermute(initial, axis, down)  32.9 us
    ppermute x8, starting transfers between devices, padded(): before = lax.ppermute(last, axis, up)  21.8 us
    ppermute x8, waiting for transfers between devices, padded(): before = lax.ppermute(last, axis, up)  20.5 us
    dot_general x12, matrix products, head_forward(): jnp.dot(weights.astype(jnp.bfloat16), value_head, preferred_element_type=...  19.9 us
    ppermute x8, waiting for transfers between devices, padded(): after = lax.ppermute(initial, axis, down)  19.7 us
    dot_general x12, matrix products, head_backward(): jnp.dot(weights_low.T, upstream_head, preferred_element_type=jnp.float32)  18.9 us
    dot_general x12, matrix products, head_backward(): jnp.dot(upstream_head, value_head.T, preferred_element_type=jnp.float32)  12.8 us
  transfers between devices with their start and end apart: 18, of which 14 were waited for; matrix products, arithmetic and copies ran while one was open for 0% of the time, Pallas kernels for 0%

commit v1 on v0

v1 whole, which is shorter than its diff:
```python
import math

import jax
import jax.numpy as jnp
from jax import lax
from jax.sharding import PartitionSpec as P

HEADS = 12
MARGIN = 2

NEGATIVE = -1e30

AXES = ("lat", "lon", "pipe")
NEIGHBOURS = [(dl, dn) for dl in (-1, 0, 1) for dn in (-1, 0, 1) if (dl, dn) != (0, 0)]


def linear(l, n, p, lons, pipes):
    return (l * lons + n) * pipes + p


def pairs_from(offset, sizes, src_pipe=None, dst_pipe=None):
    lats, lons, pipes = sizes
    dl, dn = offset
    out = []
    for l in range(lats):
        sl = l + dl
        if sl < 0 or sl >= lats:
            continue
        for n in range(lons):
            sn = (n + dn) % lons
            if src_pipe is None:
                for p in range(pipes):
                    out.append((linear(sl, sn, p, lons, pipes), linear(l, n, p, lons, pipes)))
            else:
                out.append((linear(sl, sn, src_pipe, lons, pipes), linear(l, n, dst_pipe, lons, pipes)))
    return out


def edge(length, d):
    if d == -1:
        return slice(length - MARGIN, length)
    if d == 1:
        return slice(0, MARGIN)
    return slice(0, length)


def gather_window(tile, sizes, src_pipe=None, dst_pipe=None):
    rows, cols = tile.shape[0], tile.shape[1]
    pieces = {}
    for off in [(0, 0)] + NEIGHBOURS:
        dl, dn = off
        if off == (0, 0) and src_pipe is None:
            pieces[off] = tile
            continue
        part = tile[edge(rows, dl), edge(cols, dn)]
        pieces[off] = lax.ppermute(part, AXES, pairs_from(off, sizes, src_pipe, dst_pipe))
    bands = []
    for dl in (-1, 0, 1):
        bands.append(jnp.concatenate([pieces[(dl, dn)] for dn in (-1, 0, 1)], axis=1))
    return jnp.concatenate(bands, axis=0)


def window_part(length, d):
    if d == -1:
        return slice(length + MARGIN, length + 2 * MARGIN)
    if d == 1:
        return slice(0, MARGIN)
    return slice(MARGIN, length + MARGIN)


def scatter_pieces(window, sizes, src_pipe=None, dst_pipe=None):
    rows, cols = window.shape[0] - 2 * MARGIN, window.shape[1] - 2 * MARGIN
    got = {}
    for off in NEIGHBOURS:
        dl, dn = off
        part = window[window_part(rows, dl), window_part(cols, dn)].astype(jnp.bfloat16)
        got[off] = lax.ppermute(part, AXES, pairs_from(off, sizes, src_pipe, dst_pipe))
    return got


def sum_pieces(centre, got):
    rows, cols = centre.shape[0], centre.shape[1]
    total = centre
    for (dl, dn), piece in got.items():
        piece = piece.astype(jnp.float32)
        r0 = 0 if dl <= 0 else rows - MARGIN
        c0 = 0 if dn <= 0 else cols - MARGIN
        pr = [(r0, rows - r0 - piece.shape[0])]
        pc = [(c0, cols - c0 - piece.shape[1])]
        pad = pr + pc + [(0, 0)] * (piece.ndim - 2)
        total = total + jnp.pad(piece, pad)
    return total


def probabilities(q3, k3, allowed, scaling):
    scores = jnp.einsum("thd,phd->htp", q3, k3, preferred_element_type=jnp.float32) * scaling
    scores = jnp.where(allowed[None, None, :], scores, NEGATIVE)
    highest = jnp.max(scores, axis=2, keepdims=True)
    weights = jnp.exp(scores - highest)
    return weights / jnp.sum(weights, axis=2, keepdims=True)


def attend(probs_low, u3):
    return jnp.einsum("htp,phd->thd", probs_low, u3, preferred_element_type=jnp.float32).astype(
        jnp.bfloat16
    )


def backward(probs, probs_low, q3, k3, u3, d3, scaling):
    dprob = jnp.einsum("thd,phd->htp", d3, u3, preferred_element_type=jnp.float32)
    inner = jnp.sum(probs * dprob, axis=2, keepdims=True)
    dscore = (probs * (dprob - inner) * scaling).astype(jnp.bfloat16)
    grad_q = jnp.einsum("htp,phd->thd", dscore, k3, preferred_element_type=jnp.float32).astype(
        jnp.bfloat16
    )
    kterm = jnp.einsum("htp,thd->phd", dscore, q3, preferred_element_type=jnp.float32)
    vterm = jnp.einsum("htp,thd->phd", probs_low, d3, preferred_element_type=jnp.float32)
    return grad_q, kterm, vterm


def body(queries_keys, values, cotangent):
    sizes = (lax.axis_size("lat"), lax.axis_size("lon"), lax.axis_size("pipe"))
    is_first = lax.axis_index("pipe") == 0
    tile_rows, tile_cols, features = cotangent.shape
    margin = MARGIN
    rows_ext = tile_rows + 2 * margin
    cols_ext = tile_cols + 2 * margin
    window_size = rows_ext * cols_ext
    token_count = tile_rows * tile_cols
    head_dim = features // HEADS
    scaling = 1.0 / math.sqrt(head_dim)

    q3 = queries_keys[0, 0].reshape(token_count, HEADS, head_dim)
    lat_rows = lax.axis_index("lat") * tile_rows - margin + jnp.arange(rows_ext, dtype=jnp.int32)
    inside = (lat_rows >= 0) & (lat_rows < tile_rows * sizes[0])
    allowed = jnp.broadcast_to(inside[:, None], (rows_ext, cols_ext)).reshape(window_size)

    kv = gather_window(jnp.stack([queries_keys[0, 1], values[0]], axis=2), sizes)
    k3 = kv[:, :, 0].reshape(window_size, HEADS, head_dim)
    v_win = kv[:, :, 1]

    probs_a = probabilities(q3, k3, allowed, scaling)
    context_a = attend(probs_a.astype(jnp.bfloat16), v_win.reshape(window_size, HEADS, head_dim))
    context_a = context_a.reshape(tile_rows, tile_cols, features)

    c_win = gather_window(context_a, sizes, src_pipe=0, dst_pipe=1)
    u_win = (v_win.astype(jnp.float32) + c_win.astype(jnp.float32)).astype(jnp.bfloat16)
    u3 = u_win.reshape(window_size, HEADS, head_dim)

    probs_b = probabilities(q3, k3, allowed, scaling)
    probs_b_low = probs_b.astype(jnp.bfloat16)
    context_b = attend(probs_b_low, u3).reshape(tile_rows, tile_cols, features)
    d3_b = cotangent.reshape(token_count, HEADS, head_dim)
    gq_b, kterm_b, vterm_b = backward(probs_b, probs_b_low, q3, k3, u3, d3_b, scaling)
    vterm_b = vterm_b.reshape(rows_ext, cols_ext, features)
    kterm_b = kterm_b.reshape(rows_ext, cols_ext, features)

    centre = slice(margin, margin + tile_rows), slice(margin, margin + tile_cols)
    got = scatter_pieces(vterm_b, sizes, src_pipe=1, dst_pipe=0)
    own_b = lax.ppermute(vterm_b[centre], AXES, pairs_from((0, 0), sizes, 1, 0))
    d_c = sum_pieces(own_b, got).astype(jnp.bfloat16)

    d3_c = d_c.reshape(token_count, HEADS, head_dim)
    gq_c, kterm_c, vterm_c = backward(probs_b, probs_b_low, q3, k3, u3, d3_c, scaling)
    kterm_c = kterm_c.reshape(rows_ext, cols_ext, features)
    vterm_c = vterm_c.reshape(rows_ext, cols_ext, features)

    terms = jnp.where(
        is_first, jnp.stack([kterm_c, vterm_c], axis=2), jnp.stack([kterm_b, vterm_b], axis=2)
    )
    back = scatter_pieces(terms, sizes)
    owned = sum_pieces(terms[centre], back).astype(jnp.bfloat16)

    activations = jnp.where(is_first, context_a, context_b)
    grad_q = jnp.where(is_first, gq_c, gq_b).reshape(tile_rows, tile_cols, features)
    grad_qk = jnp.stack([grad_q, owned[:, :, 0]], axis=0)
    return activations[None], grad_qk[None], owned[:, :, 1][None]


def solution(mesh):
    in_specs = (
        P("pipe", None, "lat", "lon", None),
        P("pipe", "lat", "lon", None),
        P("lat", "lon", None),
    )
    out_specs = (
        P("pipe", "lat", "lon", None),
        P("pipe", None, "lat", "lon", None),
        P("pipe", "lat", "lon", None),
    )
    return jax.shard_map(body, mesh=mesh, in_specs=in_specs, out_specs=out_specs, check_vma=False)
```

time: 366 us -> 197 us (0.54)
  the two profiles are of different devices: /device:TPU:60 before, /device:TPU:6 now
where the time goes in v1:
time: 197 us; the launch traced here: 195 us
  starting transfers between devices  104 us (53%)
  local copies, waits for them, and re-layouts  42.7 us (22%)
  matrix products  25.8 us (13%)
  other arithmetic  18.2 us (9%)
  waiting for transfers between devices  3.25 us (2%)
    ppermute x16, starting transfers between devices, scatter_pieces(): lax.ppermute(part, AXES, pairs_from(off, sizes, src_pipe, dst_pipe))  53.2 us
    ppermute x17, starting transfers between devices, gather_window(): lax.ppermute(part, AXES, pairs_from(off, sizes, src_pipe, dst_pipe))  48.8 us
    dot_general x2, matrix products, backward(): jnp.einsum('htp,thd->phd', dscore, q3, preferred_element_type=jnp.float32)  9.12 us
    dot_general x2, matrix products, backward(): jnp.einsum('htp,phd->thd', dscore, k3, preferred_element_type=jnp.float32)  8.22 us
    another operation x2, other arithmetic  7.49 us
    transpose x2, local copies, waits for them, and re-layouts, backward(): jnp.einsum('htp,thd->phd', dscore, q3, preferred_element_type=jnp.float32)  4.95 us
    another operation x2, local copies, waits for them, and re-layouts, body(): jnp.stack([kterm_c, vterm_c], axis=2)  4.4 us
    another operation x2, local copies, waits for them, and re-layouts, body(): jnp.stack([kterm_b, vterm_b], axis=2)  4.24 us
  transfers between devices with their start and end apart: 34, of which 1 were waited for; matrix products, arithmetic and copies ran while one was open for 23% of the time, Pallas kernels for 0%

profile of v1, /device:TPU:6, one launch (start us, length us, event | category | flops | bytes accessed | tf_op | source)
XLA Modules:
  0.0 195.5 jit_solution(12418713171749044156)
XLA Ops:
  2.0 3.1 %collective-permute-start = (bf16[2,2,2,1536]{3,1,0,2:T(2,128)(2,1)S(1)}, bf16[2,2,2,1536]{3,1,0,2:T(2,128)(2,1)S(1)}, u32[]{:S(2)}, u32[]{:S(2)}) collective-permute-start(bf16[2,2,2,1536]{3,1,0,2:T(2,128)(2,1)S(1)} %get-tuple-element.27), channel_id=1, source_target_pairs={{46,48},{47,49},{0,50},{1,51},{2,52},{3,53},{4,54},{5,55},{6,56},{... | collective-permute-start | bytes 73736 | tf_op jit(solution)/shard_map/ppermute | solution.py:56
  5.0 8.1 %collective-permute-start.5 = (bf16[2,2,2,1536]{3,1,0,2:T(2,128)(2,1)S(1)}, bf16[2,2,2,1536]{3,1,0,2:T(2,128)(2,1)S(1)}, u32[]{:S(2)}, u32[]{:S(2)}) collective-permute-start(bf16[2,2,2,1536]{3,1,0,2:T(2,128)(2,1)S(1)} %get-tuple-element.28), channel_id=1, source_target_pairs={{94,0},{95,1},{48,2},{49,3},{50,4},{51,5},{52,6},{53,7},{54,8},{55... | collective-permute-start | bytes 73736 | tf_op jit(solution)/shard_map/ppermute | solution.py:56
  13.1 10.6 %collective-permute-start.7 = (bf16[2,2,2,1536]{3,1,0,2:T(2,128)(2,1)S(1)}, bf16[2,2,2,1536]{3,1,0,2:T(2,128)(2,1)S(1)}, u32[]{:S(2)}, u32[]{:S(2)}) collective-permute-start(bf16[2,2,2,1536]{3,1,0,2:T(2,128)(2,1)S(1)} %get-tuple-element.29), channel_id=1, source_target_pairs={{50,0},{51,1},{52,2},{53,3},{54,4},{55,5},{56,6},{57,7},{58,8},{59... | collective-permute-start | bytes 73736 | tf_op jit(solution)/shard_map/ppermute | solution.py:56
  24.3 2.9 %collective-permute-start.4 = (bf16[16,2,2,1536]{3,1,0,2:T(2,128)(2,1)S(1)}, bf16[16,2,2,1536]{3,1,0,2:T(2,128)(2,1)S(1)}, u32[]{:S(2)}, u32[]{:S(2)}) collective-permute-start(bf16[16,2,2,1536]{3,1,0,2:T(2,128)(2,1)S(1)} %get-tuple-element.34), channel_id=1, source_target_pairs={{2,0},{3,1},{4,2},{5,3},{6,4},{7,5},{8,6},{9,7},{10,8},{11,9},{12,... | collective-permute-start | bytes 589832 | tf_op jit(solution)/shard_map/ppermute | solution.py:56
  27.2 3.0 %collective-permute-start.2 = (bf16[2,2,2,1536]{3,1,0,2:T(2,128)(2,1)S(1)}, bf16[2,2,2,1536]{3,1,0,2:T(2,128)(2,1)S(1)}, u32[]{:S(2)}, u32[]{:S(2)}) collective-permute-start(bf16[2,2,2,1536]{3,1,0,2:T(2,128)(2,1)S(1)} %get-tuple-element.30), channel_id=1, source_target_pairs={{2,48},{3,49},{4,50},{5,51},{6,52},{7,53},{8,54},{9,55},{10,56},{1... | collective-permute-start | bytes 73736 | tf_op jit(solution)/shard_map/ppermute | solution.py:56
  30.3 1.9 collective-permute-start.1
  32.2 7.5 %collective-permute-start.6 = (bf16[2,8,2,1536]{3,1,0,2:T(8,128)(2,1)S(1)}, bf16[2,8,2,1536]{3,1,0,2:T(8,128)(2,1)S(1)}, u32[]{:S(2)}, u32[]{:S(2)}) collective-permute-start(bf16[2,8,2,1536]{3,1,0,2:T(8,128)(2,1)S(1)} %get-tuple-element.32), channel_id=1, source_target_pairs={{48,0},{49,1},{50,2},{51,3},{52,4},{53,5},{54,6},{55,7},{56,8},{57... | collective-permute-start | bytes 294920 | tf_op jit(solution)/shard_map/ppermute | solution.py:56
  48.2 2.0 %fusion.103 = (f32[12,128]{1,0:T(8,128)S(1)}, f32[12,128,240]{1,2,0:T(8,128)S(1)}) fusion(bf16[128,12,128]{2,1,0:T(8,128)(2,1)S(1)} %copy-done.10, bf16[240,12,128]{2,1,0:T(8,128)(2,1)} %reshape_squeeze.10, pred[240]{0:T(512)(128)(4,1)S(1)} %broadcast_in_dim.35), kind=kOutput, calls=%fused_computation.111 | convolution fusion | flops 95846640 | bytes 2611440 | tf_op jit(solution)/shard_map/sub | solution.py:99
  69.3 3.2 %collective-permute-done.8 = bf16[2,2,1536]{2,1,0:T(2,128)(2,1)} collective-permute-done((bf16[2,2,1536]{2,1,0:T(2,128)(2,1)}, bf16[2,2,1536]{2,1,0:T(2,128)(2,1)}, u32[]{:S(2)}, u32[]{:S(2)}) %collective-permute-start.8) | collective-permute-done | bytes 12320 | tf_op jit(solution)/shard_map/ppermute | solution.py:56
  80.7 2.4 %slice.202 = f32[16,8,1536]{2,1,0:T(8,128)} slice(f32[20,12,1536]{2,1,0:T(8,128)} %reshape.59), slice={[2:18], [2:10], [0:1536]} | slice | bytes 1572864 | tf_op jit(solution)/shard_map/slice | solution.py:160
  83.1 6.6 %collective-permute-start.18 = (bf16[2,2,1536]{2,1,0:T(2,128)(2,1)}, bf16[2,2,1536]{2,1,0:T(2,128)(2,1)S(1)}, u32[]{:S(2)}, u32[]{:S(2)}) collective-permute-start(bf16[2,2,1536]{2,1,0:T(2,128)(2,1)} %get-tuple-element.15), channel_id=1, source_target_pairs={{47,48},{1,50},{3,52},{5,54},{7,56},{9,58},{11,60},{13,62},{15,64}... | collective-permute-start | bytes 36872 | tf_op jit(solution)/shard_map/ppermute | solution.py:77
  89.7 6.3 %collective-permute-start.25 = (bf16[2,2,1536]{2,1,0:T(2,128)(2,1)}, bf16[2,2,1536]{2,1,0:T(2,128)(2,1)}, u32[]{:S(2)}, u32[]{:S(2)}) collective-permute-start(bf16[2,2,1536]{2,1,0:T(2,128)(2,1)} %get-tuple-element.16), channel_id=1, source_target_pairs={{51,0},{53,2},{55,4},{57,6},{59,8},{61,10},{63,12},{65,14},{67,16}... | collective-permute-start | bytes 36872 | tf_op jit(solution)/shard_map/ppermute | solution.py:77
  96.0 1.9 collective-permute-start.23
  97.9 1.9 collective-permute-start.20
  99.8 2.2 %collective-permute-start.17 = (f32[16,8,1536]{2,1,0:T(8,128)}, f32[16,8,1536]{2,1,0:T(8,128)}, u32[]{:S(2)}, u32[]{:S(2)}) collective-permute-start(f32[16,8,1536]{2,1,0:T(8,128)} %slice.202), channel_id=1, source_target_pairs={{1,0},{3,2},{5,4},{7,6},{9,8},{11,10},{13,12},{15,14},{17,16},{19,... | collective-permute-start | bytes 2359304 | tf_op jit(solution)/shard_map/ppermute | solution.py:160
  105.2 2.0 %add_convert_fusion = bf16[240,12,128]{2,1,0:T(8,128)(2,1)S(1)} fusion(f32[240,12,128]{2,1,0:T(8,128)} %reshape.61, bf16[240,12,128]{2,1,0:T(8,128)(2,1)} %copy-done.1), kind=kLoop, calls=%fused_computation.5 | loop fusion | flops 1105920 | bytes 2949120 | tf_op jit(solution)/shard_map/convert_element_type | solution.py:147
  110.0 4.5 %convolution_bitcast_fusion.1 = f32[240,12,128]{2,0,1:T(8,128)} fusion(f32[12,240,128]{2,1,0:T(8,128)} %fusion.49, bf16[128,12,128]{2,1,0:T(8,128)(2,1)S(1)} %copy-done.11, f32[12,128,240]{1,2,0:T(8,128)} %copy-done.7, f32[12,128]{1,0:T(8,128)S(1)} %copy-done.19), kind=kOutput, calls=%fused_computation.30 | convolution fusion | flops 96954096 | bytes 4823040 | tf_op jit(solution)/shard_map/htp,thd->phd/dot_general | solution.py:116
  119.8 4.5 %convolution_convert_fusion = bf16[12,128,128]{2,1,0:T(8,128)(2,1)} fusion(f32[12,240,128]{2,1,0:T(8,128)} %fusion.49, bf16[240,12,128]{2,1,0:T(8,128)(2,1)} %reshape_squeeze.10, f32[12,128,240]{1,2,0:T(8,128)} %copy-done.7, f32[12,128]{1,0:T(8,128)S(1)} %copy-done.19), kind=kOutput, calls=%fused_computation.35 | convolution fusion | flops 97150704 | bytes 4085760 | tf_op jit(solution)/shard_map/htp,phd->thd/dot_general | solution.py:113
  125.5 3.2 %copy.33 = f32[240,12,128]{2,1,0:T(8,128)} copy(f32[240,12,128]{2,0,1:T(8,128)} %convolution_bitcast_fusion.1) | data formatting | bytes 2949120 | tf_op jit(solution)/shard_map/htp,thd->phd/transpose | solution.py:116
  128.7 2.7 %stack_reshape.18 = f32[20,12,1,1536]{3,1,0,2:T(8,128)} reshape(f32[240,12,128]{2,1,0:T(8,128)} %copy.33) | data formatting | bytes 2949120 | tf_op jit(solution)/shard_map/stack;reshape | solution.py:169
  137.3 4.6 %fusion.28 = f32[240,12,128]{2,0,1:T(8,128)} fusion(f32[12,128,240]{1,2,0:T(8,128)} %fusion.51, bf16[128,12,128]{2,1,0:T(8,128)(2,1)S(1)} %copy-done.12, f32[12,128,240]{1,2,0:T(8,128)} %copy-done.7, f32[12,128]{1,0:T(8,128)S(1)} %copy-done.19), kind=kOutput, calls=%fused_computation.33 | convolution fusion | flops 96954096 | bytes 4823040 | tf_op jit(solution)/shard_map/htp,thd->phd/dot_general | solution.py:116
  146.1 2.8 %stack_reshape.16 = f32[20,12,1,1536]{3,1,0,2:T(8,128)} reshape(f32[240,12,128]{2,1,0:T(8,128)} %copy.29) | data formatting | bytes 2949120 | tf_op jit(solution)/shard_map/stack;reshape | solution.py:169
  148.9 5.8 %fusion.91 = (bf16[20,12,2,1536]{3,1,0,2:T(8,128)(2,1)S(1)}, f32[20,12,2,1536]{3,1,0,2:T(8,128)}) fusion(f32[20,12,1,1536]{3,1,0,2:T(8,128)S(1)} %copy-done, f32[20,12,1,1536]{3,1,0,2:T(8,128)} %stack_reshape.18, f32[20,12,1,1536]{3,1,0,2:T(8,128)} %stack_reshape.17, f32[20,12,1,1536]{3,1,0,2:T(8,128)} %stack_reshape.16, pred[]{:T(512)S(6)} %eq.3), kind=kLoop, calls=%fused_computation.99 | loop fusion | flops 2949120 | bytes 10321921 | tf_op jit(solution)/shard_map/convert.40
  155.1 1.9 collective-permute-start.26
  157.1 9.4 %collective-permute-start.33 = (bf16[2,2,2,1536]{3,1,0,2:T(2,128)(2,1)S(1)}, bf16[2,2,2,1536]{3,1,0,2:T(2,128)(2,1)S(1)}, u32[]{:S(2)}, u32[]{:S(2)}) collective-permute-start(bf16[2,2,2,1536]{3,1,0,2:T(2,128)(2,1)S(1)} %get-tuple-element.6), channel_id=1, source_target_pairs={{50,0},{51,1},{52,2},{53,3},{54,4},{55,5},{56,6},{57,7},{58,8},{59... | collective-permute-start | bytes 73736 | tf_op jit(solution)/shard_map/ppermute | solution.py:77
  166.4 1.9 collective-permute-start.31
  168.4 5.8 %collective-permute-start.28 = (bf16[2,2,2,1536]{3,1,0,2:T(2,128)(2,1)S(1)}, bf16[2,2,2,1536]{3,1,0,2:T(2,128)(2,1)S(1)}, u32[]{:S(2)}, u32[]{:S(2)}) collective-permute-start(bf16[2,2,2,1536]{3,1,0,2:T(2,128)(2,1)S(1)} %get-tuple-element.8), channel_id=1, source_target_pairs={{2,48},{3,49},{4,50},{5,51},{6,52},{7,53},{8,54},{9,55},{10,56},{1... | collective-permute-start | bytes 73736 | tf_op jit(solution)/shard_map/ppermute | solution.py:77
  174.2 1.9 collective-permute-start.27
  176.1 7.5 %collective-permute-start.32 = (bf16[2,8,2,1536]{3,1,0,2:T(8,128)(2,1)S(1)}, bf16[2,8,2,1536]{3,1,0,2:T(8,128)(2,1)S(1)}, u32[]{:S(2)}, u32[]{:S(2)}) collective-permute-start(bf16[2,8,2,1536]{3,1,0,2:T(8,128)(2,1)S(1)} %get-tuple-element.10), channel_id=1, source_target_pairs={{48,0},{49,1},{50,2},{51,3},{52,4},{53,5},{54,6},{55,7},{56,8},{57... | collective-permute-start | bytes 294920 | tf_op jit(solution)/shard_map/ppermute | solution.py:77
  183.7 2.9 %collective-permute-start.30 = (bf16[16,2,2,1536]{3,1,0,2:T(2,128)(2,1)S(1)}, bf16[16,2,2,1536]{3,1,0,2:T(2,128)(2,1)S(1)}, u32[]{:S(2)}, u32[]{:S(2)}) collective-permute-start(bf16[16,2,2,1536]{3,1,0,2:T(2,128)(2,1)S(1)} %get-tuple-element.12), channel_id=1, source_target_pairs={{2,0},{3,1},{4,2},{5,3},{6,4},{7,5},{8,6},{9,7},{10,8},{11,9},{12,... | collective-permute-start | bytes 589832 | tf_op jit(solution)/shard_map/ppermute | solution.py:77
  186.7 3.7 %fusion.40 = bf16[128,12,128]{0,2,1:T(8,128)(2,1)S(1)} fusion(bf16[12,128,128]{2,1,0:T(8,128)(2,1)} %convolution_convert_fusion, f32[12,128,240]{1,2,0:T(8,128)} %fusion.51, pred[]{:T(512)S(6)} %eq.3, bf16[240,12,128]{2,1,0:T(8,128)(2,1)S(1)} %copy-done.9, f32[12,128,240]{1,2,0:T(8,128)} %copy-done.7, f32[12,128]{1,0:T(8,128)S(1)} %copy-done.19), kind=kOutput, calls=%fused_computation.42 | convolution fusion | flops 97347312 | bytes 4478977 | tf_op jit(solution)/shard_map/htp,phd->thd/dot_general | solution.py:113
  191.2 2.6 %fusion.11 = bf16[16,8,2,1536]{3,1,0,2:T(8,128)(2,1)S(1)} fusion(f32[20,12,2,1536]{3,1,0,2:T(8,128)} %get-tuple-element.4, bf16[2,2,2,1536]{3,1,0,2:T(2,128)(2,1)S(1)} %collective-permute-done.33, bf16[2,8,2,1536]{3,1,0,2:T(8,128)(2,1)S(1)} %collective-permute-done.32, bf16[2,2,2,1536]{3,1,0,2:T(2,128)(2,1)S(1)} %collective-permute-done.31, ...), kind=kLoop, calls=%fused_computation.15 | loop fusion | flops 6684672 | bytes 3047424 | tf_op jit(solution)/shard_map/convert_element_type | solution.py:172
  (140 shorter events, 62.7 us)
Async XLA Ops:
  2.0 25.3 %collective-permute-start = (bf16[2,2,2,1536]{3,1,0,2:T(2,128)(2,1)S(1)}, bf16[2,2,2,1536]{3,1,0,2:T(2,128)(2,1)S(1)}, u32[]{:S(2)}, u32[]{:S(2)}) collective-permute-start(bf16[2,2,2,1536]{3,1,0,2:T(2,128)(2,1)S(1)} %get-tuple-element.27), channel_id=1, source_target_pairs={{46,48},{47,49},{0,50},{1,51},{2,52},{3,53},{4,54},{5,55},{6,56},{... | collective-permute-start | bytes 73736 | tf_op jit(solution)/shard_map/ppermute | solution.py:56
  5.0 25.3 %collective-permute-start.5 = (bf16[2,2,2,1536]{3,1,0,2:T(2,128)(2,1)S(1)}, bf16[2,2,2,1536]{3,1,0,2:T(2,128)(2,1)S(1)}, u32[]{:S(2)}, u32[]{:S(2)}) collective-permute-start(bf16[2,2,2,1536]{3,1,0,2:T(2,128)(2,1)S(1)} %get-tuple-element.28), channel_id=1, source_target_pairs={{94,0},{95,1},{48,2},{49,3},{50,4},{51,5},{52,6},{53,7},{54,8},{55... | collective-permute-start | bytes 73736 | tf_op jit(solution)/shard_map/ppermute | solution.py:56
  13.1 19.1 %collective-permute-start.7 = (bf16[2,2,2,1536]{3,1,0,2:T(2,128)(2,1)S(1)}, bf16[2,2,2,1536]{3,1,0,2:T(2,128)(2,1)S(1)}, u32[]{:S(2)}, u32[]{:S(2)}) collective-permute-start(bf16[2,2,2,1536]{3,1,0,2:T(2,128)(2,1)S(1)} %get-tuple-element.29), channel_id=1, source_target_pairs={{50,0},{51,1},{52,2},{53,3},{54,4},{55,5},{56,6},{57,7},{58,8},{59... | collective-permute-start | bytes 73736 | tf_op jit(solution)/shard_map/ppermute | solution.py:56
  24.2 17.9 %collective-permute-start.3 = (bf16[16,2,2,1536]{3,1,0,2:T(2,128)(2,1)S(1)}, bf16[16,2,2,1536]{3,1,0,2:T(2,128)(2,1)S(1)}, u32[]{:S(2)}, u32[]{:S(2)}) collective-permute-start(bf16[16,2,2,1536]{3,1,0,2:T(2,128)(2,1)S(1)} %get-tuple-element.33), channel_id=1, source_target_pairs={{46,0},{47,1},{0,2},{1,3},{2,4},{3,5},{4,6},{5,7},{6,8},{7,9},{8,1... | collective-permute-start | bytes 589832 | tf_op jit(solution)/shard_map/ppermute | solution.py:56
  24.3 17.9 %collective-permute-start.4 = (bf16[16,2,2,1536]{3,1,0,2:T(2,128)(2,1)S(1)}, bf16[16,2,2,1536]{3,1,0,2:T(2,128)(2,1)S(1)}, u32[]{:S(2)}, u32[]{:S(2)}) collective-permute-start(bf16[16,2,2,1536]{3,1,0,2:T(2,128)(2,1)S(1)} %get-tuple-element.34), channel_id=1, source_target_pairs={{2,0},{3,1},{4,2},{5,3},{6,4},{7,5},{8,6},{9,7},{10,8},{11,9},{12,... | collective-permute-start | bytes 589832 | tf_op jit(solution)/shard_map/ppermute | solution.py:56
  27.2 14.9 %collective-permute-start.2 = (bf16[2,2,2,1536]{3,1,0,2:T(2,128)(2,1)S(1)}, bf16[2,2,2,1536]{3,1,0,2:T(2,128)(2,1)S(1)}, u32[]{:S(2)}, u32[]{:S(2)}) collective-permute-start(bf16[2,2,2,1536]{3,1,0,2:T(2,128)(2,1)S(1)} %get-tuple-element.30), channel_id=1, source_target_pairs={{2,48},{3,49},{4,50},{5,51},{6,52},{7,53},{8,54},{9,55},{10,56},{1... | collective-permute-start | bytes 73736 | tf_op jit(solution)/shard_map/ppermute | solution.py:56
  30.3 11.8 %collective-permute-start.1 = (bf16[2,8,2,1536]{3,1,0,2:T(8,128)(2,1)S(1)}, bf16[2,8,2,1536]{3,1,0,2:T(8,128)(2,1)S(1)}, u32[]{:S(2)}, u32[]{:S(2)}) collective-permute-start(bf16[2,8,2,1536]{3,1,0,2:T(8,128)(2,1)S(1)} %get-tuple-element.31), channel_id=1, source_target_pairs={{0,48},{1,49},{2,50},{3,51},{4,52},{5,53},{6,54},{7,55},{8,56},{9,... | collective-permute-start | bytes 294920 | tf_op jit(solution)/shard_map/ppermute | solution.py:56
  32.2 9.9 %collective-permute-start.6 = (bf16[2,8,2,1536]{3,1,0,2:T(8,128)(2,1)S(1)}, bf16[2,8,2,1536]{3,1,0,2:T(8,128)(2,1)S(1)}, u32[]{:S(2)}, u32[]{:S(2)}) collective-permute-start(bf16[2,8,2,1536]{3,1,0,2:T(8,128)(2,1)S(1)} %get-tuple-element.32), channel_id=1, source_target_pairs={{48,0},{49,1},{50,2},{51,3},{52,4},{53,5},{54,6},{55,7},{56,8},{57... | collective-permute-start | bytes 294920 | tf_op jit(solution)/shard_map/ppermute | solution.py:56
  53.9 45.9 %collective-permute-start.12 = (bf16[16,8,1536]{2,1,0:T(8,128)(2,1)S(1)}, bf16[16,8,1536]{2,1,0:T(8,128)(2,1)}, u32[]{:S(2)}, u32[]{:S(2)}) collective-permute-start(bf16[16,8,1536]{2,1,0:T(8,128)(2,1)S(1)} %reshape.57), channel_id=1, source_target_pairs={{0,1},{2,3},{4,5},{6,7},{8,9},{10,11},{12,13},{14,15},{16,17},{18,... | collective-permute-start | bytes 1179656 | tf_op jit(solution)/shard_map/ppermute | solution.py:56
  61.3 11.1 %collective-permute-start.8 = (bf16[2,2,1536]{2,1,0:T(2,128)(2,1)}, bf16[2,2,1536]{2,1,0:T(2,128)(2,1)}, u32[]{:S(2)}, u32[]{:S(2)}) collective-permute-start(bf16[2,2,1536]{2,1,0:T(2,128)(2,1)} %get-tuple-element.35), channel_id=1, source_target_pairs={{46,49},{0,51},{2,53},{4,55},{6,57},{8,59},{10,61},{12,63},{14,65}... | collective-permute-start | bytes 36872 | tf_op jit(solution)/shard_map/ppermute | solution.py:56
  62.6 11.1 %collective-permute-start.16 = (bf16[2,2,1536]{2,1,0:T(2,128)(2,1)}, bf16[2,2,1536]{2,1,0:T(2,128)(2,1)}, u32[]{:S(2)}, u32[]{:S(2)}) collective-permute-start(bf16[2,2,1536]{2,1,0:T(2,128)(2,1)} %get-tuple-element.36), channel_id=1, source_target_pairs={{50,1},{52,3},{54,5},{56,7},{58,9},{60,11},{62,13},{64,15},{66,17}... | collective-permute-start | bytes 36872 | tf_op jit(solution)/shard_map/ppermute | solution.py:56
  63.9 11.2 %collective-permute-start.14 = (bf16[2,2,1536]{2,1,0:T(2,128)(2,1)}, bf16[2,2,1536]{2,1,0:T(2,128)(2,1)}, u32[]{:S(2)}, u32[]{:S(2)}) collective-permute-start(bf16[2,2,1536]{2,1,0:T(2,128)(2,1)} %get-tuple-element.37), channel_id=1, source_target_pairs={{94,1},{48,3},{50,5},{52,7},{54,9},{56,11},{58,13},{60,15},{62,17}... | collective-permute-start | bytes 36872 | tf_op jit(solution)/shard_map/ppermute | solution.py:56
  65.2 11.2 %collective-permute-start.10 = (bf16[2,2,1536]{2,1,0:T(2,128)(2,1)}, bf16[2,2,1536]{2,1,0:T(2,128)(2,1)}, u32[]{:S(2)}, u32[]{:S(2)}) collective-permute-start(bf16[2,2,1536]{2,1,0:T(2,128)(2,1)} %get-tuple-element.38), channel_id=1, source_target_pairs={{2,49},{4,51},{6,53},{8,55},{10,57},{12,59},{14,61},{16,63},{18,65... | collective-permute-start | bytes 36872 | tf_op jit(solution)/shard_map/ppermute | solution.py:56
  72.4 10.7 %collective-permute-start.9 = (bf16[2,8,1536]{2,1,0:T(8,128)(2,1)}, bf16[2,8,1536]{2,1,0:T(8,128)(2,1)S(1)}, u32[]{:S(2)}, u32[]{:S(2)}) collective-permute-start(bf16[2,8,1536]{2,1,0:T(8,128)(2,1)} %slice.156), channel_id=1, source_target_pairs={{0,49},{2,51},{4,53},{6,55},{8,57},{10,59},{12,61},{14,63},{16,65}... | collective-permute-start | bytes 147464 | tf_op jit(solution)/shard_map/ppermute | solution.py:56
  73.7 16.0 %collective-permute-start.15 = (bf16[2,8,1536]{2,1,0:T(8,128)(2,1)}, bf16[2,8,1536]{2,1,0:T(8,128)(2,1)}, u32[]{:S(2)}, u32[]{:S(2)}) collective-permute-start(bf16[2,8,1536]{2,1,0:T(8,128)(2,1)} %slice.162), channel_id=1, source_target_pairs={{48,1},{50,3},{52,5},{54,7},{56,9},{58,11},{60,13},{62,15},{64,17}... | collective-permute-start | bytes 147464 | tf_op jit(solution)/shard_map/ppermute | solution.py:56
  75.0 21.0 %collective-permute-start.11 = (bf16[16,2,1536]{2,1,0:T(2,128)(2,1)}, bf16[16,2,1536]{2,1,0:T(2,128)(2,1)}, u32[]{:S(2)}, u32[]{:S(2)}) collective-permute-start(bf16[16,2,1536]{2,1,0:T(2,128)(2,1)} %get-tuple-element.41), channel_id=1, source_target_pairs={{46,1},{0,3},{2,5},{4,7},{6,9},{8,11},{10,13},{12,15},{14,17},{16,... | collective-permute-start | bytes 294920 | tf_op jit(solution)/shard_map/ppermute | solution.py:56
  76.3 21.6 %collective-permute-start.13 = (bf16[16,2,1536]{2,1,0:T(2,128)(2,1)}, bf16[16,2,1536]{2,1,0:T(2,128)(2,1)}, u32[]{:S(2)}, u32[]{:S(2)}) collective-permute-start(bf16[16,2,1536]{2,1,0:T(2,128)(2,1)} %get-tuple-element.42), channel_id=1, source_target_pairs={{2,1},{4,3},{6,5},{8,7},{10,9},{12,11},{14,13},{16,15},{18,17},{20... | collective-permute-start | bytes 294920 | tf_op jit(solution)/shard_map/ppermute | solution.py:56
  83.1 31.4 %collective-permute-start.18 = (bf16[2,2,1536]{2,1,0:T(2,128)(2,1)}, bf16[2,2,1536]{2,1,0:T(2,128)(2,1)S(1)}, u32[]{:S(2)}, u32[]{:S(2)}) collective-permute-start(bf16[2,2,1536]{2,1,0:T(2,128)(2,1)} %get-tuple-element.15), channel_id=1, source_target_pairs={{47,48},{1,50},{3,52},{5,54},{7,56},{9,58},{11,60},{13,62},{15,64}... | collective-permute-start | bytes 36872 | tf_op jit(solution)/shard_map/ppermute | solution.py:77
  89.7 26.1 %collective-permute-start.25 = (bf16[2,2,1536]{2,1,0:T(2,128)(2,1)}, bf16[2,2,1536]{2,1,0:T(2,128)(2,1)}, u32[]{:S(2)}, u32[]{:S(2)}) collective-permute-start(bf16[2,2,1536]{2,1,0:T(2,128)(2,1)} %get-tuple-element.16), channel_id=1, source_target_pairs={{51,0},{53,2},{55,4},{57,6},{59,8},{61,10},{63,12},{65,14},{67,16}... | collective-permute-start | bytes 36872 | tf_op jit(solution)/shard_map/ppermute | solution.py:77
  96.0 21.1 %collective-permute-start.23 = (bf16[2,2,1536]{2,1,0:T(2,128)(2,1)}, bf16[2,2,1536]{2,1,0:T(2,128)(2,1)}, u32[]{:S(2)}, u32[]{:S(2)}) collective-permute-start(bf16[2,2,1536]{2,1,0:T(2,128)(2,1)} %get-tuple-element.17), channel_id=1, source_target_pairs={{95,0},{49,2},{51,4},{53,6},{55,8},{57,10},{59,12},{61,14},{63,16}... | collective-permute-start | bytes 36872 | tf_op jit(solution)/shard_map/ppermute | solution.py:77
  97.9 20.5 %collective-permute-start.20 = (bf16[2,2,1536]{2,1,0:T(2,128)(2,1)}, bf16[2,2,1536]{2,1,0:T(2,128)(2,1)}, u32[]{:S(2)}, u32[]{:S(2)}) collective-permute-start(bf16[2,2,1536]{2,1,0:T(2,128)(2,1)} %get-tuple-element.18), channel_id=1, source_target_pairs={{3,48},{5,50},{7,52},{9,54},{11,56},{13,58},{15,60},{17,62},{19,64... | collective-permute-start | bytes 36872 | tf_op jit(solution)/shard_map/ppermute | solution.py:77
  99.8 31.6 %collective-permute-start.17 = (f32[16,8,1536]{2,1,0:T(8,128)}, f32[16,8,1536]{2,1,0:T(8,128)}, u32[]{:S(2)}, u32[]{:S(2)}) collective-permute-start(f32[16,8,1536]{2,1,0:T(8,128)} %slice.202), channel_id=1, source_target_pairs={{1,0},{3,2},{5,4},{7,6},{9,8},{11,10},{13,12},{15,14},{17,16},{19,... | collective-permute-start | bytes 2359304 | tf_op jit(solution)/shard_map/ppermute | solution.py:160
  114.5 16.9 %collective-permute-start.19 = (bf16[2,8,1536]{2,1,0:T(8,128)(2,1)S(1)}, bf16[2,8,1536]{2,1,0:T(8,128)(2,1)S(1)}, u32[]{:S(2)}, u32[]{:S(2)}) collective-permute-start(bf16[2,8,1536]{2,1,0:T(8,128)(2,1)S(1)} %copy-done.17), channel_id=1, source_target_pairs={{1,48},{3,50},{5,52},{7,54},{9,56},{11,58},{13,60},{15,62},{17,64}... | collective-permute-start | bytes 147464 | tf_op jit(solution)/shard_map/ppermute | solution.py:77
  115.8 15.6 %collective-permute-start.24 = (bf16[2,8,1536]{2,1,0:T(8,128)(2,1)S(1)}, bf16[2,8,1536]{2,1,0:T(8,128)(2,1)S(1)}, u32[]{:S(2)}, u32[]{:S(2)}) collective-permute-start(bf16[2,8,1536]{2,1,0:T(8,128)(2,1)S(1)} %copy-done.16), channel_id=1, source_target_pairs={{49,0},{51,2},{53,4},{55,6},{57,8},{59,10},{61,12},{63,14},{65,16}... | collective-permute-start | bytes 147464 | tf_op jit(solution)/shard_map/ppermute | solution.py:77
  117.1 14.3 %collective-permute-start.21 = (bf16[16,2,1536]{2,1,0:T(2,128)(2,1)S(1)}, bf16[16,2,1536]{2,1,0:T(2,128)(2,1)S(1)}, u32[]{:S(2)}, u32[]{:S(2)}) collective-permute-start(bf16[16,2,1536]{2,1,0:T(2,128)(2,1)S(1)} %copy-done.15), channel_id=1, source_target_pairs={{47,0},{1,2},{3,4},{5,6},{7,8},{9,10},{11,12},{13,14},{15,16},{17,... | collective-permute-start | bytes 294920 | tf_op jit(solution)/shard_map/ppermute | solution.py:77
  118.4 13.0 %collective-permute-start.22 = (bf16[16,2,1536]{2,1,0:T(2,128)(2,1)S(1)}, bf16[16,2,1536]{2,1,0:T(2,128)(2,1)S(1)}, u32[]{:S(2)}, u32[]{:S(2)}) collective-permute-start(bf16[16,2,1536]{2,1,0:T(2,128)(2,1)S(1)} %copy-done.14), channel_id=1, source_target_pairs={{3,0},{5,2},{7,4},{9,6},{11,8},{13,10},{15,12},{17,14},{19,16},{21... | collective-permute-start | bytes 294920 | tf_op jit(solution)/shard_map/ppermute | solution.py:77
  155.1 21.0 %collective-permute-start.26 = (bf16[2,2,2,1536]{3,1,0,2:T(2,128)(2,1)S(1)}, bf16[2,2,2,1536]{3,1,0,2:T(2,128)(2,1)S(1)}, u32[]{:S(2)}, u32[]{:S(2)}) collective-permute-start(bf16[2,2,2,1536]{3,1,0,2:T(2,128)(2,1)S(1)} %get-tuple-element.5), channel_id=1, source_target_pairs={{46,48},{47,49},{0,50},{1,51},{2,52},{3,53},{4,54},{5,55},{6,56},{... | collective-permute-start | bytes 73736 | tf_op jit(solution)/shard_map/ppermute | solution.py:77
  157.1 26.6 %collective-permute-start.33 = (bf16[2,2,2,1536]{3,1,0,2:T(2,128)(2,1)S(1)}, bf16[2,2,2,1536]{3,1,0,2:T(2,128)(2,1)S(1)}, u32[]{:S(2)}, u32[]{:S(2)}) collective-permute-start(bf16[2,2,2,1536]{3,1,0,2:T(2,128)(2,1)S(1)} %get-tuple-element.6), channel_id=1, source_target_pairs={{50,0},{51,1},{52,2},{53,3},{54,4},{55,5},{56,6},{57,7},{58,8},{59... | collective-permute-start | bytes 73736 | tf_op jit(solution)/shard_map/ppermute | solution.py:77
  166.4 17.3 %collective-permute-start.31 = (bf16[2,2,2,1536]{3,1,0,2:T(2,128)(2,1)S(1)}, bf16[2,2,2,1536]{3,1,0,2:T(2,128)(2,1)S(1)}, u32[]{:S(2)}, u32[]{:S(2)}) collective-permute-start(bf16[2,2,2,1536]{3,1,0,2:T(2,128)(2,1)S(1)} %get-tuple-element.7), channel_id=1, source_target_pairs={{94,0},{95,1},{48,2},{49,3},{50,4},{51,5},{52,6},{53,7},{54,8},{55... | collective-permute-start | bytes 73736 | tf_op jit(solution)/shard_map/ppermute | solution.py:77
  168.4 22.7 %collective-permute-start.28 = (bf16[2,2,2,1536]{3,1,0,2:T(2,128)(2,1)S(1)}, bf16[2,2,2,1536]{3,1,0,2:T(2,128)(2,1)S(1)}, u32[]{:S(2)}, u32[]{:S(2)}) collective-permute-start(bf16[2,2,2,1536]{3,1,0,2:T(2,128)(2,1)S(1)} %get-tuple-element.8), channel_id=1, source_target_pairs={{2,48},{3,49},{4,50},{5,51},{6,52},{7,53},{8,54},{9,55},{10,56},{1... | collective-permute-start | bytes 73736 | tf_op jit(solution)/shard_map/ppermute | solution.py:77
  174.2 16.9 %collective-permute-start.27 = (bf16[2,8,2,1536]{3,1,0,2:T(8,128)(2,1)S(1)}, bf16[2,8,2,1536]{3,1,0,2:T(8,128)(2,1)S(1)}, u32[]{:S(2)}, u32[]{:S(2)}) collective-permute-start(bf16[2,8,2,1536]{3,1,0,2:T(8,128)(2,1)S(1)} %get-tuple-element.9), channel_id=1, source_target_pairs={{0,48},{1,49},{2,50},{3,51},{4,52},{5,53},{6,54},{7,55},{8,56},{9,... | collective-permute-start | bytes 294920 | tf_op jit(solution)/shard_map/ppermute | solution.py:77
  176.1 15.0 %collective-permute-start.32 = (bf16[2,8,2,1536]{3,1,0,2:T(8,128)(2,1)S(1)}, bf16[2,8,2,1536]{3,1,0,2:T(8,128)(2,1)S(1)}, u32[]{:S(2)}, u32[]{:S(2)}) collective-permute-start(bf16[2,8,2,1536]{3,1,0,2:T(8,128)(2,1)S(1)} %get-tuple-element.10), channel_id=1, source_target_pairs={{48,0},{49,1},{50,2},{51,3},{52,4},{53,5},{54,6},{55,7},{56,8},{57... | collective-permute-start | bytes 294920 | tf_op jit(solution)/shard_map/ppermute | solution.py:77
  (22 other events, 144.7 us)

commit v2 on v1

--- a/solution.py
+++ b/solution.py
@@ -1,8 +1,11 @@
+import functools
 import math
 
 import jax
 import jax.numpy as jnp
 from jax import lax
+from jax.experimental import pallas as pl
+from jax.experimental.pallas import tpu as pltpu
 from jax.sharding import PartitionSpec as P
 
 HEADS = 12
@@ -92,30 +95,82 @@
     return total
 
 
-def probabilities(q3, k3, allowed, scaling):
-    scores = jnp.einsum("thd,phd->htp", q3, k3, preferred_element_type=jnp.float32) * scaling
-    scores = jnp.where(allowed[None, None, :], scores, NEGATIVE)
-    highest = jnp.max(scores, axis=2, keepdims=True)
-    weights = jnp.exp(scores - highest)
-    return weights / jnp.sum(weights, axis=2, keepdims=True)
-
-
-def attend(probs_low, u3):
-    return jnp.einsum("htp,phd->thd", probs_low, u3, preferred_element_type=jnp.float32).astype(
-        jnp.bfloat16
-    )
-
-
-def backward(probs, probs_low, q3, k3, u3, d3, scaling):
-    dprob = jnp.einsum("thd,phd->htp", d3, u3, preferred_element_type=jnp.float32)
-    inner = jnp.sum(probs * dprob, axis=2, keepdims=True)
-    dscore = (probs * (dprob - inner) * scaling).astype(jnp.bfloat16)
-    grad_q = jnp.einsum("htp,phd->thd", dscore, k3, preferred_element_type=jnp.float32).astype(
-        jnp.bfloat16
-    )
-    kterm = jnp.einsum("htp,thd->phd", dscore, q3, preferred_element_type=jnp.float32)
-    vterm = jnp.einsum("htp,thd->phd", probs_low, d3, preferred_element_type=jnp.float32)
-    return grad_q, kterm, vterm
+def attention_kernel(scaling, with_context, with_backward, *refs):
+    mask_ref, q_ref, k_ref, u_ref = refs[:4]
+    refs = refs[4:]
+    if with_backward:
+        d_ref, refs = refs[0], refs[1:]
+    if with_context:
+        c_ref, refs = refs[0], refs[1:]
+    if with_backward:
+        gq_ref, kt_ref, vt_ref = refs
+    head_dim = q_ref.shape[1] // HEADS
+    nt = (((1,), (1,)), ((), ()))
+
+    def head(h, carry):
+        lanes = pl.ds(pl.multiple_of(h * head_dim, head_dim), head_dim)
+        qh = q_ref[:, lanes]
+        kh = k_ref[:, lanes]
+        uh = u_ref[:, lanes]
+        scores = lax.dot_general(qh, kh, nt, preferred_element_type=jnp.float32) * scaling
+        scores = jnp.where(mask_ref[...] > 0.5, scores, NEGATIVE)
+        highest = jnp.max(scores, axis=1, keepdims=True)
+        weights = jnp.exp(scores - highest)
+        probs = weights / jnp.sum(weights, axis=1, keepdims=True)
+        probs_low = probs.astype(jnp.bfloat16)
+        if with_context:
+            c_ref[:, lanes] = jnp.dot(
+                probs_low, uh, preferred_element_type=jnp.float32
+            ).astype(c_ref.dtype)
+        if with_backward:
+            dh = d_ref[:, lanes]
+            dprob = lax.dot_general(dh, uh, nt, preferred_element_type=jnp.float32)
+            inner = jnp.sum(probs * dprob, axis=1, keepdims=True)
+            dscore = probs * (dprob - inner) * scaling
+            gq_ref[:, lanes] = jnp.dot(
+                dscore.astype(jnp.bfloat16), kh, preferred_element_type=jnp.float32
+            ).astype(gq_ref.dtype)
+            kt_ref[:, lanes] = jnp.dot(
+                dscore.T.astype(jnp.bfloat16), qh, preferred_element_type=jnp.float32
+            )
+            vt_ref[:, lanes] = jnp.dot(
+                probs.T.astype(jnp.bfloat16), dh, preferred_element_type=jnp.float32
+            )
+        return carry
+
+    lax.fori_loop(0, HEADS, head, 0)
+
+
+def attention(mask, q, k, u, d=None, with_context=True, scaling=1.0):
+    tokens, features = q.shape
+    keys = k.shape[0]
+    with_backward = d is not None
+    outs = []
+    if with_context:
+        outs.append(jax.ShapeDtypeStruct((tokens, features), jnp.bfloat16))
+    if with_backward:
+        outs += [
+            jax.ShapeDtypeStruct((tokens, features), jnp.bfloat16),
+            jax.ShapeDtypeStruct((keys, features), jnp.float32),
+            jax.ShapeDtypeStruct((keys, features), jnp.float32),
+        ]
+    args = [mask, q, k, u] + ([d] if with_backward else [])
+    matmuls = (1 if with_context else 0) + (5 if with_backward else 1)
+    flops = 2 * tokens * keys * features * matmuls
+    bytes_accessed = sum(a.size * a.dtype.itemsize for a in args) + sum(
+        math.prod(o.shape) * o.dtype.itemsize for o in outs
+    )
+    vmem = pl.BlockSpec(memory_space=pltpu.VMEM)
+    return pl.pallas_call(
+        functools.partial(attention_kernel, scaling, with_context, with_backward),
+        out_shape=outs,
+        in_specs=[vmem] * len(args),
+        out_specs=[vmem] * len(outs),
+        cost_estimate=pl.CostEstimate(
+            flops=flops, transcendentals=tokens * keys * HEADS, bytes_accessed=bytes_accessed
+        ),
+        compiler_params=pltpu.CompilerParams(vmem_limit_bytes=48 * 1024 * 1024),
+    )(*args)
 
 
 def body(queries_keys, values, cotangent):
@@ -126,44 +181,49 @@
     rows_ext = tile_rows + 2 * margin
     cols_ext = tile_cols + 2 * margin
     window_size = rows_ext * cols_ext
+    keys = -(-window_size // 128) * 128
     token_count = tile_rows * tile_cols
-    head_dim = features // HEADS
-    scaling = 1.0 / math.sqrt(head_dim)
-
-    q3 = queries_keys[0, 0].reshape(token_count, HEADS, head_dim)
+    scaling = 1.0 / math.sqrt(features // HEADS)
+
+    def flat_keys(window):
+        flat = window.reshape(window_size, features)
+        return jnp.concatenate([flat, jnp.zeros((keys - window_size, features), flat.dtype)], axis=0)
+
+    def window_of(flat):
+        return flat[:window_size].reshape(rows_ext, cols_ext, features)
+
+    q = queries_keys[0, 0].reshape(token_count, features)
     lat_rows = lax.axis_index("lat") * tile_rows - margin + jnp.arange(rows_ext, dtype=jnp.int32)
     inside = (lat_rows >= 0) & (lat_rows < tile_rows * sizes[0])
     allowed = jnp.broadcast_to(inside[:, None], (rows_ext, cols_ext)).reshape(window_size)
+    allowed = jnp.concatenate([allowed, jnp.zeros((keys - window_size,), bool)])
+    mask = allowed.astype(jnp.float32)[None, :]
 
     kv = gather_window(jnp.stack([queries_keys[0, 1], values[0]], axis=2), sizes)
-    k3 = kv[:, :, 0].reshape(window_size, HEADS, head_dim)
+    k = flat_keys(kv[:, :, 0])
     v_win = kv[:, :, 1]
 
-    probs_a = probabilities(q3, k3, allowed, scaling)
-    context_a = attend(probs_a.astype(jnp.bfloat16), v_win.reshape(window_size, HEADS, head_dim))
+    (context_a,) = attention(mask, q, k, flat_keys(v_win), scaling=scaling)
     context_a = context_a.reshape(tile_rows, tile_cols, features)
 
     c_win = gather_window(context_a, sizes, src_pipe=0, dst_pipe=1)
     u_win = (v_win.astype(jnp.float32) + c_win.astype(jnp.float32)).astype(jnp.bfloat16)
-    u3 = u_win.reshape(window_size, HEADS, head_dim)
-
-    probs_b = probabilities(q3, k3, allowed, scaling)
-    probs_b_low = probs_b.astype(jnp.bfloat16)
-    context_b = attend(probs_b_low, u3).reshape(tile_rows, tile_cols, features)
-    d3_b = cotangent.reshape(token_count, HEADS, head_dim)
-    gq_b, kterm_b, vterm_b = backward(probs_b, probs_b_low, q3, k3, u3, d3_b, scaling)
-    vterm_b = vterm_b.reshape(rows_ext, cols_ext, features)
-    kterm_b = kterm_b.reshape(rows_ext, cols_ext, features)
+    u = flat_keys(u_win)
+
+    d_b = cotangent.reshape(token_count, features)
+    context_b, gq_b, kterm_b, vterm_b = attention(mask, q, k, u, d_b, scaling=scaling)
+    context_b = context_b.reshape(tile_rows, tile_cols, features)
+    kterm_b = window_of(kterm_b)
+    vterm_b = window_of(vterm_b)
 
     centre = slice(margin, margin + tile_rows), slice(margin, margin + tile_cols)
     got = scatter_pieces(vterm_b, sizes, src_pipe=1, dst_pipe=0)
     own_b = lax.ppermute(vterm_b[centre], AXES, pairs_from((0, 0), sizes, 1, 0))
-    d_c = sum_pieces(own_b, got).astype(jnp.bfloat16)
-
-    d3_c = d_c.reshape(token_count, HEADS, head_dim)
-    gq_c, kterm_c, vterm_c = backward(probs_b, probs_b_low, q3, k3, u3, d3_c, scaling)
-    kterm_c = kterm_c.reshape(rows_ext, cols_ext, features)
-    vterm_c = vterm_c.reshape(rows_ext, cols_ext, features)
+    d_c = sum_pieces(own_b, got).astype(jnp.bfloat16).reshape(token_count, features)
+
+    gq_c, kterm_c, vterm_c = attention(mask, q, k, u, d_c, with_context=False, scaling=scaling)
+    kterm_c = window_of(kterm_c)
+    vterm_c = window_of(vterm_c)
 
     terms = jnp.where(
         is_first, jnp.stack([kterm_c, vterm_c], axis=2), jnp.stack([kterm_b, vterm_b], axis=2)

time: 197 us -> 195 us (0.990)
  matrix products: 25.8 us -> 0 us
  Pallas kernels: 0 us -> 24.4 us
  waiting for transfers between devices: 3.25 us -> 17.8 us
  local copies, waits for them, and re-layouts: 42.7 us -> 36.2 us
  starting transfers between devices: 104 us -> 98 us
  other arithmetic: 18.2 us -> 15 us
    pallas_call x0 -> x3, Pallas kernels: none -> 24.4 us  [attention(): pl.pallas_call(functools.partial(attention_kernel, scaling, with_context,...]
    dot_general x10 -> x0, matrix products: 23.8 us -> none  [the longest x2 9.12 us: backward(): jnp.einsum('htp,thd->phd', dscore, q3, preferred_element_type=jnp.float32)]
    ppermute x17, waiting for transfers between devices: 3.2 us -> 14.7 us  [gather_window(): lax.ppermute(part, AXES, pairs_from(off, sizes, src_pipe, dst_pipe))]
    slice x1 -> x4, local copies, waits for them, and re-layouts: 1.22 us -> 7.79 us  [window_of(): return flat[:window_size].reshape(rows_ext, cols_ext, features)]
    ppermute x16, starting transfers between devices: 53.2 us -> 47.1 us  [scatter_pieces(): lax.ppermute(part, AXES, pairs_from(off, sizes, src_pipe, dst_pipe))]
    transpose x4 -> x0, local copies, waits for them, and re-layouts: 5.96 us -> none  [the longest x2 4.95 us: backward(): jnp.einsum('htp,thd->phd', dscore, q3, preferred_element_type=jnp.float32)]
    slice x7 -> x3, local copies, waits for them, and re-layouts: 4.24 us -> 0.18 us  [gather_window(): part = tile[edge(rows, dl), edge(cols, dn)]]
    ppermute x16, waiting for transfers between devices: 0.04 us -> 3.11 us  [scatter_pieces(): lax.ppermute(part, AXES, pairs_from(off, sizes, src_pipe, dst_pipe))]
  transfers between devices with their start and end apart: 34 -> 34, of which waited for: 1 -> 8; matrix products, arithmetic and copies ran while one was open for 23% -> 5% of each run, Pallas kernels for 0% -> 0%
where the time goes in v2:
time: 195 us; the launch traced here: 193 us
  starting transfers between devices  98 us (50%)
  local copies, waits for them, and re-layouts  36.2 us (19%)
  Pallas kernels  24.4 us (13%)
  waiting for transfers between devices  17.8 us (9%)
  other arithmetic  15 us (8%)
    ppermute x17, starting transfers between devices, gather_window(): lax.ppermute(part, AXES, pairs_from(off, sizes, src_pipe, dst_pipe))  48.7 us
    ppermute x16, starting transfers between devices, scatter_pieces(): lax.ppermute(part, AXES, pairs_from(off, sizes, src_pipe, dst_pipe))  47.1 us
    pallas_call x3, Pallas kernels, attention(): pl.pallas_call(functools.partial(attention_kernel, scaling, with_context,...  24.4 us
    ppermute x17, waiting for transfers between devices, gather_window(): lax.ppermute(part, AXES, pairs_from(off, sizes, src_pipe, dst_pipe))  14.7 us
    slice x4, local copies, waits for them, and re-layouts, window_of(): return flat[:window_size].reshape(rows_ext, cols_ext, features)  7.79 us
    another operation x2, other arithmetic  6.02 us
    another operation x2, local copies, waits for them, and re-layouts, body(): jnp.stack([kterm_c, vterm_c], axis=2)  5.48 us
    another operation x2, local copies, waits for them, and re-layouts, body(): jnp.stack([kterm_b, vterm_b], axis=2)  5.26 us
  transfers between devices with their start and end apart: 34, of which 8 were waited for; matrix products, arithmetic and copies ran while one was open for 5% of the time, Pallas kernels for 0%

profile of v2, /device:TPU:6, one launch (start us, length us, event | category | flops | bytes accessed | tf_op | source)
XLA Modules:
  0.0 192.6 jit_solution(16690857964401291424)
XLA Ops:
  2.8 2.9 %collective-permute-start = (bf16[2,2,2,1536]{3,1,0,2:T(2,128)(2,1)S(1)}, bf16[2,2,2,1536]{3,1,0,2:T(2,128)(2,1)S(1)}, u32[]{:S(2)}, u32[]{:S(2)}) collective-permute-start(bf16[2,2,2,1536]{3,1,0,2:T(2,128)(2,1)S(1)} %get-tuple-element.39), channel_id=1, source_target_pairs={{46,48},{47,49},{0,50},{1,51},{2,52},{3,53},{4,54},{5,55},{6,56},{... | collective-permute-start | bytes 73736 | tf_op jit(solution)/shard_map/ppermute | solution.py:59
  5.7 8.1 %collective-permute-start.5 = (bf16[2,2,2,1536]{3,1,0,2:T(2,128)(2,1)S(1)}, bf16[2,2,2,1536]{3,1,0,2:T(2,128)(2,1)S(1)}, u32[]{:S(2)}, u32[]{:S(2)}) collective-permute-start(bf16[2,2,2,1536]{3,1,0,2:T(2,128)(2,1)S(1)} %get-tuple-element.40), channel_id=1, source_target_pairs={{94,0},{95,1},{48,2},{49,3},{50,4},{51,5},{52,6},{53,7},{54,8},{55... | collective-permute-start | bytes 73736 | tf_op jit(solution)/shard_map/ppermute | solution.py:59
  13.8 10.6 %collective-permute-start.7 = (bf16[2,2,2,1536]{3,1,0,2:T(2,128)(2,1)S(1)}, bf16[2,2,2,1536]{3,1,0,2:T(2,128)(2,1)S(1)}, u32[]{:S(2)}, u32[]{:S(2)}) collective-permute-start(bf16[2,2,2,1536]{3,1,0,2:T(2,128)(2,1)S(1)} %get-tuple-element.41), channel_id=1, source_target_pairs={{50,0},{51,1},{52,2},{53,3},{54,4},{55,5},{56,6},{57,7},{58,8},{59... | collective-permute-start | bytes 73736 | tf_op jit(solution)/shard_map/ppermute | solution.py:59
  25.0 2.9 %collective-permute-start.4 = (bf16[16,2,2,1536]{3,1,0,2:T(2,128)(2,1)S(1)}, bf16[16,2,2,1536]{3,1,0,2:T(2,128)(2,1)S(1)}, u32[]{:S(2)}, u32[]{:S(2)}) collective-permute-start(bf16[16,2,2,1536]{3,1,0,2:T(2,128)(2,1)S(1)} %get-tuple-element.46), channel_id=1, source_target_pairs={{2,0},{3,1},{4,2},{5,3},{6,4},{7,5},{8,6},{9,7},{10,8},{11,9},{12,... | collective-permute-start | bytes 589832 | tf_op jit(solution)/shard_map/ppermute | solution.py:59
  28.2 3.0 %collective-permute-start.2 = (bf16[2,2,2,1536]{3,1,0,2:T(2,128)(2,1)S(1)}, bf16[2,2,2,1536]{3,1,0,2:T(2,128)(2,1)S(1)}, u32[]{:S(2)}, u32[]{:S(2)}) collective-permute-start(bf16[2,2,2,1536]{3,1,0,2:T(2,128)(2,1)S(1)} %get-tuple-element.42), channel_id=1, source_target_pairs={{2,48},{3,49},{4,50},{5,51},{6,52},{7,53},{8,54},{9,55},{10,56},{1... | collective-permute-start | bytes 73736 | tf_op jit(solution)/shard_map/ppermute | solution.py:59
  31.2 1.9 collective-permute-start.1
  33.2 7.5 %collective-permute-start.6 = (bf16[2,8,2,1536]{3,1,0,2:T(8,128)(2,1)S(1)}, bf16[2,8,2,1536]{3,1,0,2:T(8,128)(2,1)S(1)}, u32[]{:S(2)}, u32[]{:S(2)}) collective-permute-start(bf16[2,8,2,1536]{3,1,0,2:T(8,128)(2,1)S(1)} %get-tuple-element.44), channel_id=1, source_target_pairs={{48,0},{49,1},{50,2},{51,3},{52,4},{53,5},{54,6},{55,7},{56,8},{57... | collective-permute-start | bytes 294920 | tf_op jit(solution)/shard_map/ppermute | solution.py:59
  49.1 5.7 %shard_map.58 = bf16[128,1536]{1,0:T(8,128)(2,1)S(1)} custom-call(f32[1,256]{1,0:T(1,128)S(1)} %bitcast.32, bf16[128,1536]{1,0:T(8,128)(2,1)S(1)} %get-tuple-element.48.refs_1_, bf16[256,1536]{1,0:T(8,128)(2,1)S(1)} %concatenate.41.refs_2_, bf16[256,1536]{1,0:T(8,128)(2,1)S(1)} %concatenate.42.refs_3_), custom_call_target="tpu_custom_call" | custom-call | flops 201326592 | bytes 2360320 | tf_op jit(solution)/shard_map/pallas_call | solution.py:164
  61.5 3.8 %collective-permute-done.8 = bf16[2,2,1536]{2,1,0:T(2,128)(2,1)S(1)} collective-permute-done((bf16[2,2,1536]{2,1,0:T(2,128)(2,1)S(1)}, bf16[2,2,1536]{2,1,0:T(2,128)(2,1)S(1)}, u32[]{:S(2)}, u32[]{:S(2)}) %collective-permute-start.8) | collective-permute-done | bytes 12320 | tf_op jit(solution)/shard_map/ppermute | solution.py:59
  70.5 7.4 %collective-permute-done.9 = bf16[2,8,1536]{2,1,0:T(8,128)(2,1)S(1)} collective-permute-done((bf16[2,8,1536]{2,1,0:T(8,128)(2,1)S(1)}, bf16[2,8,1536]{2,1,0:T(8,128)(2,1)S(1)}, u32[]{:S(2)}, u32[]{:S(2)}) %collective-permute-start.9) | collective-permute-done | bytes 49184 | tf_op jit(solution)/shard_map/ppermute | solution.py:59
  82.8 10.8 %shard_map.59 = (bf16[128,1536]{1,0:T(8,128)(2,1)S(1)}, bf16[128,1536]{1,0:T(8,128)(2,1)S(1)}, f32[256,1536]{1,0:T(8,128)S(1)}, f32[256,1536]{1,0:T(8,128)}) custom-call(f32[1,256]{1,0:T(1,128)S(1)} %bitcast.33, bf16[128,1536]{1,0:T(8,128)(2,1)S(1)} %get-tuple-element.48.refs_1_, bf16[256,1536]{1,0:T(8,128)(2,1)S(1)} %concatenate.41.refs_2_, ...), custom_call_target="tpu_custom_call" | custom-call | flops 603979776 | bytes 6292480 | tf_op jit(solution)/shard_map/pallas_call | solution.py:164
  94.8 2.6 %slice.176 = f32[240,1536]{1,0:T(8,128)} slice(f32[256,1536]{1,0:T(8,128)} %get-tuple-element.11), slice={[0:240], [0:1536]} | slice | bytes 2949120 | tf_op jit(solution)/shard_map/slice | solution.py:193
  97.4 2.6 %reshape.58 = f32[20,12,1536]{2,1,0:T(8,128)} reshape(f32[240,1536]{1,0:T(8,128)} %slice.176) | data formatting | bytes 2949120 | tf_op jit(solution)/shard_map/reshape | solution.py:193
  100.0 2.4 %slice.218 = f32[16,8,1536]{2,1,0:T(8,128)} slice(f32[20,12,1536]{2,1,0:T(8,128)} %reshape.58), slice={[2:18], [2:10], [0:1536]} | slice | bytes 1572864 | tf_op jit(solution)/shard_map/slice | solution.py:221
  105.4 2.5 %collective-permute-start.25 = (bf16[2,2,1536]{2,1,0:T(2,128)(2,1)S(1)}, bf16[2,2,1536]{2,1,0:T(2,128)(2,1)S(1)}, u32[]{:S(2)}, u32[]{:S(2)}) collective-permute-start(bf16[2,2,1536]{2,1,0:T(2,128)(2,1)S(1)} %get-tuple-element.30), channel_id=1, source_target_pairs={{51,0},{53,2},{55,4},{57,6},{59,8},{61,10},{63,12},{65,14},{67,16}... | collective-permute-start | bytes 36872 | tf_op jit(solution)/shard_map/ppermute | solution.py:80
  107.9 2.2 %collective-permute-start.17 = (f32[16,8,1536]{2,1,0:T(8,128)}, f32[16,8,1536]{2,1,0:T(8,128)}, u32[]{:S(2)}, u32[]{:S(2)}) collective-permute-start(f32[16,8,1536]{2,1,0:T(8,128)} %slice.218), channel_id=1, source_target_pairs={{1,0},{3,2},{5,4},{7,6},{9,8},{11,10},{13,12},{15,14},{17,16},{19,... | collective-permute-start | bytes 2359304 | tf_op jit(solution)/shard_map/ppermute | solution.py:221
  120.1 3.5 %collective-permute-start.24 = (bf16[2,8,1536]{2,1,0:T(8,128)(2,1)}, bf16[2,8,1536]{2,1,0:T(8,128)(2,1)}, u32[]{:S(2)}, u32[]{:S(2)}) collective-permute-start(bf16[2,8,1536]{2,1,0:T(8,128)(2,1)} %get-tuple-element.34), channel_id=1, source_target_pairs={{49,0},{51,2},{53,4},{55,6},{57,8},{59,10},{61,12},{63,14},{65,16}... | collective-permute-start | bytes 147464 | tf_op jit(solution)/shard_map/ppermute | solution.py:80
  123.6 2.6 %stack_reshape.19 = f32[20,12,1,1536]{3,1,0,2:T(8,128)} reshape(f32[240,1536]{1,0:T(8,128)} %slice.176) | data formatting | bytes 2949120 | tf_op jit(solution)/shard_map/stack;reshape | solution.py:229
  126.2 2.6 %slice.188 = f32[240,1536]{1,0:T(8,128)} slice(f32[256,1536]{1,0:T(8,128)} %copy-done), slice={[0:240], [0:1536]} | slice | bytes 2949120 | tf_op jit(solution)/shard_map/slice | solution.py:193
  128.8 2.6 %stack_reshape.18 = f32[20,12,1,1536]{3,1,0,2:T(8,128)} reshape(f32[240,1536]{1,0:T(8,128)} %slice.188) | data formatting | bytes 2949120 | tf_op jit(solution)/shard_map/stack;reshape | solution.py:229
  133.4 7.9 %shard_map.60 = (bf16[128,1536]{1,0:T(8,128)(2,1)S(1)}, f32[256,1536]{1,0:T(8,128)S(1)}, f32[256,1536]{1,0:T(8,128)S(1)}) custom-call(f32[1,256]{1,0:T(1,128)S(1)} %bitcast.34, bf16[128,1536]{1,0:T(8,128)(2,1)S(1)} %get-tuple-element.48.refs_1_, bf16[256,1536]{1,0:T(8,128)(2,1)S(1)} %concatenate.41.refs_2_, bf16[256,1536]{1,0:T(8,128)(2,1)S(1)} %concatenate.47.refs_3_, ...), custom_call_target="tpu_custom_call" | custom-call | flops 503316480 | bytes 5899264 | tf_op jit(solution)/shard_map/pallas_call | solution.py:164
  143.8 2.8 %stack_reshape.16 = f32[20,12,1,1536]{3,1,0,2:T(8,128)} reshape(f32[240,1536]{1,0:T(8,128)} %slice.186) | data formatting | bytes 2949120 | tf_op jit(solution)/shard_map/stack;reshape | solution.py:229
  147.9 2.7 %stack_reshape.17 = f32[20,12,1,1536]{3,1,0,2:T(8,128)} reshape(f32[240,1536]{1,0:T(8,128)} %slice.187) | data formatting | bytes 2949120 | tf_op jit(solution)/shard_map/stack;reshape | solution.py:229
  150.6 4.4 %fusion.13 = (bf16[20,12,2,1536]{3,1,0,2:T(8,128)(2,1)S(1)}, f32[20,12,2,1536]{3,1,0,2:T(8,128)S(1)}) fusion(f32[20,12,1,1536]{3,1,0,2:T(8,128)} %stack_reshape.19, f32[20,12,1,1536]{3,1,0,2:T(8,128)} %stack_reshape.18, f32[20,12,1,1536]{3,1,0,2:T(8,128)} %stack_reshape.17, f32[20,12,1,1536]{3,1,0,2:T(8,128)} %stack_reshape.16, pred[]{:T(512)S(6)} %eq.3), kind=kLoop, calls=%fused_computation.42 | loop fusion | flops 2949120 | bytes 10321921 | tf_op jit(solution)/shard_map/convert.41
  155.3 3.5 %collective-permute-start.26 = (bf16[2,2,2,1536]{3,1,0,2:T(2,128)(2,1)S(1)}, bf16[2,2,2,1536]{3,1,0,2:T(2,128)(2,1)S(1)}, u32[]{:S(2)}, u32[]{:S(2)}) collective-permute-start(bf16[2,2,2,1536]{3,1,0,2:T(2,128)(2,1)S(1)} %get-tuple-element.19), channel_id=1, source_target_pairs={{46,48},{47,49},{0,50},{1,51},{2,52},{3,53},{4,54},{5,55},{6,56},{... | collective-permute-start | bytes 73736 | tf_op jit(solution)/shard_map/ppermute | solution.py:80
  158.8 7.8 %collective-permute-start.33 = (bf16[2,2,2,1536]{3,1,0,2:T(2,128)(2,1)S(1)}, bf16[2,2,2,1536]{3,1,0,2:T(2,128)(2,1)S(1)}, u32[]{:S(2)}, u32[]{:S(2)}) collective-permute-start(bf16[2,2,2,1536]{3,1,0,2:T(2,128)(2,1)S(1)} %get-tuple-element.20), channel_id=1, source_target_pairs={{50,0},{51,1},{52,2},{53,3},{54,4},{55,5},{56,6},{57,7},{58,8},{59... | collective-permute-start | bytes 73736 | tf_op jit(solution)/shard_map/ppermute | solution.py:80
  166.7 1.9 collective-permute-start.31
  168.6 5.8 %collective-permute-start.28 = (bf16[2,2,2,1536]{3,1,0,2:T(2,128)(2,1)S(1)}, bf16[2,2,2,1536]{3,1,0,2:T(2,128)(2,1)S(1)}, u32[]{:S(2)}, u32[]{:S(2)}) collective-permute-start(bf16[2,2,2,1536]{3,1,0,2:T(2,128)(2,1)S(1)} %get-tuple-element.22), channel_id=1, source_target_pairs={{2,48},{3,49},{4,50},{5,51},{6,52},{7,53},{8,54},{9,55},{10,56},{1... | collective-permute-start | bytes 73736 | tf_op jit(solution)/shard_map/ppermute | solution.py:80
  174.4 1.9 collective-permute-start.27
  176.3 7.5 %collective-permute-start.32 = (bf16[2,8,2,1536]{3,1,0,2:T(8,128)(2,1)S(1)}, bf16[2,8,2,1536]{3,1,0,2:T(8,128)(2,1)S(1)}, u32[]{:S(2)}, u32[]{:S(2)}) collective-permute-start(bf16[2,8,2,1536]{3,1,0,2:T(8,128)(2,1)S(1)} %get-tuple-element.24), channel_id=1, source_target_pairs={{48,0},{49,1},{50,2},{51,3},{52,4},{53,5},{54,6},{55,7},{56,8},{57... | collective-permute-start | bytes 294920 | tf_op jit(solution)/shard_map/ppermute | solution.py:80
  183.9 2.9 %collective-permute-start.30 = (bf16[16,2,2,1536]{3,1,0,2:T(2,128)(2,1)S(1)}, bf16[16,2,2,1536]{3,1,0,2:T(2,128)(2,1)S(1)}, u32[]{:S(2)}, u32[]{:S(2)}) collective-permute-start(bf16[16,2,2,1536]{3,1,0,2:T(2,128)(2,1)S(1)} %get-tuple-element.26), channel_id=1, source_target_pairs={{2,0},{3,1},{4,2},{5,3},{6,4},{7,5},{8,6},{9,7},{10,8},{11,9},{12,... | collective-permute-start | bytes 589832 | tf_op jit(solution)/shard_map/ppermute | solution.py:80
  187.7 2.5 %collective-permute-done.29 = bf16[16,2,2,1536]{3,1,0,2:T(2,128)(2,1)S(1)} collective-permute-done((bf16[16,2,2,1536]{3,1,0,2:T(2,128)(2,1)S(1)}, bf16[16,2,2,1536]{3,1,0,2:T(2,128)(2,1)S(1)}, u32[]{:S(2)}, u32[]{:S(2)}) %collective-permute-start.29) | collective-permute-done | bytes 196640 | tf_op jit(solution)/shard_map/ppermute | solution.py:80
  (97 shorter events, 51.4 us)
Async XLA Ops:
  2.8 25.3 %collective-permute-start = (bf16[2,2,2,1536]{3,1,0,2:T(2,128)(2,1)S(1)}, bf16[2,2,2,1536]{3,1,0,2:T(2,128)(2,1)S(1)}, u32[]{:S(2)}, u32[]{:S(2)}) collective-permute-start(bf16[2,2,2,1536]{3,1,0,2:T(2,128)(2,1)S(1)} %get-tuple-element.39), channel_id=1, source_target_pairs={{46,48},{47,49},{0,50},{1,51},{2,52},{3,53},{4,54},{5,55},{6,56},{... | collective-permute-start | bytes 73736 | tf_op jit(solution)/shard_map/ppermute | solution.py:59
  5.7 25.5 %collective-permute-start.5 = (bf16[2,2,2,1536]{3,1,0,2:T(2,128)(2,1)S(1)}, bf16[2,2,2,1536]{3,1,0,2:T(2,128)(2,1)S(1)}, u32[]{:S(2)}, u32[]{:S(2)}) collective-permute-start(bf16[2,2,2,1536]{3,1,0,2:T(2,128)(2,1)S(1)} %get-tuple-element.40), channel_id=1, source_target_pairs={{94,0},{95,1},{48,2},{49,3},{50,4},{51,5},{52,6},{53,7},{54,8},{55... | collective-permute-start | bytes 73736 | tf_op jit(solution)/shard_map/ppermute | solution.py:59
  13.8 19.3 %collective-permute-start.7 = (bf16[2,2,2,1536]{3,1,0,2:T(2,128)(2,1)S(1)}, bf16[2,2,2,1536]{3,1,0,2:T(2,128)(2,1)S(1)}, u32[]{:S(2)}, u32[]{:S(2)}) collective-permute-start(bf16[2,2,2,1536]{3,1,0,2:T(2,128)(2,1)S(1)} %get-tuple-element.41), channel_id=1, source_target_pairs={{50,0},{51,1},{52,2},{53,3},{54,4},{55,5},{56,6},{57,7},{58,8},{59... | collective-permute-start | bytes 73736 | tf_op jit(solution)/shard_map/ppermute | solution.py:59
  25.0 17.9 %collective-permute-start.3 = (bf16[16,2,2,1536]{3,1,0,2:T(2,128)(2,1)S(1)}, bf16[16,2,2,1536]{3,1,0,2:T(2,128)(2,1)S(1)}, u32[]{:S(2)}, u32[]{:S(2)}) collective-permute-start(bf16[16,2,2,1536]{3,1,0,2:T(2,128)(2,1)S(1)} %get-tuple-element.45), channel_id=1, source_target_pairs={{46,0},{47,1},{0,2},{1,3},{2,4},{3,5},{4,6},{5,7},{6,8},{7,9},{8,1... | collective-permute-start | bytes 589832 | tf_op jit(solution)/shard_map/ppermute | solution.py:59
  25.0 17.9 %collective-permute-start.4 = (bf16[16,2,2,1536]{3,1,0,2:T(2,128)(2,1)S(1)}, bf16[16,2,2,1536]{3,1,0,2:T(2,128)(2,1)S(1)}, u32[]{:S(2)}, u32[]{:S(2)}) collective-permute-start(bf16[16,2,2,1536]{3,1,0,2:T(2,128)(2,1)S(1)} %get-tuple-element.46), channel_id=1, source_target_pairs={{2,0},{3,1},{4,2},{5,3},{6,4},{7,5},{8,6},{9,7},{10,8},{11,9},{12,... | collective-permute-start | bytes 589832 | tf_op jit(solution)/shard_map/ppermute | solution.py:59
  28.2 12.6 %collective-permute-start.2 = (bf16[2,2,2,1536]{3,1,0,2:T(2,128)(2,1)S(1)}, bf16[2,2,2,1536]{3,1,0,2:T(2,128)(2,1)S(1)}, u32[]{:S(2)}, u32[]{:S(2)}) collective-permute-start(bf16[2,2,2,1536]{3,1,0,2:T(2,128)(2,1)S(1)} %get-tuple-element.42), channel_id=1, source_target_pairs={{2,48},{3,49},{4,50},{5,51},{6,52},{7,53},{8,54},{9,55},{10,56},{1... | collective-permute-start | bytes 73736 | tf_op jit(solution)/shard_map/ppermute | solution.py:59
  31.2 10.1 %collective-permute-start.1 = (bf16[2,8,2,1536]{3,1,0,2:T(8,128)(2,1)S(1)}, bf16[2,8,2,1536]{3,1,0,2:T(8,128)(2,1)S(1)}, u32[]{:S(2)}, u32[]{:S(2)}) collective-permute-start(bf16[2,8,2,1536]{3,1,0,2:T(8,128)(2,1)S(1)} %get-tuple-element.43), channel_id=1, source_target_pairs={{0,48},{1,49},{2,50},{3,51},{4,52},{5,53},{6,54},{7,55},{8,56},{9,... | collective-permute-start | bytes 294920 | tf_op jit(solution)/shard_map/ppermute | solution.py:59
  33.2 9.7 %collective-permute-start.6 = (bf16[2,8,2,1536]{3,1,0,2:T(8,128)(2,1)S(1)}, bf16[2,8,2,1536]{3,1,0,2:T(8,128)(2,1)S(1)}, u32[]{:S(2)}, u32[]{:S(2)}) collective-permute-start(bf16[2,8,2,1536]{3,1,0,2:T(8,128)(2,1)S(1)} %get-tuple-element.44), channel_id=1, source_target_pairs={{48,0},{49,1},{50,2},{51,3},{52,4},{53,5},{54,6},{55,7},{56,8},{57... | collective-permute-start | bytes 294920 | tf_op jit(solution)/shard_map/ppermute | solution.py:59
  54.9 10.4 %collective-permute-start.8 = (bf16[2,2,1536]{2,1,0:T(2,128)(2,1)S(1)}, bf16[2,2,1536]{2,1,0:T(2,128)(2,1)S(1)}, u32[]{:S(2)}, u32[]{:S(2)}) collective-permute-start(bf16[2,2,1536]{2,1,0:T(2,128)(2,1)S(1)} %get-tuple-element.49), channel_id=1, source_target_pairs={{46,49},{0,51},{2,53},{4,55},{6,57},{8,59},{10,61},{12,63},{14,65}... | collective-permute-start | bytes 36872 | tf_op jit(solution)/shard_map/ppermute | solution.py:59
  56.2 10.4 %collective-permute-start.16 = (bf16[2,2,1536]{2,1,0:T(2,128)(2,1)S(1)}, bf16[2,2,1536]{2,1,0:T(2,128)(2,1)S(1)}, u32[]{:S(2)}, u32[]{:S(2)}) collective-permute-start(bf16[2,2,1536]{2,1,0:T(2,128)(2,1)S(1)} %get-tuple-element.50), channel_id=1, source_target_pairs={{50,1},{52,3},{54,5},{56,7},{58,9},{60,11},{62,13},{64,15},{66,17}... | collective-permute-start | bytes 36872 | tf_op jit(solution)/shard_map/ppermute | solution.py:59
  57.6 21.6 %collective-permute-start.12 = (bf16[16,8,1536]{2,1,0:T(8,128)(2,1)S(1)}, bf16[16,8,1536]{2,1,0:T(8,128)(2,1)S(1)}, u32[]{:S(2)}, u32[]{:S(2)}) collective-permute-start(bf16[16,8,1536]{2,1,0:T(8,128)(2,1)S(1)} %bitcast.30), channel_id=1, source_target_pairs={{0,1},{2,3},{4,5},{6,7},{8,9},{10,11},{12,13},{14,15},{16,17},{18,... | collective-permute-start | bytes 1179656 | tf_op jit(solution)/shard_map/ppermute | solution.py:59
  58.9 9.0 %collective-permute-start.14 = (bf16[2,2,1536]{2,1,0:T(2,128)(2,1)S(1)}, bf16[2,2,1536]{2,1,0:T(2,128)(2,1)S(1)}, u32[]{:S(2)}, u32[]{:S(2)}) collective-permute-start(bf16[2,2,1536]{2,1,0:T(2,128)(2,1)S(1)} %get-tuple-element.51), channel_id=1, source_target_pairs={{94,1},{48,3},{50,5},{52,7},{54,9},{56,11},{58,13},{60,15},{62,17}... | collective-permute-start | bytes 36872 | tf_op jit(solution)/shard_map/ppermute | solution.py:59
  60.2 9.0 %collective-permute-start.10 = (bf16[2,2,1536]{2,1,0:T(2,128)(2,1)S(1)}, bf16[2,2,1536]{2,1,0:T(2,128)(2,1)S(1)}, u32[]{:S(2)}, u32[]{:S(2)}) collective-permute-start(bf16[2,2,1536]{2,1,0:T(2,128)(2,1)S(1)} %get-tuple-element.52), channel_id=1, source_target_pairs={{2,49},{4,51},{6,53},{8,55},{10,57},{12,59},{14,61},{16,63},{18,65... | collective-permute-start | bytes 36872 | tf_op jit(solution)/shard_map/ppermute | solution.py:59
  65.3 12.6 %collective-permute-start.11 = (bf16[16,2,1536]{2,1,0:T(2,128)(2,1)S(1)}, bf16[16,2,1536]{2,1,0:T(2,128)(2,1)S(1)}, u32[]{:S(2)}, u32[]{:S(2)}) collective-permute-start(bf16[16,2,1536]{2,1,0:T(2,128)(2,1)S(1)} %get-tuple-element.55), channel_id=1, source_target_pairs={{46,1},{0,3},{2,5},{4,7},{6,9},{8,11},{10,13},{12,15},{14,17},{16,... | collective-permute-start | bytes 294920 | tf_op jit(solution)/shard_map/ppermute | solution.py:59
  66.6 12.5 %collective-permute-start.13 = (bf16[16,2,1536]{2,1,0:T(2,128)(2,1)S(1)}, bf16[16,2,1536]{2,1,0:T(2,128)(2,1)S(1)}, u32[]{:S(2)}, u32[]{:S(2)}) collective-permute-start(bf16[16,2,1536]{2,1,0:T(2,128)(2,1)S(1)} %get-tuple-element.56), channel_id=1, source_target_pairs={{2,1},{4,3},{6,5},{8,7},{10,9},{12,11},{14,13},{16,15},{18,17},{20... | collective-permute-start | bytes 294920 | tf_op jit(solution)/shard_map/ppermute | solution.py:59
  67.9 10.0 %collective-permute-start.9 = (bf16[2,8,1536]{2,1,0:T(8,128)(2,1)S(1)}, bf16[2,8,1536]{2,1,0:T(8,128)(2,1)S(1)}, u32[]{:S(2)}, u32[]{:S(2)}) collective-permute-start(bf16[2,8,1536]{2,1,0:T(8,128)(2,1)S(1)} %get-tuple-element.53), channel_id=1, source_target_pairs={{0,49},{2,51},{4,53},{6,55},{8,57},{10,59},{12,61},{14,63},{16,65}... | collective-permute-start | bytes 147464 | tf_op jit(solution)/shard_map/ppermute | solution.py:59
  69.2 8.7 %collective-permute-start.15 = (bf16[2,8,1536]{2,1,0:T(8,128)(2,1)S(1)}, bf16[2,8,1536]{2,1,0:T(8,128)(2,1)S(1)}, u32[]{:S(2)}, u32[]{:S(2)}) collective-permute-start(bf16[2,8,1536]{2,1,0:T(8,128)(2,1)S(1)} %get-tuple-element.54), channel_id=1, source_target_pairs={{48,1},{50,3},{52,5},{54,7},{56,9},{58,11},{60,13},{62,15},{64,17}... | collective-permute-start | bytes 147464 | tf_op jit(solution)/shard_map/ppermute | solution.py:59
  104.1 9.9 %collective-permute-start.18 = (bf16[2,2,1536]{2,1,0:T(2,128)(2,1)S(1)}, bf16[2,2,1536]{2,1,0:T(2,128)(2,1)S(1)}, u32[]{:S(2)}, u32[]{:S(2)}) collective-permute-start(bf16[2,2,1536]{2,1,0:T(2,128)(2,1)S(1)} %get-tuple-element.29), channel_id=1, source_target_pairs={{47,48},{1,50},{3,52},{5,54},{7,56},{9,58},{11,60},{13,62},{15,64}... | collective-permute-start | bytes 36872 | tf_op jit(solution)/shard_map/ppermute | solution.py:80
  105.4 9.9 %collective-permute-start.25 = (bf16[2,2,1536]{2,1,0:T(2,128)(2,1)S(1)}, bf16[2,2,1536]{2,1,0:T(2,128)(2,1)S(1)}, u32[]{:S(2)}, u32[]{:S(2)}) collective-permute-start(bf16[2,2,1536]{2,1,0:T(2,128)(2,1)S(1)} %get-tuple-element.30), channel_id=1, source_target_pairs={{51,0},{53,2},{55,4},{57,6},{59,8},{61,10},{63,12},{65,14},{67,16}... | collective-permute-start | bytes 36872 | tf_op jit(solution)/shard_map/ppermute | solution.py:80
  107.9 24.1 %collective-permute-start.17 = (f32[16,8,1536]{2,1,0:T(8,128)}, f32[16,8,1536]{2,1,0:T(8,128)}, u32[]{:S(2)}, u32[]{:S(2)}) collective-permute-start(f32[16,8,1536]{2,1,0:T(8,128)} %slice.218), channel_id=1, source_target_pairs={{1,0},{3,2},{5,4},{7,6},{9,8},{11,10},{13,12},{15,14},{17,16},{19,... | collective-permute-start | bytes 2359304 | tf_op jit(solution)/shard_map/ppermute | solution.py:221
  110.3 7.9 %collective-permute-start.23 = (bf16[2,2,1536]{2,1,0:T(2,128)(2,1)S(1)}, bf16[2,2,1536]{2,1,0:T(2,128)(2,1)}, u32[]{:S(2)}, u32[]{:S(2)}) collective-permute-start(bf16[2,2,1536]{2,1,0:T(2,128)(2,1)S(1)} %get-tuple-element.31), channel_id=1, source_target_pairs={{95,0},{49,2},{51,4},{53,6},{55,8},{57,10},{59,12},{61,14},{63,16}... | collective-permute-start | bytes 36872 | tf_op jit(solution)/shard_map/ppermute | solution.py:80
  112.2 7.9 %collective-permute-start.20 = (bf16[2,2,1536]{2,1,0:T(2,128)(2,1)S(1)}, bf16[2,2,1536]{2,1,0:T(2,128)(2,1)}, u32[]{:S(2)}, u32[]{:S(2)}) collective-permute-start(bf16[2,2,1536]{2,1,0:T(2,128)(2,1)S(1)} %get-tuple-element.32), channel_id=1, source_target_pairs={{3,48},{5,50},{7,52},{9,54},{11,56},{13,58},{15,60},{17,62},{19,64... | collective-permute-start | bytes 36872 | tf_op jit(solution)/shard_map/ppermute | solution.py:80
  114.1 17.9 %collective-permute-start.21 = (bf16[16,2,1536]{2,1,0:T(2,128)(2,1)S(1)}, bf16[16,2,1536]{2,1,0:T(2,128)(2,1)S(1)}, u32[]{:S(2)}, u32[]{:S(2)}) collective-permute-start(bf16[16,2,1536]{2,1,0:T(2,128)(2,1)S(1)} %get-tuple-element.35), channel_id=1, source_target_pairs={{47,0},{1,2},{3,4},{5,6},{7,8},{9,10},{11,12},{13,14},{15,16},{17,... | collective-permute-start | bytes 294920 | tf_op jit(solution)/shard_map/ppermute | solution.py:80
  116.0 16.0 %collective-permute-start.22 = (bf16[16,2,1536]{2,1,0:T(2,128)(2,1)S(1)}, bf16[16,2,1536]{2,1,0:T(2,128)(2,1)S(1)}, u32[]{:S(2)}, u32[]{:S(2)}) collective-permute-start(bf16[16,2,1536]{2,1,0:T(2,128)(2,1)S(1)} %get-tuple-element.36), channel_id=1, source_target_pairs={{3,0},{5,2},{7,4},{9,6},{11,8},{13,10},{15,12},{17,14},{19,16},{21... | collective-permute-start | bytes 294920 | tf_op jit(solution)/shard_map/ppermute | solution.py:80
  118.2 13.3 %collective-permute-start.19 = (bf16[2,8,1536]{2,1,0:T(8,128)(2,1)}, bf16[2,8,1536]{2,1,0:T(8,128)(2,1)}, u32[]{:S(2)}, u32[]{:S(2)}) collective-permute-start(bf16[2,8,1536]{2,1,0:T(8,128)(2,1)} %get-tuple-element.33), channel_id=1, source_target_pairs={{1,48},{3,50},{5,52},{7,54},{9,56},{11,58},{13,60},{15,62},{17,64}... | collective-permute-start | bytes 147464 | tf_op jit(solution)/shard_map/ppermute | solution.py:80
  120.1 11.4 %collective-permute-start.24 = (bf16[2,8,1536]{2,1,0:T(8,128)(2,1)}, bf16[2,8,1536]{2,1,0:T(8,128)(2,1)}, u32[]{:S(2)}, u32[]{:S(2)}) collective-permute-start(bf16[2,8,1536]{2,1,0:T(8,128)(2,1)} %get-tuple-element.34), channel_id=1, source_target_pairs={{49,0},{51,2},{53,4},{55,6},{57,8},{59,10},{61,12},{63,14},{65,16}... | collective-permute-start | bytes 147464 | tf_op jit(solution)/shard_map/ppermute | solution.py:80
  155.3 21.0 %collective-permute-start.26 = (bf16[2,2,2,1536]{3,1,0,2:T(2,128)(2,1)S(1)}, bf16[2,2,2,1536]{3,1,0,2:T(2,128)(2,1)S(1)}, u32[]{:S(2)}, u32[]{:S(2)}) collective-permute-start(bf16[2,2,2,1536]{3,1,0,2:T(2,128)(2,1)S(1)} %get-tuple-element.19), channel_id=1, source_target_pairs={{46,48},{47,49},{0,50},{1,51},{2,52},{3,53},{4,54},{5,55},{6,56},{... | collective-permute-start | bytes 73736 | tf_op jit(solution)/shard_map/ppermute | solution.py:80
  158.8 25.0 %collective-permute-start.33 = (bf16[2,2,2,1536]{3,1,0,2:T(2,128)(2,1)S(1)}, bf16[2,2,2,1536]{3,1,0,2:T(2,128)(2,1)S(1)}, u32[]{:S(2)}, u32[]{:S(2)}) collective-permute-start(bf16[2,2,2,1536]{3,1,0,2:T(2,128)(2,1)S(1)} %get-tuple-element.20), channel_id=1, source_target_pairs={{50,0},{51,1},{52,2},{53,3},{54,4},{55,5},{56,6},{57,7},{58,8},{59... | collective-permute-start | bytes 73736 | tf_op jit(solution)/shard_map/ppermute | solution.py:80
  166.7 17.3 %collective-permute-start.31 = (bf16[2,2,2,1536]{3,1,0,2:T(2,128)(2,1)S(1)}, bf16[2,2,2,1536]{3,1,0,2:T(2,128)(2,1)S(1)}, u32[]{:S(2)}, u32[]{:S(2)}) collective-permute-start(bf16[2,2,2,1536]{3,1,0,2:T(2,128)(2,1)S(1)} %get-tuple-element.21), channel_id=1, source_target_pairs={{94,0},{95,1},{48,2},{49,3},{50,4},{51,5},{52,6},{53,7},{54,8},{55... | collective-permute-start | bytes 73736 | tf_op jit(solution)/shard_map/ppermute | solution.py:80
  168.6 19.1 %collective-permute-start.28 = (bf16[2,2,2,1536]{3,1,0,2:T(2,128)(2,1)S(1)}, bf16[2,2,2,1536]{3,1,0,2:T(2,128)(2,1)S(1)}, u32[]{:S(2)}, u32[]{:S(2)}) collective-permute-start(bf16[2,2,2,1536]{3,1,0,2:T(2,128)(2,1)S(1)} %get-tuple-element.22), channel_id=1, source_target_pairs={{2,48},{3,49},{4,50},{5,51},{6,52},{7,53},{8,54},{9,55},{10,56},{1... | collective-permute-start | bytes 73736 | tf_op jit(solution)/shard_map/ppermute | solution.py:80
  174.4 13.3 %collective-permute-start.27 = (bf16[2,8,2,1536]{3,1,0,2:T(8,128)(2,1)S(1)}, bf16[2,8,2,1536]{3,1,0,2:T(8,128)(2,1)S(1)}, u32[]{:S(2)}, u32[]{:S(2)}) collective-permute-start(bf16[2,8,2,1536]{3,1,0,2:T(8,128)(2,1)S(1)} %get-tuple-element.23), channel_id=1, source_target_pairs={{0,48},{1,49},{2,50},{3,51},{4,52},{5,53},{6,54},{7,55},{8,56},{9,... | collective-permute-start | bytes 294920 | tf_op jit(solution)/shard_map/ppermute | solution.py:80
  176.3 11.4 %collective-permute-start.32 = (bf16[2,8,2,1536]{3,1,0,2:T(8,128)(2,1)S(1)}, bf16[2,8,2,1536]{3,1,0,2:T(8,128)(2,1)S(1)}, u32[]{:S(2)}, u32[]{:S(2)}) collective-permute-start(bf16[2,8,2,1536]{3,1,0,2:T(8,128)(2,1)S(1)} %get-tuple-element.24), channel_id=1, source_target_pairs={{48,0},{49,1},{50,2},{51,3},{52,4},{53,5},{54,6},{55,7},{56,8},{57... | collective-permute-start | bytes 294920 | tf_op jit(solution)/shard_map/ppermute | solution.py:80
  (9 other events, 46.3 us)

commit v3 on v2

--- a/solution.py
+++ b/solution.py
@@ -14,7 +14,6 @@
 NEGATIVE = -1e30
 
 AXES = ("lat", "lon", "pipe")
-NEIGHBOURS = [(dl, dn) for dl in (-1, 0, 1) for dn in (-1, 0, 1) if (dl, dn) != (0, 0)]
 
 
 def linear(l, n, p, lons, pipes):
@@ -39,59 +38,79 @@
     return out
 
 
-def edge(length, d):
-    if d == -1:
-        return slice(length - MARGIN, length)
-    if d == 1:
-        return slice(0, MARGIN)
-    return slice(0, length)
-
-
-def gather_window(tile, sizes, src_pipe=None, dst_pipe=None):
-    rows, cols = tile.shape[0], tile.shape[1]
-    pieces = {}
-    for off in [(0, 0)] + NEIGHBOURS:
-        dl, dn = off
-        if off == (0, 0) and src_pipe is None:
-            pieces[off] = tile
-            continue
-        part = tile[edge(rows, dl), edge(cols, dn)]
-        pieces[off] = lax.ppermute(part, AXES, pairs_from(off, sizes, src_pipe, dst_pipe))
-    bands = []
-    for dl in (-1, 0, 1):
-        bands.append(jnp.concatenate([pieces[(dl, dn)] for dn in (-1, 0, 1)], axis=1))
-    return jnp.concatenate(bands, axis=0)
-
-
-def window_part(length, d):
-    if d == -1:
-        return slice(length + MARGIN, length + 2 * MARGIN)
-    if d == 1:
-        return slice(0, MARGIN)
-    return slice(MARGIN, length + MARGIN)
-
-
-def scatter_pieces(window, sizes, src_pipe=None, dst_pipe=None):
-    rows, cols = window.shape[0] - 2 * MARGIN, window.shape[1] - 2 * MARGIN
-    got = {}
-    for off in NEIGHBOURS:
-        dl, dn = off
-        part = window[window_part(rows, dl), window_part(cols, dn)].astype(jnp.bfloat16)
-        got[off] = lax.ppermute(part, AXES, pairs_from(off, sizes, src_pipe, dst_pipe))
-    return got
-
-
-def sum_pieces(centre, got):
-    rows, cols = centre.shape[0], centre.shape[1]
-    total = centre
-    for (dl, dn), piece in got.items():
-        piece = piece.astype(jnp.float32)
-        r0 = 0 if dl <= 0 else rows - MARGIN
-        c0 = 0 if dn <= 0 else cols - MARGIN
-        pr = [(r0, rows - r0 - piece.shape[0])]
-        pc = [(c0, cols - c0 - piece.shape[1])]
-        pad = pr + pc + [(0, 0)] * (piece.ndim - 2)
-        total = total + jnp.pad(piece, pad)
+def shifted(x, offset, sizes, src_pipe=None, dst_pipe=None):
+    return lax.ppermute(x, AXES, pairs_from(offset, sizes, src_pipe, dst_pipe))
+
+
+def flat(x):
+    return x.reshape((-1,) + x.shape[2:])
+
+
+def gather_keys(tile, sizes, src_pipe=None, dst_pipe=None):
+    rows = tile.shape[0]
+    if src_pipe is None:
+        own = tile
+    else:
+        own = shifted(tile, (0, 0), sizes, src_pipe, dst_pipe)
+    top = shifted(tile[rows - MARGIN :], (-1, 0), sizes, src_pipe, dst_pipe)
+    bottom = shifted(tile[:MARGIN], (1, 0), sizes, src_pipe, dst_pipe)
+    ext = jnp.concatenate([top, own, bottom], axis=0)
+    cols = tile.shape[1]
+    left = shifted(ext[:, cols - MARGIN :], (0, -1), sizes)
+    right = shifted(ext[:, :MARGIN], (0, 1), sizes)
+    return [flat(own), flat(top), flat(bottom), flat(left), flat(right)]
+
+
+def piece_bounds(rows, cols):
+    counts = [rows * cols, MARGIN * cols, MARGIN * cols, (rows + 2 * MARGIN) * MARGIN,
+              (rows + 2 * MARGIN) * MARGIN]
+    starts = [sum(counts[:i]) for i in range(len(counts))]
+    return [(s, s + c) for s, c in zip(starts, counts)]
+
+
+def place(piece, rows, cols, r0, c0):
+    pad = [(r0, rows - r0 - piece.shape[0]), (c0, cols - c0 - piece.shape[1])]
+    return jnp.pad(piece.astype(jnp.float32), pad + [(0, 0)] * (piece.ndim - 2))
+
+
+def return_terms(terms, rows, cols, sizes, src_pipe=None, dst_pipe=None):
+    tail = terms.shape[1:]
+    (c0, c1), (t0, t1), (b0, b1), (l0, l1), (r0, r1) = piece_bounds(rows, cols)
+    centre = terms[c0:c1].reshape((rows, cols) + tail)
+    top = terms[t0:t1].astype(jnp.bfloat16)
+    bottom = terms[b0:b1].astype(jnp.bfloat16)
+    strip = (rows + 2 * MARGIN, MARGIN) + tail
+    left = terms[l0:l1].astype(jnp.bfloat16).reshape(strip)
+    right = terms[r0:r1].astype(jnp.bfloat16).reshape(strip)
+    from_right = shifted(left, (0, 1), sizes)
+    from_left = shifted(right, (0, -1), sizes)
+    inner = slice(MARGIN, MARGIN + rows)
+    partial = (
+        centre
+        + place(from_right[inner], rows, cols, 0, cols - MARGIN)
+        + place(from_left[inner], rows, cols, 0, 0)
+    )
+    up = jnp.concatenate(
+        [top, flat(from_left[:MARGIN]), flat(from_right[:MARGIN])], axis=0
+    )
+    down = jnp.concatenate(
+        [bottom, flat(from_left[rows + MARGIN :]), flat(from_right[rows + MARGIN :])], axis=0
+    )
+    if src_pipe is not None:
+        partial = shifted(partial, (0, 0), sizes, src_pipe, dst_pipe)
+    from_below = shifted(up, (1, 0), sizes, src_pipe, dst_pipe)
+    from_above = shifted(down, (-1, 0), sizes, src_pipe, dst_pipe)
+    band = MARGIN * cols
+    corner = MARGIN * MARGIN
+    total = partial
+    for got, r in ((from_above, 0), (from_below, rows - MARGIN)):
+        total = total + place(got[:band].reshape((MARGIN, cols) + tail), rows, cols, r, 0)
+        total = total + place(
+            got[band : band + corner].reshape((MARGIN, MARGIN) + tail), rows, cols, r, 0
+        )
+        total = total + place(
+            got[band + corner :].reshape((MARGIN, MARGIN) + tail), rows, cols, r, cols - MARGIN
+        )
     return total
 
 
@@ -178,60 +197,59 @@
     is_first = lax.axis_index("pipe") == 0
     tile_rows, tile_cols, features = cotangent.shape
     margin = MARGIN
-    rows_ext = tile_rows + 2 * margin
-    cols_ext = tile_cols + 2 * margin
-    window_size = rows_ext * cols_ext
+    token_count = tile_rows * tile_cols
+    bounds = piece_bounds(tile_rows, tile_cols)
+    window_size = bounds[-1][1]
     keys = -(-window_size // 128) * 128
-    token_count = tile_rows * tile_cols
     scaling = 1.0 / math.sqrt(features // HEADS)
 
-    def flat_keys(window):
-        flat = window.reshape(window_size, features)
-        return jnp.concatenate([flat, jnp.zeros((keys - window_size, features), flat.dtype)], axis=0)
-
-    def window_of(flat):
-        return flat[:window_size].reshape(rows_ext, cols_ext, features)
+    def keys_of(pieces):
+        pad = jnp.zeros((keys - window_size,) + pieces[0].shape[1:], pieces[0].dtype)
+        return jnp.concatenate(pieces + [pad], axis=0)
+
+    lat = lax.axis_index("lat")
+    has_above = lat > 0
+    has_below = lat < sizes[0] - 1
+    strip_row = jnp.arange((tile_rows + 2 * margin) * margin, dtype=jnp.int32) // margin
+    strip_ok = ((strip_row >= margin) | has_above) & ((strip_row < tile_rows + margin) | has_below)
+    allowed = jnp.concatenate(
+        [
+            jnp.ones((token_count,), bool),
+            jnp.broadcast_to(has_above, (margin * tile_cols,)),
+            jnp.broadcast_to(has_below, (margin * tile_cols,)),
+            strip_ok,
+            strip_ok,
+            jnp.zeros((keys - window_size,), bool),
+        ]
+    )
+    mask = allowed.astype(jnp.float32)[None, :]
 
     q = queries_keys[0, 0].reshape(token_count, features)
-    lat_rows = lax.axis_index("lat") * tile_rows - margin + jnp.arange(rows_ext, dtype=jnp.int32)
-    inside = (lat_rows >= 0) & (lat_rows < tile_rows * sizes[0])
-    allowed = jnp.broadcast_to(inside[:, None], (rows_ext, cols_ext)).reshape(window_size)
-    allowed = jnp.concatenate([allowed, jnp.zeros((keys - window_size,), bool)])
-    mask = allowed.astype(jnp.float32)[None, :]
-
-    kv = gather_window(jnp.stack([queries_keys[0, 1], values[0]], axis=2), sizes)
-    k = flat_keys(kv[:, :, 0])
-    v_win = kv[:, :, 1]
-
-    (context_a,) = attention(mask, q, k, flat_keys(v_win), scaling=scaling)
-    context_a = context_a.reshape(tile_rows, tile_cols, features)
-
-    c_win = gather_window(context_a, sizes, src_pipe=0, dst_pipe=1)
-    u_win = (v_win.astype(jnp.float32) + c_win.astype(jnp.float32)).astype(jnp.bfloat16)
-    u = flat_keys(u_win)
+
+    kv = keys_of(gather_keys(jnp.stack([queries_keys[0, 1], values[0]], axis=2), sizes))
+    k = kv[:, 0]
+    v = kv[:, 1]
+
+    (context_a,) = attention(mask, q, k, v, scaling=scaling)
+
+    c = keys_of(gather_keys(context_a.reshape(tile_rows, tile_cols, features), sizes, 0, 1))
+    u = (v.astype(jnp.float32) + c.astype(jnp.float32)).astype(jnp.bfloat16)
 
     d_b = cotangent.reshape(token_count, features)
     context_b, gq_b, kterm_b, vterm_b = attention(mask, q, k, u, d_b, scaling=scaling)
-    context_b = context_b.reshape(tile_rows, tile_cols, features)
-    kterm_b = window_of(kterm_b)
-    vterm_b = window_of(vterm_b)
-
-    centre = slice(margin, margin + tile_rows), slice(margin, margin + tile_cols)
-    got = scatter_pieces(vterm_b, sizes, src_pipe=1, dst_pipe=0)
-    own_b = lax.ppermute(vterm_b[centre], AXES, pairs_from((0, 0), sizes, 1, 0))
-    d_c = sum_pieces(own_b, got).astype(jnp.bfloat16).reshape(token_count, features)
-
-    gq_c, kterm_c, vterm_c = attention(mask, q, k, u, d_c, with_context=False, scaling=scaling)
-    kterm_c = window_of(kterm_c)
-    vterm_c = window_of(vterm_c)
+
+    d_c = return_terms(vterm_b, tile_rows, tile_cols, sizes, 1, 0).astype(jnp.bfloat16)
+
+    gq_c, kterm_c, vterm_c = attention(
+        mask, q, k, u, d_c.reshape(token_count, features), with_context=False, scaling=scaling
+    )
 
     terms = jnp.where(
-        is_first, jnp.stack([kterm_c, vterm_c], axis=2), jnp.stack([kterm_b, vterm_b], axis=2)
-    )
-    back = scatter_pieces(terms, sizes)
-    owned = sum_pieces(terms[centre], back).astype(jnp.bfloat16)
-
-    activations = jnp.where(is_first, context_a, context_b)
+        is_first, jnp.stack([kterm_c, vterm_c], axis=1), jnp.stack([kterm_b, vterm_b], axis=1)
+    )
+    owned = return_terms(terms, tile_rows, tile_cols, sizes).astype(jnp.bfloat16)
+
+    activations = jnp.where(is_first, context_a, context_b).reshape(tile_rows, tile_cols, features)
     grad_q = jnp.where(is_first, gq_c, gq_b).reshape(tile_rows, tile_cols, features)
     grad_qk = jnp.stack([grad_q, owned[:, :, 0]], axis=0)
     return activations[None], grad_qk[None], owned[:, :, 1][None]

time: 195 us -> 151 us (0.77)
  starting transfers between devices: 98 us -> 42 us
  waiting for transfers between devices: 17.8 us -> 55.9 us
  local copies, waits for them, and re-layouts: 36.2 us -> 14 us
  other arithmetic: 15 us -> 12.4 us
    ppermute x34 -> x18, starting transfers between devices: 98 us -> 42 us  [shifted(): return lax.ppermute(x, AXES, pairs_from(offset, sizes, src_pipe, dst_pipe))]
    ppermute x34 -> x18, waiting for transfers between devices: 17.8 us -> 55.9 us  [shifted(): return lax.ppermute(x, AXES, pairs_from(offset, sizes, src_pipe, dst_pipe))]
    another operation x6 -> x0, local copies, waits for them, and re-layouts: 13.2 us -> none  [the longest x2 5.48 us: body(): jnp.stack([kterm_c, vterm_c], axis=2)]
    slice x15 -> x18, local copies, waits for them, and re-layouts: 12.8 us -> 2.6 us  [the longest x2 1.79 us: return_terms(): bottom = terms[b0:b1].astype(jnp.bfloat16)]
    unnamed x14 -> x27, local copies, waits for them, and re-layouts: 2.92 us -> 7.7 us
    reshape x2 -> x16, local copies, waits for them, and re-layouts: 2.74 us -> 0.69 us  [the longest x12 0.4 us: flat(): return x.reshape((-1,) + x.shape[2:])]
    another operation x2 -> x3, other arithmetic: 6.02 us -> 4.67 us
  transfers between devices with their start and end apart: 34 -> 18, of which waited for: 8 -> 11; matrix products, arithmetic and copies ran while one was open for 5% -> 5% of each run, Pallas kernels for 0% -> 0%
where the time goes in v3:
time: 151 us; the launch traced here: 150 us
  waiting for transfers between devices  55.9 us (37%)
  starting transfers between devices  42 us (28%)
  Pallas kernels  24.4 us (16%)
  local copies, waits for them, and re-layouts  14 us (9%)
  other arithmetic  12.4 us (8%)
    ppermute x18, waiting for transfers between devices, shifted(): return lax.ppermute(x, AXES, pairs_from(offset, sizes, src_pipe, dst_pipe))  55.9 us
    ppermute x18, starting transfers between devices, shifted(): return lax.ppermute(x, AXES, pairs_from(offset, sizes, src_pipe, dst_pipe))  42 us
    pallas_call x3, Pallas kernels, attention(): pl.pallas_call(functools.partial(attention_kernel, scaling, with_context,...  24.4 us
    unnamed x27, local copies, waits for them, and re-layouts  7.7 us
    another operation x2, other arithmetic  3.88 us
  transfers between devices with their start and end apart: 18, of which 11 were waited for; matrix products, arithmetic and copies ran while one was open for 5% of the time, Pallas kernels for 0%

profile of v3, /device:TPU:6, one launch (start us, length us, event | category | flops | bytes accessed | tf_op | source)
XLA Modules:
  0.0 150.0 jit_solution(12261581638869690000)
XLA Ops:
  0.6 1.2 slice_bitcast_fusion.6
  1.9 6.2 %collective-permute-start.1 = (bf16[2,8,2,1536]{3,1,0,2:T(8,128)(2,1)S(1)}, bf16[2,8,2,1536]{3,1,0,2:T(8,128)(2,1)S(1)}, u32[]{:S(2)}, u32[]{:S(2)}) collective-permute-start(bf16[2,8,2,1536]{3,1,0,2:T(8,128)(2,1)S(1)} %get-tuple-element.33), channel_id=1, source_target_pairs={{48,0},{49,1},{50,2},{51,3},{52,4},{53,5},{54,6},{55,7},{56,8},{57... | collective-permute-start | bytes 294920 | tf_op jit(solution)/shard_map/ppermute | solution.py:42
  8.2 1.9 %collective-permute-start = (bf16[2,8,2,1536]{3,1,0,2:T(8,128)(2,1)S(1)}, bf16[2,8,2,1536]{3,1,0,2:T(8,128)(2,1)S(1)}, u32[]{:S(2)}, u32[]{:S(2)}) collective-permute-start(bf16[2,8,2,1536]{3,1,0,2:T(8,128)(2,1)S(1)} %get-tuple-element.34), channel_id=1, source_target_pairs={{0,48},{1,49},{2,50},{3,51},{4,52},{5,53},{6,54},{7,55},{8,56},{9,... | collective-permute-start | bytes 294920 | tf_op jit(solution)/shard_map/ppermute | solution.py:42
  10.3 7.9 %collective-permute-done = bf16[2,8,2,1536]{3,1,0,2:T(8,128)(2,1)S(1)} collective-permute-done((bf16[2,8,2,1536]{3,1,0,2:T(8,128)(2,1)S(1)}, bf16[2,8,2,1536]{3,1,0,2:T(8,128)(2,1)S(1)}, u32[]{:S(2)}, u32[]{:S(2)}) %collective-permute-start) | collective-permute-done | bytes 98336 | tf_op jit(solution)/shard_map/ppermute | solution.py:42
  18.6 10.7 %collective-permute-start.3 = (bf16[20,2,2,1536]{3,1,0,2:T(2,128)(2,1)S(1)}, bf16[20,2,2,1536]{3,1,0,2:T(2,128)(2,1)S(1)}, u32[]{:S(2)}, u32[]{:S(2)}) collective-permute-start(bf16[20,2,2,1536]{3,1,0,2:T(2,128)(2,1)S(1)} %get-tuple-element.25), channel_id=1, source_target_pairs={{2,0},{3,1},{4,2},{5,3},{6,4},{7,5},{8,6},{9,7},{10,8},{11,9},{12,... | collective-permute-start | bytes 737288 | tf_op jit(solution)/shard_map/ppermute | solution.py:42
  29.3 6.8 %collective-permute-done.2 = bf16[20,2,2,1536]{3,1,0,2:T(2,128)(2,1)S(1)} collective-permute-done((bf16[20,2,2,1536]{3,1,0,2:T(2,128)(2,1)S(1)}, bf16[20,2,2,1536]{3,1,0,2:T(2,128)(2,1)S(1)}, u32[]{:S(2)}, u32[]{:S(2)}) %collective-permute-start.2) | collective-permute-done | bytes 245792 | tf_op jit(solution)/shard_map/ppermute | solution.py:42
  37.6 5.7 %shard_map.58 = bf16[128,1536]{1,0:T(8,128)(2,1)S(1)} custom-call(f32[1,256]{1,0:T(1,128)S(1)} %convert_element_type.117.refs_0_, bf16[128,1536]{1,0:T(8,128)(2,1)S(1)} %get-tuple-element.37.refs_1_, bf16[256,1536]{1,0:T(8,128)(2,1)S(1)} %get-tuple-element.24.refs_2_, bf16[256,1536]{1,0:T(8,128)(2,1)S(1)} %get-tuple-element.23.refs_3_), custom_call_target="tpu_custom_call" | custom-call | flops 201326592 | bytes 2360320 | tf_op jit(solution)/shard_map/pallas_call | solution.py:183
  43.3 1.3 collective-permute-start.4
  44.6 1.3 collective-permute-start.5
  45.9 1.3 collective-permute-start.6
  47.2 6.7 %collective-permute-done.5 = bf16[2,8,1536]{2,1,0:T(8,128)(2,1)S(1)} collective-permute-done((bf16[2,8,1536]{2,1,0:T(8,128)(2,1)S(1)}, bf16[2,8,1536]{2,1,0:T(8,128)(2,1)S(1)}, u32[]{:S(2)}, u32[]{:S(2)}) %collective-permute-start.5) | collective-permute-done | bytes 49184 | tf_op jit(solution)/shard_map/ppermute | solution.py:42
  54.1 1.8 %collective-permute-start.8 = (bf16[20,2,1536]{2,1,0:T(2,128)(2,1)S(1)}, bf16[20,2,1536]{2,1,0:T(2,128)(2,1)S(1)}, u32[]{:S(2)}, u32[]{:S(2)}) collective-permute-start(bf16[20,2,1536]{2,1,0:T(2,128)(2,1)S(1)} %get-tuple-element.38), channel_id=1, source_target_pairs={{2,0},{3,1},{4,2},{5,3},{6,4},{7,5},{8,6},{9,7},{10,8},{11,9},{12,... | collective-permute-start | bytes 368648 | tf_op jit(solution)/shard_map/ppermute | solution.py:42
  58.0 3.5 %collective-permute-done.7 = bf16[20,2,1536]{2,1,0:T(2,128)(2,1)S(1)} collective-permute-done((bf16[20,2,1536]{2,1,0:T(2,128)(2,1)S(1)}, bf16[20,2,1536]{2,1,0:T(2,128)(2,1)S(1)}, u32[]{:S(2)}, u32[]{:S(2)}) %collective-permute-start.7) | collective-permute-done | bytes 122912 | tf_op jit(solution)/shard_map/ppermute | solution.py:42
  63.5 1.6 %add_convert_fusion.refs_3_ = bf16[256,1536]{1,0:T(8,128)(2,1)S(1)} fusion(bf16[256,1536]{1,0:T(8,128)(2,1)} %constant_dynamic-update-slice_fusion.5, bf16[256,2,1536]{2,0,1:T(8,128)(2,1)} %copy-done.4), kind=kLoop, calls=%fused_computation.11 | loop fusion | flops 1572864 | bytes 2359296 | tf_op jit(solution)/shard_map/convert_element_type | solution.py:236
  65.1 10.8 %shard_map.59 = (bf16[128,1536]{1,0:T(8,128)(2,1)S(1)}, bf16[128,1536]{1,0:T(8,128)(2,1)S(1)}, f32[256,1536]{1,0:T(8,128)S(1)}, f32[256,1536]{1,0:T(8,128)}) custom-call(f32[1,256]{1,0:T(1,128)S(1)} %convert_element_type.117.refs_0_, bf16[128,1536]{1,0:T(8,128)(2,1)S(1)} %get-tuple-element.37.refs_1_, bf16[256,1536]{1,0:T(8,128)(2,1)S(1)} %get-tuple-element.24.refs_2_, ...), custom_call_target="tpu_custom_call" | custom-call | flops 603979776 | bytes 6292480 | tf_op jit(solution)/shard_map/pallas_call | solution.py:183
  77.1 1.5 convert.56
  81.2 3.0 %collective-permute-start.9 = (bf16[20,2,1536]{2,1,0:T(2,128)(2,1)S(1)}, bf16[20,2,1536]{2,1,0:T(2,128)(2,1)S(1)}, u32[]{:S(2)}, u32[]{:S(2)}) collective-permute-start(bf16[20,2,1536]{2,1,0:T(2,128)(2,1)S(1)} %reshape.187), channel_id=1, source_target_pairs={{2,0},{3,1},{4,2},{5,3},{6,4},{7,5},{8,6},{9,7},{10,8},{11,9},{12,... | collective-permute-start | bytes 368648 | tf_op jit(solution)/shard_map/ppermute | solution.py:42
  85.1 1.5 %collective-permute-done.9 = bf16[20,2,1536]{2,1,0:T(2,128)(2,1)S(1)} collective-permute-done((bf16[20,2,1536]{2,1,0:T(2,128)(2,1)S(1)}, bf16[20,2,1536]{2,1,0:T(2,128)(2,1)S(1)}, u32[]{:S(2)}, u32[]{:S(2)}) %collective-permute-start.9) | collective-permute-done | bytes 122912 | tf_op jit(solution)/shard_map/ppermute | solution.py:42
  86.7 1.3 collective-permute-start.13
  88.1 1.3 collective-permute-start.12
  89.5 1.4 fusion.9
  90.9 2.3 %collective-permute-start.11 = (f32[16,8,1536]{2,1,0:T(8,128)S(1)}, f32[16,8,1536]{2,1,0:T(8,128)}, u32[]{:S(2)}, u32[]{:S(2)}) collective-permute-start(f32[16,8,1536]{2,1,0:T(8,128)S(1)} %fusion.9), channel_id=1, source_target_pairs={{1,0},{3,2},{5,4},{7,6},{9,8},{11,10},{13,12},{15,14},{17,16},{19,... | collective-permute-start | bytes 2359304 | tf_op jit(solution)/shard_map/ppermute | solution.py:42
  93.4 14.4 %collective-permute-done.11 = f32[16,8,1536]{2,1,0:T(8,128)} collective-permute-done((f32[16,8,1536]{2,1,0:T(8,128)S(1)}, f32[16,8,1536]{2,1,0:T(8,128)}, u32[]{:S(2)}, u32[]{:S(2)}) %collective-permute-start.11) | collective-permute-done | bytes 786464 | tf_op jit(solution)/shard_map/ppermute | solution.py:42
  109.0 7.9 %shard_map.60 = (bf16[128,1536]{1,0:T(8,128)(2,1)S(1)}, f32[256,1536]{1,0:T(8,128)S(1)}, f32[256,1536]{1,0:T(8,128)S(1)}) custom-call(f32[1,256]{1,0:T(1,128)S(1)} %convert_element_type.117.refs_0_, bf16[128,1536]{1,0:T(8,128)(2,1)S(1)} %get-tuple-element.37.refs_1_, bf16[256,1536]{1,0:T(8,128)(2,1)S(1)} %get-tuple-element.24.refs_2_, ...), custom_call_target="tpu_custom_call" | custom-call | flops 503316480 | bytes 5899264 | tf_op jit(solution)/shard_map/pallas_call | solution.py:183
  117.0 2.4 %fusion.11 = (bf16[256,2,1536]{2,0,1:T(8,128)(2,1)S(1)}, f32[256,2,1536]{2,0,1:T(8,128)}) fusion(f32[256,1,1536]{2,0,1:T(8,128)S(1)} %bitcast.109, f32[256,1,1536]{2,0,1:T(8,128)S(1)} %bitcast.105, f32[256,1,1536]{2,0,1:T(8,128)S(1)} %bitcast.107, f32[256,1,1536]{2,0,1:T(8,128)S(1)} %bitcast.106, pred[]{:T(512)S(6)} %eq.3), kind=kLoop, calls=%fused_computation.62 | loop fusion | flops 3145728 | bytes 11010049 | tf_op jit(solution)/shard_map/convert.47
  120.8 2.2 %collective-permute-start.14 = (bf16[20,2,2,1536]{3,1,0,2:T(2,128)(2,1)S(1)}, bf16[20,2,2,1536]{3,1,0,2:T(2,128)(2,1)S(1)}, u32[]{:S(2)}, u32[]{:S(2)}) collective-permute-start(bf16[20,2,2,1536]{3,1,0,2:T(2,128)(2,1)S(1)} %reshape.195), channel_id=1, source_target_pairs={{2,0},{3,1},{4,2},{5,3},{6,4},{7,5},{8,6},{9,7},{10,8},{11,9},{12,... | collective-permute-start | bytes 737288 | tf_op jit(solution)/shard_map/ppermute | solution.py:42
  124.0 2.7 %collective-permute-done.14 = bf16[20,2,2,1536]{3,1,0,2:T(2,128)(2,1)S(1)} collective-permute-done((bf16[20,2,2,1536]{3,1,0,2:T(2,128)(2,1)S(1)}, bf16[20,2,2,1536]{3,1,0,2:T(2,128)(2,1)S(1)}, u32[]{:S(2)}, u32[]{:S(2)}) %collective-permute-start.14) | collective-permute-done | bytes 245792 | tf_op jit(solution)/shard_map/ppermute | solution.py:42
  126.8 3.0 %collective-permute-done.15 = bf16[20,2,2,1536]{3,1,0,2:T(2,128)(2,1)S(1)} collective-permute-done((bf16[20,2,2,1536]{3,1,0,2:T(2,128)(2,1)S(1)}, bf16[20,2,2,1536]{3,1,0,2:T(2,128)(2,1)S(1)}, u32[]{:S(2)}, u32[]{:S(2)}) %collective-permute-start.15) | collective-permute-done | bytes 245792 | tf_op jit(solution)/shard_map/ppermute | solution.py:42
  130.0 5.5 %collective-permute-start.17 = (bf16[24,2,1536]{2,0,1:T(8,128)(2,1)S(1)}, bf16[24,2,1536]{2,0,1:T(8,128)(2,1)S(1)}, u32[]{:S(2)}, u32[]{:S(2)}) collective-permute-start(bf16[24,2,1536]{2,0,1:T(8,128)(2,1)S(1)} %pad_maximum_fusion.5), channel_id=1, source_target_pairs={{48,0},{49,1},{50,2},{51,3},{52,4},{53,5},{54,6},{55,7},{56,8},{57... | collective-permute-start | bytes 442376 | tf_op jit(solution)/shard_map/ppermute | solution.py:42
  135.5 1.9 %collective-permute-start.16 = (bf16[24,2,1536]{2,0,1:T(8,128)(2,1)S(1)}, bf16[24,2,1536]{2,0,1:T(8,128)(2,1)S(1)}, u32[]{:S(2)}, u32[]{:S(2)}) collective-permute-start(bf16[24,2,1536]{2,0,1:T(8,128)(2,1)S(1)} %pad_maximum_fusion.4), channel_id=1, source_target_pairs={{0,48},{1,49},{2,50},{3,51},{4,52},{5,53},{6,54},{7,55},{8,56},{9,... | collective-permute-start | bytes 442376 | tf_op jit(solution)/shard_map/ppermute | solution.py:42
  138.1 8.0 %collective-permute-done.16 = bf16[24,2,1536]{2,0,1:T(8,128)(2,1)S(1)} collective-permute-done((bf16[24,2,1536]{2,0,1:T(8,128)(2,1)S(1)}, bf16[24,2,1536]{2,0,1:T(8,128)(2,1)S(1)}, u32[]{:S(2)}, u32[]{:S(2)}) %collective-permute-start.16) | collective-permute-done | bytes 147488 | tf_op jit(solution)/shard_map/ppermute | solution.py:42
  146.2 2.0 %fusion.8 = bf16[16,8,2,1536]{3,1,0,2:T(8,128)(2,1)S(1)} fusion(f32[256,2,1536]{2,0,1:T(8,128)} %get-tuple-element.18, bf16[2,2,2,1536]{3,1,0,2:T(2,128)(2,1)S(1)} %convert_element_type.133, bf16[2,2,2,1536]{3,1,0,2:T(2,128)(2,1)S(1)} %convert_element_type.132, bf16[2,8,2,1536]{3,1,0,2:T(8,128)(2,1)S(1)} %slice_bitcast_fusion.8, ...), kind=kLoop, calls=%fused_computation.10 | loop fusion | flops 6684672 | bytes 3047424 | tf_op jit(solution)/shard_map/convert_element_type | solution.py:250
  (109 shorter events, 17.7 us)
Async XLA Ops:
  0.6 1.3 copy-start.5
  1.9 8.4 %collective-permute-start.1 = (bf16[2,8,2,1536]{3,1,0,2:T(8,128)(2,1)S(1)}, bf16[2,8,2,1536]{3,1,0,2:T(8,128)(2,1)S(1)}, u32[]{:S(2)}, u32[]{:S(2)}) collective-permute-start(bf16[2,8,2,1536]{3,1,0,2:T(8,128)(2,1)S(1)} %get-tuple-element.33), channel_id=1, source_target_pairs={{48,0},{49,1},{50,2},{51,3},{52,4},{53,5},{54,6},{55,7},{56,8},{57... | collective-permute-start | bytes 294920 | tf_op jit(solution)/shard_map/ppermute | solution.py:42
  8.2 10.1 %collective-permute-start = (bf16[2,8,2,1536]{3,1,0,2:T(8,128)(2,1)S(1)}, bf16[2,8,2,1536]{3,1,0,2:T(8,128)(2,1)S(1)}, u32[]{:S(2)}, u32[]{:S(2)}) collective-permute-start(bf16[2,8,2,1536]{3,1,0,2:T(8,128)(2,1)S(1)} %get-tuple-element.34), channel_id=1, source_target_pairs={{0,48},{1,49},{2,50},{3,51},{4,52},{5,53},{6,54},{7,55},{8,56},{9,... | collective-permute-start | bytes 294920 | tf_op jit(solution)/shard_map/ppermute | solution.py:42
  18.6 17.7 %collective-permute-start.3 = (bf16[20,2,2,1536]{3,1,0,2:T(2,128)(2,1)S(1)}, bf16[20,2,2,1536]{3,1,0,2:T(2,128)(2,1)S(1)}, u32[]{:S(2)}, u32[]{:S(2)}) collective-permute-start(bf16[20,2,2,1536]{3,1,0,2:T(2,128)(2,1)S(1)} %get-tuple-element.25), channel_id=1, source_target_pairs={{2,0},{3,1},{4,2},{5,3},{6,4},{7,5},{8,6},{9,7},{10,8},{11,9},{12,... | collective-permute-start | bytes 737288 | tf_op jit(solution)/shard_map/ppermute | solution.py:42
  29.3 6.8 %collective-permute-start.2 = (bf16[20,2,2,1536]{3,1,0,2:T(2,128)(2,1)S(1)}, bf16[20,2,2,1536]{3,1,0,2:T(2,128)(2,1)S(1)}, u32[]{:S(2)}, u32[]{:S(2)}) collective-permute-start(bf16[20,2,2,1536]{3,1,0,2:T(2,128)(2,1)S(1)} %get-tuple-element.26), channel_id=1, source_target_pairs={{46,0},{47,1},{0,2},{1,3},{2,4},{3,5},{4,6},{5,7},{6,8},{7,9},{8,1... | collective-permute-start | bytes 737288 | tf_op jit(solution)/shard_map/ppermute | solution.py:42
  36.4 1.2 copy-start.4
  43.3 10.6 %collective-permute-start.4 = (bf16[16,8,1536]{2,1,0:T(8,128)(2,1)S(1)}, bf16[16,8,1536]{2,1,0:T(8,128)(2,1)S(1)}, u32[]{:S(2)}, u32[]{:S(2)}) collective-permute-start(bf16[16,8,1536]{2,1,0:T(8,128)(2,1)S(1)} %bitcast.104), channel_id=1, source_target_pairs={{0,1},{2,3},{4,5},{6,7},{8,9},{10,11},{12,13},{14,15},{16,17},{18,... | collective-permute-start | bytes 1179656 | tf_op jit(solution)/shard_map/ppermute | solution.py:42
  44.6 9.3 %collective-permute-start.5 = (bf16[2,8,1536]{2,1,0:T(8,128)(2,1)S(1)}, bf16[2,8,1536]{2,1,0:T(8,128)(2,1)S(1)}, u32[]{:S(2)}, u32[]{:S(2)}) collective-permute-start(bf16[2,8,1536]{2,1,0:T(8,128)(2,1)S(1)} %get-tuple-element.41), channel_id=1, source_target_pairs={{0,49},{2,51},{4,53},{6,55},{8,57},{10,59},{12,61},{14,63},{16,65}... | collective-permute-start | bytes 147464 | tf_op jit(solution)/shard_map/ppermute | solution.py:42
  45.9 8.0 %collective-permute-start.6 = (bf16[2,8,1536]{2,1,0:T(8,128)(2,1)S(1)}, bf16[2,8,1536]{2,1,0:T(8,128)(2,1)S(1)}, u32[]{:S(2)}, u32[]{:S(2)}) collective-permute-start(bf16[2,8,1536]{2,1,0:T(8,128)(2,1)S(1)} %get-tuple-element.40), channel_id=1, source_target_pairs={{48,1},{50,3},{52,5},{54,7},{56,9},{58,11},{60,13},{62,15},{64,17}... | collective-permute-start | bytes 147464 | tf_op jit(solution)/shard_map/ppermute | solution.py:42
  54.1 8.0 %collective-permute-start.8 = (bf16[20,2,1536]{2,1,0:T(2,128)(2,1)S(1)}, bf16[20,2,1536]{2,1,0:T(2,128)(2,1)S(1)}, u32[]{:S(2)}, u32[]{:S(2)}) collective-permute-start(bf16[20,2,1536]{2,1,0:T(2,128)(2,1)S(1)} %get-tuple-element.38), channel_id=1, source_target_pairs={{2,0},{3,1},{4,2},{5,3},{6,4},{7,5},{8,6},{9,7},{10,8},{11,9},{12,... | collective-permute-start | bytes 368648 | tf_op jit(solution)/shard_map/ppermute | solution.py:42
  55.9 5.5 %collective-permute-start.7 = (bf16[20,2,1536]{2,1,0:T(2,128)(2,1)S(1)}, bf16[20,2,1536]{2,1,0:T(2,128)(2,1)S(1)}, u32[]{:S(2)}, u32[]{:S(2)}) collective-permute-start(bf16[20,2,1536]{2,1,0:T(2,128)(2,1)S(1)} %get-tuple-element.39), channel_id=1, source_target_pairs={{46,0},{47,1},{0,2},{1,3},{2,4},{3,5},{4,6},{5,7},{6,8},{7,9},{8,1... | collective-permute-start | bytes 368648 | tf_op jit(solution)/shard_map/ppermute | solution.py:42
  61.5 3.6 %copy-start.2 = (bf16[16,8,1536]{2,1,0:T(8,128)(2,1)S(1)}, bf16[16,8,1536]{2,1,0:T(8,128)(2,1)}, u32[]{:S(2)}) copy-start(bf16[16,8,1536]{2,1,0:T(8,128)(2,1)} %param.5) | copy-start | bytes 1179652
  75.9 1.2 copy-start
  78.6 0.9 copy-start.7
  79.5 5.5 %collective-permute-start.10 = (bf16[20,2,1536]{2,1,0:T(2,128)(2,1)S(1)}, bf16[20,2,1536]{2,1,0:T(2,128)(2,1)S(1)}, u32[]{:S(2)}, u32[]{:S(2)}) collective-permute-start(bf16[20,2,1536]{2,1,0:T(2,128)(2,1)S(1)} %reshape.188), channel_id=1, source_target_pairs={{46,0},{47,1},{0,2},{1,3},{2,4},{3,5},{4,6},{5,7},{6,8},{7,9},{8,1... | collective-permute-start | bytes 368648 | tf_op jit(solution)/shard_map/ppermute | solution.py:42
  81.2 5.4 %collective-permute-start.9 = (bf16[20,2,1536]{2,1,0:T(2,128)(2,1)S(1)}, bf16[20,2,1536]{2,1,0:T(2,128)(2,1)S(1)}, u32[]{:S(2)}, u32[]{:S(2)}) collective-permute-start(bf16[20,2,1536]{2,1,0:T(2,128)(2,1)S(1)} %reshape.187), channel_id=1, source_target_pairs={{2,0},{3,1},{4,2},{5,3},{6,4},{7,5},{8,6},{9,7},{10,8},{11,9},{12,... | collective-permute-start | bytes 368648 | tf_op jit(solution)/shard_map/ppermute | solution.py:42
  86.7 6.5 %collective-permute-start.13 = (bf16[24,1536]{1,0:T(8,128)(2,1)S(1)}, bf16[24,1536]{1,0:T(8,128)(2,1)S(1)}, u32[]{:S(2)}, u32[]{:S(2)}) collective-permute-start(bf16[24,1536]{1,0:T(8,128)(2,1)S(1)} %pad_maximum_fusion.9), channel_id=1, source_target_pairs={{49,0},{51,2},{53,4},{55,6},{57,8},{59,10},{61,12},{63,14},{65,16}... | collective-permute-start | bytes 221192 | tf_op jit(solution)/shard_map/ppermute | solution.py:42
  88.1 5.2 %collective-permute-start.12 = (bf16[24,1536]{1,0:T(8,128)(2,1)S(1)}, bf16[24,1536]{1,0:T(8,128)(2,1)S(1)}, u32[]{:S(2)}, u32[]{:S(2)}) collective-permute-start(bf16[24,1536]{1,0:T(8,128)(2,1)S(1)} %pad_maximum_fusion.8), channel_id=1, source_target_pairs={{1,48},{3,50},{5,52},{7,54},{9,56},{11,58},{13,60},{15,62},{17,64}... | collective-permute-start | bytes 221192 | tf_op jit(solution)/shard_map/ppermute | solution.py:42
  90.9 16.9 %collective-permute-start.11 = (f32[16,8,1536]{2,1,0:T(8,128)S(1)}, f32[16,8,1536]{2,1,0:T(8,128)}, u32[]{:S(2)}, u32[]{:S(2)}) collective-permute-start(f32[16,8,1536]{2,1,0:T(8,128)S(1)} %fusion.9), channel_id=1, source_target_pairs={{1,0},{3,2},{5,4},{7,6},{9,8},{11,10},{13,12},{15,14},{17,16},{19,... | collective-permute-start | bytes 2359304 | tf_op jit(solution)/shard_map/ppermute | solution.py:42
  93.4 23.6 %copy-start.1 = (f32[256,1536]{1,0:T(8,128)S(1)}, f32[256,1536]{1,0:T(8,128)}, u32[]{:S(2)}) copy-start(f32[256,1536]{1,0:T(8,128)} %copy-done) | copy-start | bytes 4718596
  93.4 23.6 %copy-start.3 = (f32[256,1536]{1,0:T(8,128)S(1)}, f32[256,1536]{1,0:T(8,128)}, u32[]{:S(2)}) copy-start(f32[256,1536]{1,0:T(8,128)} %get-tuple-element.11) | copy-start | bytes 4718596
  119.4 1.2 copy-start.6
  120.8 5.9 %collective-permute-start.14 = (bf16[20,2,2,1536]{3,1,0,2:T(2,128)(2,1)S(1)}, bf16[20,2,2,1536]{3,1,0,2:T(2,128)(2,1)S(1)}, u32[]{:S(2)}, u32[]{:S(2)}) collective-permute-start(bf16[20,2,2,1536]{3,1,0,2:T(2,128)(2,1)S(1)} %reshape.195), channel_id=1, source_target_pairs={{2,0},{3,1},{4,2},{5,3},{6,4},{7,5},{8,6},{9,7},{10,8},{11,9},{12,... | collective-permute-start | bytes 737288 | tf_op jit(solution)/shard_map/ppermute | solution.py:42
  123.0 6.8 %collective-permute-start.15 = (bf16[20,2,2,1536]{3,1,0,2:T(2,128)(2,1)S(1)}, bf16[20,2,2,1536]{3,1,0,2:T(2,128)(2,1)S(1)}, u32[]{:S(2)}, u32[]{:S(2)}) collective-permute-start(bf16[20,2,2,1536]{3,1,0,2:T(2,128)(2,1)S(1)} %reshape.196), channel_id=1, source_target_pairs={{46,0},{47,1},{0,2},{1,3},{2,4},{3,5},{4,6},{5,7},{6,8},{7,9},{8,1... | collective-permute-start | bytes 737288 | tf_op jit(solution)/shard_map/ppermute | solution.py:42
  130.0 8.1 %collective-permute-start.17 = (bf16[24,2,1536]{2,0,1:T(8,128)(2,1)S(1)}, bf16[24,2,1536]{2,0,1:T(8,128)(2,1)S(1)}, u32[]{:S(2)}, u32[]{:S(2)}) collective-permute-start(bf16[24,2,1536]{2,0,1:T(8,128)(2,1)S(1)} %pad_maximum_fusion.5), channel_id=1, source_target_pairs={{48,0},{49,1},{50,2},{51,3},{52,4},{53,5},{54,6},{55,7},{56,8},{57... | collective-permute-start | bytes 442376 | tf_op jit(solution)/shard_map/ppermute | solution.py:42
  135.5 10.7 %collective-permute-start.16 = (bf16[24,2,1536]{2,0,1:T(8,128)(2,1)S(1)}, bf16[24,2,1536]{2,0,1:T(8,128)(2,1)S(1)}, u32[]{:S(2)}, u32[]{:S(2)}) collective-permute-start(bf16[24,2,1536]{2,0,1:T(8,128)(2,1)S(1)} %pad_maximum_fusion.4), channel_id=1, source_target_pairs={{0,48},{1,49},{2,50},{3,51},{4,52},{5,53},{6,54},{7,55},{8,56},{9,... | collective-permute-start | bytes 442376 | tf_op jit(solution)/shard_map/ppermute | solution.py:42

commit v4 on v3

--- a/solution.py
+++ b/solution.py
@@ -73,10 +73,11 @@
     return jnp.pad(piece.astype(jnp.float32), pad + [(0, 0)] * (piece.ndim - 2))
 
 
-def return_terms(terms, rows, cols, sizes, src_pipe=None, dst_pipe=None):
+def return_terms(terms, rows, cols, sizes, src_pipe=None, dst_pipe=None, centre=None):
     tail = terms.shape[1:]
     (c0, c1), (t0, t1), (b0, b1), (l0, l1), (r0, r1) = piece_bounds(rows, cols)
-    centre = terms[c0:c1].reshape((rows, cols) + tail)
+    if centre is None:
+        centre = terms[c0:c1].reshape((rows, cols) + tail)
     top = terms[t0:t1].astype(jnp.bfloat16)
     bottom = terms[b0:b1].astype(jnp.bfloat16)
     strip = (rows + 2 * MARGIN, MARGIN) + tail
@@ -85,10 +86,13 @@
     from_right = shifted(left, (0, 1), sizes)
     from_left = shifted(right, (0, -1), sizes)
     inner = slice(MARGIN, MARGIN + rows)
+    sides = jnp.stack([from_right[inner], from_left[inner]], axis=0)
+    if src_pipe is not None:
+        sides = shifted(sides, (0, 0), sizes, src_pipe, dst_pipe)
     partial = (
         centre
-        + place(from_right[inner], rows, cols, 0, cols - MARGIN)
-        + place(from_left[inner], rows, cols, 0, 0)
+        + place(sides[0], rows, cols, 0, cols - MARGIN)
+        + place(sides[1], rows, cols, 0, 0)
     )
     up = jnp.concatenate(
         [top, flat(from_left[:MARGIN]), flat(from_right[:MARGIN])], axis=0
@@ -96,8 +100,6 @@
     down = jnp.concatenate(
         [bottom, flat(from_left[rows + MARGIN :]), flat(from_right[rows + MARGIN :])], axis=0
     )
-    if src_pipe is not None:
-        partial = shifted(partial, (0, 0), sizes, src_pipe, dst_pipe)
     from_below = shifted(up, (1, 0), sizes, src_pipe, dst_pipe)
     from_above = shifted(down, (-1, 0), sizes, src_pipe, dst_pipe)
     band = MARGIN * cols
@@ -114,15 +116,19 @@
     return total
 
 
-def attention_kernel(scaling, with_context, with_backward, *refs):
-    mask_ref, q_ref, k_ref, u_ref = refs[:4]
-    refs = refs[4:]
-    if with_backward:
+def attention_kernel(scaling, with_context, with_backward, with_vterm, *refs):
+    mask_ref, q_ref, k_ref = refs[:3]
+    refs = refs[3:]
+    if with_context or with_backward:
+        u_ref, refs = refs[0], refs[1:]
+    if with_backward or with_vterm:
         d_ref, refs = refs[0], refs[1:]
     if with_context:
         c_ref, refs = refs[0], refs[1:]
     if with_backward:
-        gq_ref, kt_ref, vt_ref = refs
+        gq_ref, kt_ref, refs = refs[0], refs[1], refs[2:]
+    if with_backward or with_vterm:
+        (vt_ref,) = refs
     head_dim = q_ref.shape[1] // HEADS
     nt = (((1,), (1,)), ((), ()))
 
@@ -130,18 +136,18 @@
         lanes = pl.ds(pl.multiple_of(h * head_dim, head_dim), head_dim)
         qh = q_ref[:, lanes]
         kh = k_ref[:, lanes]
-        uh = u_ref[:, lanes]
         scores = lax.dot_general(qh, kh, nt, preferred_element_type=jnp.float32) * scaling
         scores = jnp.where(mask_ref[...] > 0.5, scores, NEGATIVE)
         highest = jnp.max(scores, axis=1, keepdims=True)
         weights = jnp.exp(scores - highest)
         probs = weights / jnp.sum(weights, axis=1, keepdims=True)
-        probs_low = probs.astype(jnp.bfloat16)
         if with_context:
+            uh = u_ref[:, lanes]
             c_ref[:, lanes] = jnp.dot(
-                probs_low, uh, preferred_element_type=jnp.float32
+                probs.astype(jnp.bfloat16), uh, preferred_element_type=jnp.float32
             ).astype(c_ref.dtype)
         if with_backward:
+            uh = u_ref[:, lanes]
             dh = d_ref[:, lanes]
             dprob = lax.dot_general(dh, uh, nt, preferred_element_type=jnp.float32)
             inner = jnp.sum(probs * dprob, axis=1, keepdims=True)
@@ -152,18 +158,21 @@
             kt_ref[:, lanes] = jnp.dot(
                 dscore.T.astype(jnp.bfloat16), qh, preferred_element_type=jnp.float32
             )
+        if with_backward or with_vterm:
+            dh = d_ref[:, lanes]
             vt_ref[:, lanes] = jnp.dot(
                 probs.T.astype(jnp.bfloat16), dh, preferred_element_type=jnp.float32
             )
         return carry
 
-    lax.fori_loop(0, HEADS, head, 0)
-
-
-def attention(mask, q, k, u, d=None, with_context=True, scaling=1.0):
+    lax.fori_loop(0, HEADS, head, 0, unroll=True)
+
+
+def attention(mask, q, k, u=None, d=None, with_context=True, scaling=1.0):
     tokens, features = q.shape
     keys = k.shape[0]
-    with_backward = d is not None
+    with_backward = d is not None and u is not None
+    with_vterm = d is not None and u is None
     outs = []
     if with_context:
         outs.append(jax.ShapeDtypeStruct((tokens, features), jnp.bfloat16))
@@ -171,17 +180,18 @@
         outs += [
             jax.ShapeDtypeStruct((tokens, features), jnp.bfloat16),
             jax.ShapeDtypeStruct((keys, features), jnp.float32),
-            jax.ShapeDtypeStruct((keys, features), jnp.float32),
         ]
-    args = [mask, q, k, u] + ([d] if with_backward else [])
-    matmuls = (1 if with_context else 0) + (5 if with_backward else 1)
+    if with_backward or with_vterm:
+        outs.append(jax.ShapeDtypeStruct((keys, features), jnp.float32))
+    args = [mask, q, k] + [a for a in (u, d) if a is not None]
+    matmuls = 1 + (1 if with_context else 0) + (4 if with_backward else 0) + (1 if with_vterm else 0)
     flops = 2 * tokens * keys * features * matmuls
     bytes_accessed = sum(a.size * a.dtype.itemsize for a in args) + sum(
         math.prod(o.shape) * o.dtype.itemsize for o in outs
     )
     vmem = pl.BlockSpec(memory_space=pltpu.VMEM)
     return pl.pallas_call(
-        functools.partial(attention_kernel, scaling, with_context, with_backward),
+        functools.partial(attention_kernel, scaling, with_context, with_backward, with_vterm),
         out_shape=outs,
         in_specs=[vmem] * len(args),
         out_specs=[vmem] * len(outs),
@@ -230,15 +240,25 @@
     k = kv[:, 0]
     v = kv[:, 1]
 
+    qk_other = shifted(jnp.concatenate([q, k], axis=0), (0, 0), sizes, 1, 0)
+    d_b = cotangent.reshape(token_count, features)
+
     (context_a,) = attention(mask, q, k, v, scaling=scaling)
 
     c = keys_of(gather_keys(context_a.reshape(tile_rows, tile_cols, features), sizes, 0, 1))
     u = (v.astype(jnp.float32) + c.astype(jnp.float32)).astype(jnp.bfloat16)
 
-    d_b = cotangent.reshape(token_count, features)
     context_b, gq_b, kterm_b, vterm_b = attention(mask, q, k, u, d_b, scaling=scaling)
 
-    d_c = return_terms(vterm_b, tile_rows, tile_cols, sizes, 1, 0).astype(jnp.bfloat16)
+    qk_other, vterm_b = lax.optimization_barrier((qk_other, vterm_b))
+    (vterm_other,) = attention(
+        mask, qk_other[:token_count], qk_other[token_count:], d=d_b, with_context=False,
+        scaling=scaling,
+    )
+    centre_other = vterm_other[:token_count].reshape(tile_rows, tile_cols, features)
+
+    d_c = return_terms(vterm_b, tile_rows, tile_cols, sizes, 1, 0, centre_other)
+    d_c = d_c.astype(jnp.bfloat16)
 
     gq_c, kterm_c, vterm_c = attention(
         mask, q, k, u, d_c.reshape(token_count, features), with_context=False, scaling=scaling

time: 151 us -> 155 us (1.026)
  waiting for transfers between devices: 55.9 us -> 36 us
  local copies, waits for them, and re-layouts: 14 us -> 31.9 us
  starting transfers between devices: 42 us -> 53.5 us
  Pallas kernels: 24.4 us -> 16.4 us
  other arithmetic: 12.4 us -> 14.6 us
    ppermute x18 -> x19, waiting for transfers between devices: 55.9 us -> 36 us  [shifted(): return lax.ppermute(x, AXES, pairs_from(offset, sizes, src_pipe, dst_pipe))]
    ppermute x18 -> x19, starting transfers between devices: 42 us -> 53.5 us  [shifted(): return lax.ppermute(x, AXES, pairs_from(offset, sizes, src_pipe, dst_pipe))]
    pallas_call x3 -> x4, Pallas kernels: 24.4 us -> 16.4 us  [attention(): pl.pallas_call(functools.partial(attention_kernel, scaling, with_context,...]
    convert_element_type x12 -> x13, local copies, waits for them, and re-layouts: 0.15 us -> 7.08 us  [place(): return jnp.pad(piece.astype(jnp.float32), pad + [(0, 0)] * (piece.ndim - 2))]
    reshape x12, local copies, waits for them, and re-layouts: 0.4 us -> 5.02 us  [flat(): return x.reshape((-1,) + x.shape[2:])]
    slice x5 -> x4, local copies, waits for them, and re-layouts: 0.43 us -> 4.1 us  [the longest x1 2.06 us: body(): qk_other[token_count:]]
    unnamed x27 -> x33, local copies, waits for them, and re-layouts: 7.7 us -> 4.35 us
    another operation x0 -> x2, local copies, waits for them, and re-layouts: none -> 1.93 us  [return_terms(): sides = jnp.stack([from_right[inner], from_left[inner]], axis=0)]
  transfers between devices with their start and end apart: 18 -> 19, of which waited for: 11 -> 9; matrix products, arithmetic and copies ran while one was open for 5% -> 16% of each run, Pallas kernels for 0% -> 6%
where the time goes in v4:
time: 155 us; the launch traced here: 154 us
  starting transfers between devices  53.5 us (35%)
  waiting for transfers between devices  36 us (23%)
  local copies, waits for them, and re-layouts  31.9 us (21%)
  Pallas kernels  16.4 us (11%)
  other arithmetic  14.6 us (9%)
    ppermute x19, starting transfers between devices, shifted(): return lax.ppermute(x, AXES, pairs_from(offset, sizes, src_pipe, dst_pipe))  53.5 us
    ppermute x19, waiting for transfers between devices, shifted(): return lax.ppermute(x, AXES, pairs_from(offset, sizes, src_pipe, dst_pipe))  36 us
    pallas_call x4, Pallas kernels, attention(): pl.pallas_call(functools.partial(attention_kernel, scaling, with_context,...  16.4 us
    convert_element_type x13, local copies, waits for them, and re-layouts, place(): return jnp.pad(piece.astype(jnp.float32), pad + [(0, 0)] * (piece.ndim - 2))  7.08 us
    reshape x12, local copies, waits for them, and re-layouts, flat(): return x.reshape((-1,) + x.shape[2:])  5.02 us
    unnamed x33, local copies, waits for them, and re-layouts  4.35 us
    another operation x2, other arithmetic  3.86 us
  transfers between devices with their start and end apart: 19, of which 9 were waited for; matrix products, arithmetic and copies ran while one was open for 16% of the time, Pallas kernels for 6%

profile of v4, /device:TPU:6, one launch (start us, length us, event | category | flops | bytes accessed | tf_op | source)
XLA Modules:
  0.0 153.7 jit_solution(3171383232693068020)
XLA Ops:
  1.9 6.2 %collective-permute-start.1 = (bf16[2,8,2,1536]{3,1,0,2:T(8,128)(2,1)S(1)}, bf16[2,8,2,1536]{3,1,0,2:T(8,128)(2,1)S(1)}, u32[]{:S(2)}, u32[]{:S(2)}) collective-permute-start(bf16[2,8,2,1536]{3,1,0,2:T(8,128)(2,1)S(1)} %get-tuple-element.37), channel_id=1, source_target_pairs={{48,0},{49,1},{50,2},{51,3},{52,4},{53,5},{54,6},{55,7},{56,8},{57... | collective-permute-start | bytes 294920 | tf_op jit(solution)/shard_map/ppermute | solution.py:42
  8.2 1.9 %collective-permute-start = (bf16[2,8,2,1536]{3,1,0,2:T(8,128)(2,1)S(1)}, bf16[2,8,2,1536]{3,1,0,2:T(8,128)(2,1)S(1)}, u32[]{:S(2)}, u32[]{:S(2)}) collective-permute-start(bf16[2,8,2,1536]{3,1,0,2:T(8,128)(2,1)S(1)} %get-tuple-element.38), channel_id=1, source_target_pairs={{0,48},{1,49},{2,50},{3,51},{4,52},{5,53},{6,54},{7,55},{8,56},{9,... | collective-permute-start | bytes 294920 | tf_op jit(solution)/shard_map/ppermute | solution.py:42
  10.3 7.9 %collective-permute-done = bf16[2,8,2,1536]{3,1,0,2:T(8,128)(2,1)S(1)} collective-permute-done((bf16[2,8,2,1536]{3,1,0,2:T(8,128)(2,1)S(1)}, bf16[2,8,2,1536]{3,1,0,2:T(8,128)(2,1)S(1)}, u32[]{:S(2)}, u32[]{:S(2)}) %collective-permute-start) | collective-permute-done | bytes 98336 | tf_op jit(solution)/shard_map/ppermute | solution.py:42
  18.6 10.7 %collective-permute-start.3 = (bf16[20,2,2,1536]{3,1,0,2:T(2,128)(2,1)S(1)}, bf16[20,2,2,1536]{3,1,0,2:T(2,128)(2,1)S(1)}, u32[]{:S(2)}, u32[]{:S(2)}) collective-permute-start(bf16[20,2,2,1536]{3,1,0,2:T(2,128)(2,1)S(1)} %get-tuple-element.29), channel_id=1, source_target_pairs={{2,0},{3,1},{4,2},{5,3},{6,4},{7,5},{8,6},{9,7},{10,8},{11,9},{12,... | collective-permute-start | bytes 737288 | tf_op jit(solution)/shard_map/ppermute | solution.py:42
  29.3 6.8 %collective-permute-done.2 = bf16[20,2,2,1536]{3,1,0,2:T(2,128)(2,1)S(1)} collective-permute-done((bf16[20,2,2,1536]{3,1,0,2:T(2,128)(2,1)S(1)}, bf16[20,2,2,1536]{3,1,0,2:T(2,128)(2,1)S(1)}, u32[]{:S(2)}, u32[]{:S(2)}) %collective-permute-start.2) | collective-permute-done | bytes 245792 | tf_op jit(solution)/shard_map/ppermute | solution.py:42
  37.6 1.4 shard_map.58
  44.0 5.6 %collective-permute-start.9 = (bf16[384,1536]{1,0:T(8,128)(2,1)}, bf16[384,1536]{1,0:T(8,128)(2,1)}, u32[]{:S(2)}, u32[]{:S(2)}) collective-permute-start(bf16[384,1536]{1,0:T(8,128)(2,1)} %pad_maximum_fusion), channel_id=1, source_target_pairs={{1,0},{3,2},{5,4},{7,6},{9,8},{11,10},{13,12},{15,14},{17,16},{19,... | collective-permute-start | bytes 3538952 | tf_op jit(solution)/shard_map/ppermute | solution.py:42
  50.7 2.2 %collective-permute-start.8 = (bf16[20,2,1536]{2,1,0:T(2,128)(2,1)S(1)}, bf16[20,2,1536]{2,1,0:T(2,128)(2,1)S(1)}, u32[]{:S(2)}, u32[]{:S(2)}) collective-permute-start(bf16[20,2,1536]{2,1,0:T(2,128)(2,1)S(1)} %get-tuple-element.42), channel_id=1, source_target_pairs={{2,0},{3,1},{4,2},{5,3},{6,4},{7,5},{8,6},{9,7},{10,8},{11,9},{12,... | collective-permute-start | bytes 368648 | tf_op jit(solution)/shard_map/ppermute | solution.py:42
  53.0 5.5 %collective-permute-done.7 = bf16[20,2,1536]{2,1,0:T(2,128)(2,1)S(1)} collective-permute-done((bf16[20,2,1536]{2,1,0:T(2,128)(2,1)S(1)}, bf16[20,2,1536]{2,1,0:T(2,128)(2,1)S(1)}, u32[]{:S(2)}, u32[]{:S(2)}) %collective-permute-start.7) | collective-permute-done | bytes 122912 | tf_op jit(solution)/shard_map/ppermute | solution.py:42
  58.6 1.4 add_convert_fusion.refs_3_
  60.0 7.4 %shard_map.59 = (bf16[128,1536]{1,0:T(8,128)(2,1)S(1)}, bf16[128,1536]{1,0:T(8,128)(2,1)S(1)}, f32[256,1536]{1,0:T(8,128)S(1)}, f32[256,1536]{1,0:T(8,128)}) custom-call(f32[1,256]{1,0:T(1,128)S(1)} %convert_element_type.123.refs_0_, bf16[128,1536]{1,0:T(8,128)(2,1)S(1)} %get-tuple-element.41.refs_1_, bf16[256,1536]{1,0:T(8,128)(2,1)S(1)} %get-tuple-element.28.refs_2_, ...), custom_call_target="tpu_custom_call" | custom-call | flops 603979776 | bytes 6292480 | tf_op jit(solution)/shard_map/pallas_call | solution.py:193
  68.7 1.5 convert.58
  70.9 3.5 %collective-permute-start.10 = (bf16[20,2,1536]{2,1,0:T(2,128)(2,1)}, bf16[20,2,1536]{2,1,0:T(2,128)(2,1)}, u32[]{:S(2)}, u32[]{:S(2)}) collective-permute-start(bf16[20,2,1536]{2,1,0:T(2,128)(2,1)} %reshape.191), channel_id=1, source_target_pairs={{2,0},{3,1},{4,2},{5,3},{6,4},{7,5},{8,6},{9,7},{10,8},{11,9},{12,... | collective-permute-start | bytes 368648 | tf_op jit(solution)/shard_map/ppermute | solution.py:42
  75.0 1.8 %slice.184.refs_1_ = bf16[128,1536]{1,0:T(8,128)(2,1)} slice(bf16[384,1536]{1,0:T(8,128)(2,1)} %collective-permute-done.9), slice={[0:128], [0:1536]} | slice | bytes 786432 | tf_op jit(solution)/shard_map/slice | solution.py:255
  76.8 2.1 %slice.185.refs_2_ = bf16[256,1536]{1,0:T(8,128)(2,1)} slice(bf16[384,1536]{1,0:T(8,128)(2,1)} %collective-permute-done.9), slice={[128:384], [0:1536]} | slice | bytes 1572864 | tf_op jit(solution)/shard_map/slice | solution.py:255
  82.7 1.6 %shard_map.60 = f32[256,1536]{1,0:T(8,128)S(1)} custom-call(f32[1,256]{1,0:T(1,128)S(1)} %convert_element_type.123.refs_0_, bf16[128,1536]{1,0:T(8,128)(2,1)S(1)} %copy-done.1, bf16[256,1536]{1,0:T(8,128)(2,1)S(1)} %copy-done, bf16[128,1536]{1,0:T(8,128)(2,1)S(1)} %bitcast.135), custom_call_target="tpu_custom_call" | custom-call | flops 201326592 | bytes 3146752 | tf_op jit(solution)/shard_map/pallas_call | solution.py:193
  84.3 1.3 fusion.30
  86.4 1.3 reshape.196
  87.7 1.3 fusion.29
  89.0 1.3 reshape.193
  92.5 7.7 %collective-permute-start.14 = (bf16[24,1536]{1,0:T(8,128)(2,1)S(1)}, bf16[24,1536]{1,0:T(8,128)(2,1)S(1)}, u32[]{:S(2)}, u32[]{:S(2)}) collective-permute-start(bf16[24,1536]{1,0:T(8,128)(2,1)S(1)} %pad_maximum_fusion.11), channel_id=1, source_target_pairs={{49,0},{51,2},{53,4},{55,6},{57,8},{59,10},{61,12},{63,14},{65,16}... | collective-permute-start | bytes 221192 | tf_op jit(solution)/shard_map/ppermute | solution.py:42
  105.3 2.0 %collective-permute-start.12 = (bf16[2,16,2,1536]{3,2,1,0:T(2,128)(2,1)}, bf16[2,16,2,1536]{3,2,1,0:T(2,128)(2,1)}, u32[]{:S(2)}, u32[]{:S(2)}) collective-permute-start(bf16[2,16,2,1536]{3,2,1,0:T(2,128)(2,1)} %pad_maximum_fusion.5), channel_id=1, source_target_pairs={{1,0},{3,2},{5,4},{7,6},{9,8},{11,10},{13,12},{15,14},{17,16},{19,... | collective-permute-start | bytes 589832 | tf_op jit(solution)/shard_map/ppermute | solution.py:42
  115.5 1.3 fusion.18.refs_4_
  116.8 6.0 %shard_map.61 = (bf16[128,1536]{1,0:T(8,128)(2,1)S(1)}, f32[256,1536]{1,0:T(8,128)S(1)}, f32[256,1536]{1,0:T(8,128)S(1)}) custom-call(f32[1,256]{1,0:T(1,128)S(1)} %convert_element_type.123.refs_0_, bf16[128,1536]{1,0:T(8,128)(2,1)S(1)} %get-tuple-element.41.refs_1_, bf16[256,1536]{1,0:T(8,128)(2,1)S(1)} %get-tuple-element.28.refs_2_, ...), custom_call_target="tpu_custom_call" | custom-call | flops 503316480 | bytes 5899264 | tf_op jit(solution)/shard_map/pallas_call | solution.py:193
  122.9 2.4 %fusion.19 = (bf16[256,2,1536]{2,0,1:T(8,128)(2,1)S(1)}, f32[256,2,1536]{2,0,1:T(8,128)}) fusion(f32[256,1,1536]{2,0,1:T(8,128)S(1)} %bitcast.136, f32[256,1,1536]{2,0,1:T(8,128)S(1)} %bitcast.131, f32[256,1,1536]{2,0,1:T(8,128)S(1)} %bitcast.133, f32[256,1,1536]{2,0,1:T(8,128)S(1)} %bitcast.132, pred[]{:T(512)S(6)} %eq.3), kind=kLoop, calls=%fused_computation.75 | loop fusion | flops 3145728 | bytes 11010049 | tf_op jit(solution)/shard_map/convert.49
  126.2 2.7 %collective-permute-start.15 = (bf16[20,2,2,1536]{3,1,0,2:T(2,128)(2,1)}, bf16[20,2,2,1536]{3,1,0,2:T(2,128)(2,1)S(1)}, u32[]{:S(2)}, u32[]{:S(2)}) collective-permute-start(bf16[20,2,2,1536]{3,1,0,2:T(2,128)(2,1)} %reshape.199), channel_id=1, source_target_pairs={{2,0},{3,1},{4,2},{5,3},{6,4},{7,5},{8,6},{9,7},{10,8},{11,9},{12,... | collective-permute-start | bytes 737288 | tf_op jit(solution)/shard_map/ppermute | solution.py:42
  128.9 4.0 %collective-permute-done.15 = bf16[20,2,2,1536]{3,1,0,2:T(2,128)(2,1)S(1)} collective-permute-done((bf16[20,2,2,1536]{3,1,0,2:T(2,128)(2,1)}, bf16[20,2,2,1536]{3,1,0,2:T(2,128)(2,1)S(1)}, u32[]{:S(2)}, u32[]{:S(2)}) %collective-permute-start.15) | collective-permute-done | bytes 245792 | tf_op jit(solution)/shard_map/ppermute | solution.py:42
  133.0 2.7 %collective-permute-done.16 = bf16[20,2,2,1536]{3,1,0,2:T(2,128)(2,1)S(1)} collective-permute-done((bf16[20,2,2,1536]{3,1,0,2:T(2,128)(2,1)S(1)}, bf16[20,2,2,1536]{3,1,0,2:T(2,128)(2,1)S(1)}, u32[]{:S(2)}, u32[]{:S(2)}) %collective-permute-start.16) | collective-permute-done | bytes 245792 | tf_op jit(solution)/shard_map/ppermute | solution.py:42
  135.8 3.4 %collective-permute-start.18 = (bf16[24,2,1536]{2,0,1:T(8,128)(2,1)S(1)}, bf16[24,2,1536]{2,0,1:T(8,128)(2,1)S(1)}, u32[]{:S(2)}, u32[]{:S(2)}) collective-permute-start(bf16[24,2,1536]{2,0,1:T(8,128)(2,1)S(1)} %pad_maximum_fusion.7), channel_id=1, source_target_pairs={{48,0},{49,1},{50,2},{51,3},{52,4},{53,5},{54,6},{55,7},{56,8},{57... | collective-permute-start | bytes 442376 | tf_op jit(solution)/shard_map/ppermute | solution.py:42
  139.2 2.5 %collective-permute-start.17 = (bf16[24,2,1536]{2,0,1:T(8,128)(2,1)S(1)}, bf16[24,2,1536]{2,0,1:T(8,128)(2,1)S(1)}, u32[]{:S(2)}, u32[]{:S(2)}) collective-permute-start(bf16[24,2,1536]{2,0,1:T(8,128)(2,1)S(1)} %pad_maximum_fusion.6), channel_id=1, source_target_pairs={{0,48},{1,49},{2,50},{3,51},{4,52},{5,53},{6,54},{7,55},{8,56},{9,... | collective-permute-start | bytes 442376 | tf_op jit(solution)/shard_map/ppermute | solution.py:42
  142.9 7.0 %collective-permute-done.17 = bf16[24,2,1536]{2,0,1:T(8,128)(2,1)S(1)} collective-permute-done((bf16[24,2,1536]{2,0,1:T(8,128)(2,1)S(1)}, bf16[24,2,1536]{2,0,1:T(8,128)(2,1)S(1)}, u32[]{:S(2)}, u32[]{:S(2)}) %collective-permute-start.17) | collective-permute-done | bytes 147488 | tf_op jit(solution)/shard_map/ppermute | solution.py:42
  150.0 2.0 %fusion.8 = bf16[16,8,2,1536]{3,1,0,2:T(8,128)(2,1)S(1)} fusion(f32[256,2,1536]{2,0,1:T(8,128)} %get-tuple-element.22, bf16[2,2,2,1536]{3,1,0,2:T(2,128)(2,1)S(1)} %convert_element_type.141, bf16[2,2,2,1536]{3,1,0,2:T(2,128)(2,1)S(1)} %convert_element_type.140, bf16[2,8,2,1536]{3,1,0,2:T(8,128)(2,1)S(1)} %slice_bitcast_fusion.9, ...), kind=kLoop, calls=%fused_computation.10 | loop fusion | flops 6684672 | bytes 3047424 | tf_op jit(solution)/shard_map/convert_element_type | solution.py:270
  (122 shorter events, 36.2 us)
Async XLA Ops:
  0.6 1.3 copy-start.10
  1.9 8.4 %collective-permute-start.1 = (bf16[2,8,2,1536]{3,1,0,2:T(8,128)(2,1)S(1)}, bf16[2,8,2,1536]{3,1,0,2:T(8,128)(2,1)S(1)}, u32[]{:S(2)}, u32[]{:S(2)}) collective-permute-start(bf16[2,8,2,1536]{3,1,0,2:T(8,128)(2,1)S(1)} %get-tuple-element.37), channel_id=1, source_target_pairs={{48,0},{49,1},{50,2},{51,3},{52,4},{53,5},{54,6},{55,7},{56,8},{57... | collective-permute-start | bytes 294920 | tf_op jit(solution)/shard_map/ppermute | solution.py:42
  8.2 10.1 %collective-permute-start = (bf16[2,8,2,1536]{3,1,0,2:T(8,128)(2,1)S(1)}, bf16[2,8,2,1536]{3,1,0,2:T(8,128)(2,1)S(1)}, u32[]{:S(2)}, u32[]{:S(2)}) collective-permute-start(bf16[2,8,2,1536]{3,1,0,2:T(8,128)(2,1)S(1)} %get-tuple-element.38), channel_id=1, source_target_pairs={{0,48},{1,49},{2,50},{3,51},{4,52},{5,53},{6,54},{7,55},{8,56},{9,... | collective-permute-start | bytes 294920 | tf_op jit(solution)/shard_map/ppermute | solution.py:42
  18.6 17.7 %collective-permute-start.3 = (bf16[20,2,2,1536]{3,1,0,2:T(2,128)(2,1)S(1)}, bf16[20,2,2,1536]{3,1,0,2:T(2,128)(2,1)S(1)}, u32[]{:S(2)}, u32[]{:S(2)}) collective-permute-start(bf16[20,2,2,1536]{3,1,0,2:T(2,128)(2,1)S(1)} %get-tuple-element.29), channel_id=1, source_target_pairs={{2,0},{3,1},{4,2},{5,3},{6,4},{7,5},{8,6},{9,7},{10,8},{11,9},{12,... | collective-permute-start | bytes 737288 | tf_op jit(solution)/shard_map/ppermute | solution.py:42
  29.3 6.8 %collective-permute-start.2 = (bf16[20,2,2,1536]{3,1,0,2:T(2,128)(2,1)S(1)}, bf16[20,2,2,1536]{3,1,0,2:T(2,128)(2,1)S(1)}, u32[]{:S(2)}, u32[]{:S(2)}) collective-permute-start(bf16[20,2,2,1536]{3,1,0,2:T(2,128)(2,1)S(1)} %get-tuple-element.30), channel_id=1, source_target_pairs={{46,0},{47,1},{0,2},{1,3},{2,4},{3,5},{4,6},{5,7},{6,8},{7,9},{8,1... | collective-permute-start | bytes 737288 | tf_op jit(solution)/shard_map/ppermute | solution.py:42
  36.4 1.2 copy-start.8
  39.0 10.6 %collective-permute-start.5 = (bf16[2,8,1536]{2,1,0:T(8,128)(2,1)S(1)}, bf16[2,8,1536]{2,1,0:T(8,128)(2,1)S(1)}, u32[]{:S(2)}, u32[]{:S(2)}) collective-permute-start(bf16[2,8,1536]{2,1,0:T(8,128)(2,1)S(1)} %get-tuple-element.45), channel_id=1, source_target_pairs={{0,49},{2,51},{4,53},{6,55},{8,57},{10,59},{12,61},{14,63},{16,65}... | collective-permute-start | bytes 147464 | tf_op jit(solution)/shard_map/ppermute | solution.py:42
  40.3 10.2 %collective-permute-start.4 = (bf16[16,8,1536]{2,1,0:T(8,128)(2,1)S(1)}, bf16[16,8,1536]{2,1,0:T(8,128)(2,1)S(1)}, u32[]{:S(2)}, u32[]{:S(2)}) collective-permute-start(bf16[16,8,1536]{2,1,0:T(8,128)(2,1)S(1)} %bitcast.130), channel_id=1, source_target_pairs={{0,1},{2,3},{4,5},{6,7},{8,9},{10,11},{12,13},{14,15},{16,17},{18,... | collective-permute-start | bytes 1179656 | tf_op jit(solution)/shard_map/ppermute | solution.py:42
  42.7 7.8 %collective-permute-start.6 = (bf16[2,8,1536]{2,1,0:T(8,128)(2,1)S(1)}, bf16[2,8,1536]{2,1,0:T(8,128)(2,1)S(1)}, u32[]{:S(2)}, u32[]{:S(2)}) collective-permute-start(bf16[2,8,1536]{2,1,0:T(8,128)(2,1)S(1)} %get-tuple-element.44), channel_id=1, source_target_pairs={{48,1},{50,3},{52,5},{54,7},{56,9},{58,11},{60,13},{62,15},{64,17}... | collective-permute-start | bytes 147464 | tf_op jit(solution)/shard_map/ppermute | solution.py:42
  44.0 24.7 %collective-permute-start.9 = (bf16[384,1536]{1,0:T(8,128)(2,1)}, bf16[384,1536]{1,0:T(8,128)(2,1)}, u32[]{:S(2)}, u32[]{:S(2)}) collective-permute-start(bf16[384,1536]{1,0:T(8,128)(2,1)} %pad_maximum_fusion), channel_id=1, source_target_pairs={{1,0},{3,2},{5,4},{7,6},{9,8},{11,10},{13,12},{15,14},{17,16},{19,... | collective-permute-start | bytes 3538952 | tf_op jit(solution)/shard_map/ppermute | solution.py:42
  50.7 7.8 %collective-permute-start.8 = (bf16[20,2,1536]{2,1,0:T(2,128)(2,1)S(1)}, bf16[20,2,1536]{2,1,0:T(2,128)(2,1)S(1)}, u32[]{:S(2)}, u32[]{:S(2)}) collective-permute-start(bf16[20,2,1536]{2,1,0:T(2,128)(2,1)S(1)} %get-tuple-element.42), channel_id=1, source_target_pairs={{2,0},{3,1},{4,2},{5,3},{6,4},{7,5},{8,6},{9,7},{10,8},{11,9},{12,... | collective-permute-start | bytes 368648 | tf_op jit(solution)/shard_map/ppermute | solution.py:42
  52.9 5.5 %collective-permute-start.7 = (bf16[20,2,1536]{2,1,0:T(2,128)(2,1)S(1)}, bf16[20,2,1536]{2,1,0:T(2,128)(2,1)S(1)}, u32[]{:S(2)}, u32[]{:S(2)}) collective-permute-start(bf16[20,2,1536]{2,1,0:T(2,128)(2,1)S(1)} %get-tuple-element.43), channel_id=1, source_target_pairs={{46,0},{47,1},{0,2},{1,3},{2,4},{3,5},{4,6},{5,7},{6,8},{7,9},{8,1... | collective-permute-start | bytes 368648 | tf_op jit(solution)/shard_map/ppermute | solution.py:42
  58.5 1.5 copy-start.4
  67.4 2.8 %copy-start.2 = (f32[256,1536]{1,0:T(8,128)}, f32[256,1536]{1,0:T(8,128)S(1)}, u32[]{:S(2)}) copy-start(f32[256,1536]{1,0:T(8,128)S(1)} %get-tuple-element.20) | copy-start | bytes 4718596
  67.4 2.8 %copy-start.6 = (bf16[128,1536]{1,0:T(8,128)(2,1)}, bf16[128,1536]{1,0:T(8,128)(2,1)S(1)}, u32[]{:S(2)}) copy-start(bf16[128,1536]{1,0:T(8,128)(2,1)S(1)} %get-tuple-element.17) | copy-start | bytes 1179652
  70.9 13.4 %collective-permute-start.10 = (bf16[20,2,1536]{2,1,0:T(2,128)(2,1)}, bf16[20,2,1536]{2,1,0:T(2,128)(2,1)}, u32[]{:S(2)}, u32[]{:S(2)}) collective-permute-start(bf16[20,2,1536]{2,1,0:T(2,128)(2,1)} %reshape.191), channel_id=1, source_target_pairs={{2,0},{3,1},{4,2},{5,3},{6,4},{7,5},{8,6},{9,7},{10,8},{11,9},{12,... | collective-permute-start | bytes 368648 | tf_op jit(solution)/shard_map/ppermute | solution.py:42
  79.5 8.2 %collective-permute-start.11 = (bf16[20,2,1536]{2,1,0:T(2,128)(2,1)}, bf16[20,2,1536]{2,1,0:T(2,128)(2,1)}, u32[]{:S(2)}, u32[]{:S(2)}) collective-permute-start(bf16[20,2,1536]{2,1,0:T(2,128)(2,1)} %reshape.192), channel_id=1, source_target_pairs={{46,0},{47,1},{0,2},{1,3},{2,4},{3,5},{4,6},{5,7},{6,8},{7,9},{8,1... | collective-permute-start | bytes 368648 | tf_op jit(solution)/shard_map/ppermute | solution.py:42
  79.6 1.1 copy-start
  80.7 1.0 copy-start.1
  81.7 1.0 copy-start.5
  92.5 14.7 %collective-permute-start.14 = (bf16[24,1536]{1,0:T(8,128)(2,1)S(1)}, bf16[24,1536]{1,0:T(8,128)(2,1)S(1)}, u32[]{:S(2)}, u32[]{:S(2)}) collective-permute-start(bf16[24,1536]{1,0:T(8,128)(2,1)S(1)} %pad_maximum_fusion.11), channel_id=1, source_target_pairs={{49,0},{51,2},{53,4},{55,6},{57,8},{59,10},{61,12},{63,14},{65,16}... | collective-permute-start | bytes 221192 | tf_op jit(solution)/shard_map/ppermute | solution.py:42
  101.1 7.4 %collective-permute-start.13 = (bf16[24,1536]{1,0:T(8,128)(2,1)S(1)}, bf16[24,1536]{1,0:T(8,128)(2,1)S(1)}, u32[]{:S(2)}, u32[]{:S(2)}) collective-permute-start(bf16[24,1536]{1,0:T(8,128)(2,1)S(1)} %pad_maximum_fusion.10), channel_id=1, source_target_pairs={{1,48},{3,50},{5,52},{7,54},{9,56},{11,58},{13,60},{15,62},{17,64}... | collective-permute-start | bytes 221192 | tf_op jit(solution)/shard_map/ppermute | solution.py:42
  105.3 9.1 %collective-permute-start.12 = (bf16[2,16,2,1536]{3,2,1,0:T(2,128)(2,1)}, bf16[2,16,2,1536]{3,2,1,0:T(2,128)(2,1)}, u32[]{:S(2)}, u32[]{:S(2)}) collective-permute-start(bf16[2,16,2,1536]{3,2,1,0:T(2,128)(2,1)} %pad_maximum_fusion.5), channel_id=1, source_target_pairs={{1,0},{3,2},{5,4},{7,6},{9,8},{11,10},{13,12},{15,14},{17,16},{19,... | collective-permute-start | bytes 589832 | tf_op jit(solution)/shard_map/ppermute | solution.py:42
  115.5 7.4 %copy-start.3 = (f32[256,1536]{1,0:T(8,128)S(1)}, f32[256,1536]{1,0:T(8,128)}, u32[]{:S(2)}) copy-start(f32[256,1536]{1,0:T(8,128)} %copy-done.2) | copy-start | bytes 4718596
  115.5 7.4 %copy-start.9 = (f32[256,1536]{1,0:T(8,128)S(1)}, f32[256,1536]{1,0:T(8,128)}, u32[]{:S(2)}) copy-start(f32[256,1536]{1,0:T(8,128)} %get-tuple-element.15) | copy-start | bytes 4718596
  125.3 3.6 %copy-start.7 = (bf16[128,1536]{1,0:T(8,128)(2,1)S(1)}, bf16[128,1536]{1,0:T(8,128)(2,1)}, u32[]{:S(2)}) copy-start(bf16[128,1536]{1,0:T(8,128)(2,1)} %copy-done.6) | copy-start | bytes 1179652
  126.2 6.7 %collective-permute-start.15 = (bf16[20,2,2,1536]{3,1,0,2:T(2,128)(2,1)}, bf16[20,2,2,1536]{3,1,0,2:T(2,128)(2,1)S(1)}, u32[]{:S(2)}, u32[]{:S(2)}) collective-permute-start(bf16[20,2,2,1536]{3,1,0,2:T(2,128)(2,1)} %reshape.199), channel_id=1, source_target_pairs={{2,0},{3,1},{4,2},{5,3},{6,4},{7,5},{8,6},{9,7},{10,8},{11,9},{12,... | collective-permute-start | bytes 737288 | tf_op jit(solution)/shard_map/ppermute | solution.py:42
  128.9 6.8 %collective-permute-start.16 = (bf16[20,2,2,1536]{3,1,0,2:T(2,128)(2,1)S(1)}, bf16[20,2,2,1536]{3,1,0,2:T(2,128)(2,1)S(1)}, u32[]{:S(2)}, u32[]{:S(2)}) collective-permute-start(bf16[20,2,2,1536]{3,1,0,2:T(2,128)(2,1)S(1)} %reshape.200), channel_id=1, source_target_pairs={{46,0},{47,1},{0,2},{1,3},{2,4},{3,5},{4,6},{5,7},{6,8},{7,9},{8,1... | collective-permute-start | bytes 737288 | tf_op jit(solution)/shard_map/ppermute | solution.py:42
  135.8 7.0 %collective-permute-start.18 = (bf16[24,2,1536]{2,0,1:T(8,128)(2,1)S(1)}, bf16[24,2,1536]{2,0,1:T(8,128)(2,1)S(1)}, u32[]{:S(2)}, u32[]{:S(2)}) collective-permute-start(bf16[24,2,1536]{2,0,1:T(8,128)(2,1)S(1)} %pad_maximum_fusion.7), channel_id=1, source_target_pairs={{48,0},{49,1},{50,2},{51,3},{52,4},{53,5},{54,6},{55,7},{56,8},{57... | collective-permute-start | bytes 442376 | tf_op jit(solution)/shard_map/ppermute | solution.py:42
  139.2 10.7 %collective-permute-start.17 = (bf16[24,2,1536]{2,0,1:T(8,128)(2,1)S(1)}, bf16[24,2,1536]{2,0,1:T(8,128)(2,1)S(1)}, u32[]{:S(2)}, u32[]{:S(2)}) collective-permute-start(bf16[24,2,1536]{2,0,1:T(8,128)(2,1)S(1)} %pad_maximum_fusion.6), channel_id=1, source_target_pairs={{0,48},{1,49},{2,50},{3,51},{4,52},{5,53},{6,54},{7,55},{8,56},{9,... | collective-permute-start | bytes 442376 | tf_op jit(solution)/shard_map/ppermute | solution.py:42

commit v5 on v4

--- a/solution.py
+++ b/solution.py
@@ -94,25 +94,21 @@
         + place(sides[0], rows, cols, 0, cols - MARGIN)
         + place(sides[1], rows, cols, 0, 0)
     )
+    band_shape = (MARGIN, cols) + tail
     up = jnp.concatenate(
-        [top, flat(from_left[:MARGIN]), flat(from_right[:MARGIN])], axis=0
+        [top.reshape(band_shape), from_left[:MARGIN], from_right[:MARGIN]], axis=1
     )
     down = jnp.concatenate(
-        [bottom, flat(from_left[rows + MARGIN :]), flat(from_right[rows + MARGIN :])], axis=0
+        [bottom.reshape(band_shape), from_left[rows + MARGIN :], from_right[rows + MARGIN :]],
+        axis=1,
     )
     from_below = shifted(up, (1, 0), sizes, src_pipe, dst_pipe)
     from_above = shifted(down, (-1, 0), sizes, src_pipe, dst_pipe)
-    band = MARGIN * cols
-    corner = MARGIN * MARGIN
     total = partial
     for got, r in ((from_above, 0), (from_below, rows - MARGIN)):
-        total = total + place(got[:band].reshape((MARGIN, cols) + tail), rows, cols, r, 0)
-        total = total + place(
-            got[band : band + corner].reshape((MARGIN, MARGIN) + tail), rows, cols, r, 0
-        )
-        total = total + place(
-            got[band + corner :].reshape((MARGIN, MARGIN) + tail), rows, cols, r, cols - MARGIN
-        )
+        total = total + place(got[:, :cols], rows, cols, r, 0)
+        total = total + place(got[:, cols : cols + MARGIN], rows, cols, r, 0)
+        total = total + place(got[:, cols + MARGIN :], rows, cols, r, cols - MARGIN)
     return total
 
 

time: 155 us -> 136 us (0.88)
  local copies, waits for them, and re-layouts: 31.9 us -> 13.3 us
  waiting for transfers between devices: 36 us -> 42.2 us
  other arithmetic: 14.6 us -> 9.87 us
  starting transfers between devices: 53.5 us -> 51.3 us
    convert_element_type x13 -> x1, local copies, waits for them, and re-layouts: 7.08 us -> 0.14 us  [place(): return jnp.pad(piece.astype(jnp.float32), pad + [(0, 0)] * (piece.ndim - 2))]
    ppermute x19, waiting for transfers between devices: 36 us -> 42.2 us  [shifted(): return lax.ppermute(x, AXES, pairs_from(offset, sizes, src_pipe, dst_pipe))]
    reshape x12 -> x4, local copies, waits for them, and re-layouts: 5.02 us -> 0.29 us  [flat(): return x.reshape((-1,) + x.shape[2:])]
    unnamed x33, local copies, waits for them, and re-layouts: 4.35 us -> 1.46 us
    ppermute x19, starting transfers between devices: 53.5 us -> 51.3 us  [shifted(): return lax.ppermute(x, AXES, pairs_from(offset, sizes, src_pipe, dst_pipe))]
    slice x6 -> x8, local copies, waits for them, and re-layouts: 1.92 us -> 0.14 us  [the longest x4 0.11 us: return_terms(): total = total + place(got[:, cols:cols + MARGIN], rows, cols, r, 0)]
    concatenate x4, other arithmetic: 1.75 us -> 0.18 us  [the longest x2 0.09 us: return_terms(): jnp.concatenate([bottom.reshape(band_shape), from_left[rows + MARGIN:], f...]
  transfers between devices with their start and end apart: 19 -> 19, of which waited for: 9 -> 10; matrix products, arithmetic and copies ran while one was open for 16% -> 9% of each run, Pallas kernels for 6% -> 7%
where the time goes in v5:
time: 136 us; the launch traced here: 134 us
  starting transfers between devices  51.3 us (38%)
  waiting for transfers between devices  42.2 us (31%)
  Pallas kernels  16.4 us (12%)
  local copies, waits for them, and re-layouts  13.3 us (10%)
  other arithmetic  9.87 us (7%)
    ppermute x19, starting transfers between devices, shifted(): return lax.ppermute(x, AXES, pairs_from(offset, sizes, src_pipe, dst_pipe))  51.3 us
    ppermute x19, waiting for transfers between devices, shifted(): return lax.ppermute(x, AXES, pairs_from(offset, sizes, src_pipe, dst_pipe))  42.2 us
    pallas_call x4, Pallas kernels, attention(): pl.pallas_call(functools.partial(attention_kernel, scaling, with_context,...  16.4 us
    another operation x2, other arithmetic  3.85 us
  transfers between devices with their start and end apart: 19, of which 10 were waited for; matrix products, arithmetic and copies ran while one was open for 9% of the time, Pallas kernels for 7%

profile of v5, /device:TPU:6, one launch (start us, length us, event | category | flops | bytes accessed | tf_op | source)
XLA Modules:
  0.0 134.4 jit_solution(12024799075199043926)
XLA Ops:
  0.6 1.2 slice_bitcast_fusion.7
  1.9 6.2 %collective-permute-start.1 = (bf16[2,8,2,1536]{3,1,0,2:T(8,128)(2,1)S(1)}, bf16[2,8,2,1536]{3,1,0,2:T(8,128)(2,1)S(1)}, u32[]{:S(2)}, u32[]{:S(2)}) collective-permute-start(bf16[2,8,2,1536]{3,1,0,2:T(8,128)(2,1)S(1)} %get-tuple-element.37), channel_id=1, source_target_pairs={{48,0},{49,1},{50,2},{51,3},{52,4},{53,5},{54,6},{55,7},{56,8},{57... | collective-permute-start | bytes 294920 | tf_op jit(solution)/shard_map/ppermute | solution.py:42
  8.2 1.9 %collective-permute-start = (bf16[2,8,2,1536]{3,1,0,2:T(8,128)(2,1)S(1)}, bf16[2,8,2,1536]{3,1,0,2:T(8,128)(2,1)S(1)}, u32[]{:S(2)}, u32[]{:S(2)}) collective-permute-start(bf16[2,8,2,1536]{3,1,0,2:T(8,128)(2,1)S(1)} %get-tuple-element.38), channel_id=1, source_target_pairs={{0,48},{1,49},{2,50},{3,51},{4,52},{5,53},{6,54},{7,55},{8,56},{9,... | collective-permute-start | bytes 294920 | tf_op jit(solution)/shard_map/ppermute | solution.py:42
  10.3 7.9 %collective-permute-done = bf16[2,8,2,1536]{3,1,0,2:T(8,128)(2,1)S(1)} collective-permute-done((bf16[2,8,2,1536]{3,1,0,2:T(8,128)(2,1)S(1)}, bf16[2,8,2,1536]{3,1,0,2:T(8,128)(2,1)S(1)}, u32[]{:S(2)}, u32[]{:S(2)}) %collective-permute-start) | collective-permute-done | bytes 98336 | tf_op jit(solution)/shard_map/ppermute | solution.py:42
  18.6 10.7 %collective-permute-start.3 = (bf16[20,2,2,1536]{3,1,0,2:T(2,128)(2,1)S(1)}, bf16[20,2,2,1536]{3,1,0,2:T(2,128)(2,1)S(1)}, u32[]{:S(2)}, u32[]{:S(2)}) collective-permute-start(bf16[20,2,2,1536]{3,1,0,2:T(2,128)(2,1)S(1)} %get-tuple-element.29), channel_id=1, source_target_pairs={{2,0},{3,1},{4,2},{5,3},{6,4},{7,5},{8,6},{9,7},{10,8},{11,9},{12,... | collective-permute-start | bytes 737288 | tf_op jit(solution)/shard_map/ppermute | solution.py:42
  29.3 6.8 %collective-permute-done.2 = bf16[20,2,2,1536]{3,1,0,2:T(2,128)(2,1)S(1)} collective-permute-done((bf16[20,2,2,1536]{3,1,0,2:T(2,128)(2,1)S(1)}, bf16[20,2,2,1536]{3,1,0,2:T(2,128)(2,1)S(1)}, u32[]{:S(2)}, u32[]{:S(2)}) %collective-permute-start.2) | collective-permute-done | bytes 245792 | tf_op jit(solution)/shard_map/ppermute | solution.py:42
  37.6 1.3 shard_map.58
  38.9 1.3 collective-permute-start.5
  40.2 1.3 collective-permute-start.4
  42.7 1.3 collective-permute-start.6
  44.0 5.6 %collective-permute-start.9 = (bf16[384,1536]{1,0:T(8,128)(2,1)}, bf16[384,1536]{1,0:T(8,128)(2,1)}, u32[]{:S(2)}, u32[]{:S(2)}) collective-permute-start(bf16[384,1536]{1,0:T(8,128)(2,1)} %pad_maximum_fusion), channel_id=1, source_target_pairs={{1,0},{3,2},{5,4},{7,6},{9,8},{11,10},{13,12},{15,14},{17,16},{19,... | collective-permute-start | bytes 3538952 | tf_op jit(solution)/shard_map/ppermute | solution.py:42
  51.3 2.2 %collective-permute-start.8 = (bf16[20,2,1536]{2,1,0:T(2,128)(2,1)}, bf16[20,2,1536]{2,1,0:T(2,128)(2,1)S(1)}, u32[]{:S(2)}, u32[]{:S(2)}) collective-permute-start(bf16[20,2,1536]{2,1,0:T(2,128)(2,1)} %get-tuple-element.42), channel_id=1, source_target_pairs={{2,0},{3,1},{4,2},{5,3},{6,4},{7,5},{8,6},{9,7},{10,8},{11,9},{12,... | collective-permute-start | bytes 368648 | tf_op jit(solution)/shard_map/ppermute | solution.py:42
  53.6 5.5 %collective-permute-done.7 = bf16[20,2,1536]{2,1,0:T(2,128)(2,1)S(1)} collective-permute-done((bf16[20,2,1536]{2,1,0:T(2,128)(2,1)S(1)}, bf16[20,2,1536]{2,1,0:T(2,128)(2,1)S(1)}, u32[]{:S(2)}, u32[]{:S(2)}) %collective-permute-start.7) | collective-permute-done | bytes 122912 | tf_op jit(solution)/shard_map/ppermute | solution.py:42
  59.2 1.3 add_convert_fusion.refs_3_
  60.6 7.4 %shard_map.59 = (bf16[128,1536]{1,0:T(8,128)(2,1)S(1)}, bf16[128,1536]{1,0:T(8,128)(2,1)S(1)}, f32[256,1536]{1,0:T(8,128)S(1)}, f32[256,1536]{1,0:T(8,128)}) custom-call(f32[1,256]{1,0:T(1,128)S(1)} %convert_element_type.55.refs_0_, bf16[128,1536]{1,0:T(8,128)(2,1)S(1)} %get-tuple-element.41.refs_1_, bf16[256,1536]{1,0:T(8,128)(2,1)S(1)} %get-tuple-element.28.refs_2_, ...), custom_call_target="tpu_custom_call" | custom-call | flops 603979776 | bytes 6292480 | tf_op jit(solution)/shard_map/pallas_call | solution.py:189
  68.8 1.5 %convert.46 = bf16[256,1536]{1,0:T(8,128)(2,1)S(1)} convert(f32[256,1536]{1,0:T(8,128)} %get-tuple-element.15) | non-fusion elementwise | flops 393216 | bytes 2359296 | tf_op jit(solution)/shard_map/convert.41
  71.7 3.3 %collective-permute-start.10 = (bf16[20,2,1536]{2,1,0:T(2,128)(2,1)}, bf16[20,2,1536]{2,1,0:T(2,128)(2,1)}, u32[]{:S(2)}, u32[]{:S(2)}) collective-permute-start(bf16[20,2,1536]{2,1,0:T(2,128)(2,1)} %reshape.143), channel_id=1, source_target_pairs={{2,0},{3,1},{4,2},{5,3},{6,4},{7,5},{8,6},{9,7},{10,8},{11,9},{12,... | collective-permute-start | bytes 368648 | tf_op jit(solution)/shard_map/ppermute | solution.py:42
  76.6 1.2 slice.185.refs_2_
  77.8 1.6 %reshape.144 = bf16[20,2,1536]{2,1,0:T(2,128)(2,1)} reshape(bf16[40,1536]{1,0:T(8,128)(2,1)} %get-tuple-element.35) | data formatting | bytes 245760 | tf_op jit(solution)/shard_map/reshape | solution.py:85
  79.5 1.6 %shard_map.60 = f32[256,1536]{1,0:T(8,128)S(1)} custom-call(f32[1,256]{1,0:T(1,128)S(1)} %convert_element_type.55.refs_0_, bf16[128,1536]{1,0:T(8,128)(2,1)S(1)} %slice.184.refs_1_, bf16[256,1536]{1,0:T(8,128)(2,1)S(1)} %slice.185.refs_2_, bf16[128,1536]{1,0:T(8,128)(2,1)S(1)} %bitcast.119), custom_call_target="tpu_custom_call" | custom-call | flops 201326592 | bytes 3146752 | tf_op jit(solution)/shard_map/pallas_call | solution.py:189
  81.8 3.3 %collective-permute-done.11 = bf16[20,2,1536]{2,1,0:T(2,128)(2,1)S(1)} collective-permute-done((bf16[20,2,1536]{2,1,0:T(2,128)(2,1)}, bf16[20,2,1536]{2,1,0:T(2,128)(2,1)S(1)}, u32[]{:S(2)}, u32[]{:S(2)}) %collective-permute-start.11) | collective-permute-done | bytes 122912 | tf_op jit(solution)/shard_map/ppermute | solution.py:42
  85.3 7.7 %collective-permute-start.14 = (bf16[2,12,1536]{2,1,0:T(8,128)(2,1)S(1)}, bf16[2,12,1536]{2,1,0:T(8,128)(2,1)S(1)}, u32[]{:S(2)}, u32[]{:S(2)}) collective-permute-start(bf16[2,12,1536]{2,1,0:T(8,128)(2,1)S(1)} %pad_maximum_fusion.11), channel_id=1, source_target_pairs={{49,0},{51,2},{53,4},{55,6},{57,8},{59,10},{61,12},{63,14},{65,16}... | collective-permute-start | bytes 221192 | tf_op jit(solution)/shard_map/ppermute | solution.py:42
  93.0 1.3 collective-permute-start.13
  95.7 1.5 %collective-permute-start.12 = (bf16[2,16,2,1536]{3,2,1,0:T(2,128)(2,1)S(1)}, bf16[2,16,2,1536]{3,2,1,0:T(2,128)(2,1)S(1)}, u32[]{:S(2)}, u32[]{:S(2)}) collective-permute-start(bf16[2,16,2,1536]{3,2,1,0:T(2,128)(2,1)S(1)} %pad_maximum_fusion.5), channel_id=1, source_target_pairs={{1,0},{3,2},{5,4},{7,6},{9,8},{11,10},{13,12},{15,14},{17,16},{19,... | collective-permute-start | bytes 589832 | tf_op jit(solution)/shard_map/ppermute | solution.py:42
  97.2 2.9 %collective-permute-done.12 = bf16[2,16,2,1536]{3,2,1,0:T(2,128)(2,1)S(1)} collective-permute-done((bf16[2,16,2,1536]{3,2,1,0:T(2,128)(2,1)S(1)}, bf16[2,16,2,1536]{3,2,1,0:T(2,128)(2,1)S(1)}, u32[]{:S(2)}, u32[]{:S(2)}) %collective-permute-start.12) | collective-permute-done | bytes 196640 | tf_op jit(solution)/shard_map/ppermute | solution.py:42
  100.6 6.0 %shard_map.61 = (bf16[128,1536]{1,0:T(8,128)(2,1)S(1)}, f32[256,1536]{1,0:T(8,128)S(1)}, f32[256,1536]{1,0:T(8,128)S(1)}) custom-call(f32[1,256]{1,0:T(1,128)S(1)} %convert_element_type.55.refs_0_, bf16[128,1536]{1,0:T(8,128)(2,1)S(1)} %get-tuple-element.41.refs_1_, bf16[256,1536]{1,0:T(8,128)(2,1)S(1)} %get-tuple-element.28.refs_2_, ...), custom_call_target="tpu_custom_call" | custom-call | flops 503316480 | bytes 5899264 | tf_op jit(solution)/shard_map/pallas_call | solution.py:189
  106.6 2.4 %fusion.19 = (bf16[256,2,1536]{2,0,1:T(8,128)(2,1)S(1)}, f32[256,2,1536]{2,0,1:T(8,128)}) fusion(f32[256,1,1536]{2,0,1:T(8,128)S(1)} %bitcast.120, f32[256,1,1536]{2,0,1:T(8,128)S(1)} %bitcast.115, f32[256,1,1536]{2,0,1:T(8,128)S(1)} %bitcast.117, f32[256,1,1536]{2,0,1:T(8,128)S(1)} %bitcast.116, pred[]{:T(512)S(6)} %eq.3), kind=kLoop, calls=%fused_computation.75 | loop fusion | flops 3145728 | bytes 11010049 | tf_op jit(solution)/shard_map/convert.37
  110.1 2.9 %collective-permute-done.15 = bf16[20,2,2,1536]{3,1,0,2:T(2,128)(2,1)S(1)} collective-permute-done((bf16[20,2,2,1536]{3,1,0,2:T(2,128)(2,1)S(1)}, bf16[20,2,2,1536]{3,1,0,2:T(2,128)(2,1)S(1)}, u32[]{:S(2)}, u32[]{:S(2)}) %collective-permute-start.15) | collective-permute-done | bytes 245792 | tf_op jit(solution)/shard_map/ppermute | solution.py:42
  113.0 3.1 %collective-permute-done.16 = bf16[20,2,2,1536]{3,1,0,2:T(2,128)(2,1)S(1)} collective-permute-done((bf16[20,2,2,1536]{3,1,0,2:T(2,128)(2,1)S(1)}, bf16[20,2,2,1536]{3,1,0,2:T(2,128)(2,1)S(1)}, u32[]{:S(2)}, u32[]{:S(2)}) %collective-permute-start.16) | collective-permute-done | bytes 245792 | tf_op jit(solution)/shard_map/ppermute | solution.py:42
  116.2 4.5 %collective-permute-start.18 = (bf16[2,12,2,1536]{3,1,0,2:T(8,128)(2,1)S(1)}, bf16[2,12,2,1536]{3,1,0,2:T(8,128)(2,1)S(1)}, u32[]{:S(2)}, u32[]{:S(2)}) collective-permute-start(bf16[2,12,2,1536]{3,1,0,2:T(8,128)(2,1)S(1)} %pad_maximum_fusion.7), channel_id=1, source_target_pairs={{48,0},{49,1},{50,2},{51,3},{52,4},{53,5},{54,6},{55,7},{56,8},{57... | collective-permute-start | bytes 442376 | tf_op jit(solution)/shard_map/ppermute | solution.py:42
  120.8 1.9 %collective-permute-start.17 = (bf16[2,12,2,1536]{3,1,0,2:T(8,128)(2,1)S(1)}, bf16[2,12,2,1536]{3,1,0,2:T(8,128)(2,1)S(1)}, u32[]{:S(2)}, u32[]{:S(2)}) collective-permute-start(bf16[2,12,2,1536]{3,1,0,2:T(8,128)(2,1)S(1)} %pad_maximum_fusion.6), channel_id=1, source_target_pairs={{0,48},{1,49},{2,50},{3,51},{4,52},{5,53},{6,54},{7,55},{8,56},{9,... | collective-permute-start | bytes 442376 | tf_op jit(solution)/shard_map/ppermute | solution.py:42
  124.0 8.0 %collective-permute-done.17 = bf16[2,12,2,1536]{3,1,0,2:T(8,128)(2,1)S(1)} collective-permute-done((bf16[2,12,2,1536]{3,1,0,2:T(8,128)(2,1)S(1)}, bf16[2,12,2,1536]{3,1,0,2:T(8,128)(2,1)S(1)}, u32[]{:S(2)}, u32[]{:S(2)}) %collective-permute-start.17) | collective-permute-done | bytes 147488 | tf_op jit(solution)/shard_map/ppermute | solution.py:42
  (106 shorter events, 16.3 us)
Async XLA Ops:
  0.6 1.3 copy-start.8
  1.9 8.4 %collective-permute-start.1 = (bf16[2,8,2,1536]{3,1,0,2:T(8,128)(2,1)S(1)}, bf16[2,8,2,1536]{3,1,0,2:T(8,128)(2,1)S(1)}, u32[]{:S(2)}, u32[]{:S(2)}) collective-permute-start(bf16[2,8,2,1536]{3,1,0,2:T(8,128)(2,1)S(1)} %get-tuple-element.37), channel_id=1, source_target_pairs={{48,0},{49,1},{50,2},{51,3},{52,4},{53,5},{54,6},{55,7},{56,8},{57... | collective-permute-start | bytes 294920 | tf_op jit(solution)/shard_map/ppermute | solution.py:42
  8.2 10.1 %collective-permute-start = (bf16[2,8,2,1536]{3,1,0,2:T(8,128)(2,1)S(1)}, bf16[2,8,2,1536]{3,1,0,2:T(8,128)(2,1)S(1)}, u32[]{:S(2)}, u32[]{:S(2)}) collective-permute-start(bf16[2,8,2,1536]{3,1,0,2:T(8,128)(2,1)S(1)} %get-tuple-element.38), channel_id=1, source_target_pairs={{0,48},{1,49},{2,50},{3,51},{4,52},{5,53},{6,54},{7,55},{8,56},{9,... | collective-permute-start | bytes 294920 | tf_op jit(solution)/shard_map/ppermute | solution.py:42
  18.6 17.7 %collective-permute-start.3 = (bf16[20,2,2,1536]{3,1,0,2:T(2,128)(2,1)S(1)}, bf16[20,2,2,1536]{3,1,0,2:T(2,128)(2,1)S(1)}, u32[]{:S(2)}, u32[]{:S(2)}) collective-permute-start(bf16[20,2,2,1536]{3,1,0,2:T(2,128)(2,1)S(1)} %get-tuple-element.29), channel_id=1, source_target_pairs={{2,0},{3,1},{4,2},{5,3},{6,4},{7,5},{8,6},{9,7},{10,8},{11,9},{12,... | collective-permute-start | bytes 737288 | tf_op jit(solution)/shard_map/ppermute | solution.py:42
  29.3 6.8 %collective-permute-start.2 = (bf16[20,2,2,1536]{3,1,0,2:T(2,128)(2,1)S(1)}, bf16[20,2,2,1536]{3,1,0,2:T(2,128)(2,1)S(1)}, u32[]{:S(2)}, u32[]{:S(2)}) collective-permute-start(bf16[20,2,2,1536]{3,1,0,2:T(2,128)(2,1)S(1)} %get-tuple-element.30), channel_id=1, source_target_pairs={{46,0},{47,1},{0,2},{1,3},{2,4},{3,5},{4,6},{5,7},{6,8},{7,9},{8,1... | collective-permute-start | bytes 737288 | tf_op jit(solution)/shard_map/ppermute | solution.py:42
  36.4 1.2 copy-start.6
  38.9 10.6 %collective-permute-start.5 = (bf16[2,8,1536]{2,1,0:T(8,128)(2,1)S(1)}, bf16[2,8,1536]{2,1,0:T(8,128)(2,1)S(1)}, u32[]{:S(2)}, u32[]{:S(2)}) collective-permute-start(bf16[2,8,1536]{2,1,0:T(8,128)(2,1)S(1)} %get-tuple-element.45), channel_id=1, source_target_pairs={{0,49},{2,51},{4,53},{6,55},{8,57},{10,59},{12,61},{14,63},{16,65}... | collective-permute-start | bytes 147464 | tf_op jit(solution)/shard_map/ppermute | solution.py:42
  40.2 10.2 %collective-permute-start.4 = (bf16[16,8,1536]{2,1,0:T(8,128)(2,1)S(1)}, bf16[16,8,1536]{2,1,0:T(8,128)(2,1)S(1)}, u32[]{:S(2)}, u32[]{:S(2)}) collective-permute-start(bf16[16,8,1536]{2,1,0:T(8,128)(2,1)S(1)} %bitcast.114), channel_id=1, source_target_pairs={{0,1},{2,3},{4,5},{6,7},{8,9},{10,11},{12,13},{14,15},{16,17},{18,... | collective-permute-start | bytes 1179656 | tf_op jit(solution)/shard_map/ppermute | solution.py:42
  42.7 7.8 %collective-permute-start.6 = (bf16[2,8,1536]{2,1,0:T(8,128)(2,1)S(1)}, bf16[2,8,1536]{2,1,0:T(8,128)(2,1)S(1)}, u32[]{:S(2)}, u32[]{:S(2)}) collective-permute-start(bf16[2,8,1536]{2,1,0:T(8,128)(2,1)S(1)} %get-tuple-element.44), channel_id=1, source_target_pairs={{48,1},{50,3},{52,5},{54,7},{56,9},{58,11},{60,13},{62,15},{64,17}... | collective-permute-start | bytes 147464 | tf_op jit(solution)/shard_map/ppermute | solution.py:42
  44.0 24.8 %collective-permute-start.9 = (bf16[384,1536]{1,0:T(8,128)(2,1)}, bf16[384,1536]{1,0:T(8,128)(2,1)}, u32[]{:S(2)}, u32[]{:S(2)}) collective-permute-start(bf16[384,1536]{1,0:T(8,128)(2,1)} %pad_maximum_fusion), channel_id=1, source_target_pairs={{1,0},{3,2},{5,4},{7,6},{9,8},{11,10},{13,12},{15,14},{17,16},{19,... | collective-permute-start | bytes 3538952 | tf_op jit(solution)/shard_map/ppermute | solution.py:42
  51.3 7.8 %collective-permute-start.8 = (bf16[20,2,1536]{2,1,0:T(2,128)(2,1)}, bf16[20,2,1536]{2,1,0:T(2,128)(2,1)S(1)}, u32[]{:S(2)}, u32[]{:S(2)}) collective-permute-start(bf16[20,2,1536]{2,1,0:T(2,128)(2,1)} %get-tuple-element.42), channel_id=1, source_target_pairs={{2,0},{3,1},{4,2},{5,3},{6,4},{7,5},{8,6},{9,7},{10,8},{11,9},{12,... | collective-permute-start | bytes 368648 | tf_op jit(solution)/shard_map/ppermute | solution.py:42
  53.5 5.5 %collective-permute-start.7 = (bf16[20,2,1536]{2,1,0:T(2,128)(2,1)S(1)}, bf16[20,2,1536]{2,1,0:T(2,128)(2,1)S(1)}, u32[]{:S(2)}, u32[]{:S(2)}) collective-permute-start(bf16[20,2,1536]{2,1,0:T(2,128)(2,1)S(1)} %get-tuple-element.43), channel_id=1, source_target_pairs={{46,0},{47,1},{0,2},{1,3},{2,4},{3,5},{4,6},{5,7},{6,8},{7,9},{8,1... | collective-permute-start | bytes 368648 | tf_op jit(solution)/shard_map/ppermute | solution.py:42
  59.1 1.5 %copy-start.2 = (bf16[16,8,1536]{2,1,0:T(8,128)(2,1)S(1)}, bf16[16,8,1536]{2,1,0:T(8,128)(2,1)}, u32[]{:S(2)}) copy-start(bf16[16,8,1536]{2,1,0:T(8,128)(2,1)} %param.5) | copy-start | bytes 1179652
  67.9 2.3 %copy-start = (f32[256,1536]{1,0:T(8,128)}, f32[256,1536]{1,0:T(8,128)S(1)}, u32[]{:S(2)}) copy-start(f32[256,1536]{1,0:T(8,128)S(1)} %get-tuple-element.20) | copy-start | bytes 4718596
  67.9 2.4 %copy-start.3 = (bf16[128,1536]{1,0:T(8,128)(2,1)}, bf16[128,1536]{1,0:T(8,128)(2,1)S(1)}, u32[]{:S(2)}) copy-start(bf16[128,1536]{1,0:T(8,128)(2,1)S(1)} %get-tuple-element.17) | copy-start | bytes 1179652
  71.7 9.4 %collective-permute-start.10 = (bf16[20,2,1536]{2,1,0:T(2,128)(2,1)}, bf16[20,2,1536]{2,1,0:T(2,128)(2,1)}, u32[]{:S(2)}, u32[]{:S(2)}) collective-permute-start(bf16[20,2,1536]{2,1,0:T(2,128)(2,1)} %reshape.143), channel_id=1, source_target_pairs={{2,0},{3,1},{4,2},{5,3},{6,4},{7,5},{8,6},{9,7},{10,8},{11,9},{12,... | collective-permute-start | bytes 368648 | tf_op jit(solution)/shard_map/ppermute | solution.py:42
  79.5 5.8 %copy-start.10 = (bf16[2,8,1536]{2,1,0:T(8,128)(2,1)S(1)}, bf16[2,8,1536]{2,1,0:T(8,128)(2,1)}, u32[]{:S(2)}) copy-start(bf16[2,8,1536]{2,1,0:T(8,128)(2,1)} %get-tuple-element.34) | copy-start | bytes 147460
  79.5 13.5 %copy-start.9 = (bf16[2,8,1536]{2,1,0:T(8,128)(2,1)S(1)}, bf16[2,8,1536]{2,1,0:T(8,128)(2,1)}, u32[]{:S(2)}) copy-start(bf16[2,8,1536]{2,1,0:T(8,128)(2,1)} %get-tuple-element.33) | copy-start | bytes 147460
  79.5 5.7 %collective-permute-start.11 = (bf16[20,2,1536]{2,1,0:T(2,128)(2,1)}, bf16[20,2,1536]{2,1,0:T(2,128)(2,1)S(1)}, u32[]{:S(2)}, u32[]{:S(2)}) collective-permute-start(bf16[20,2,1536]{2,1,0:T(2,128)(2,1)} %reshape.144), channel_id=1, source_target_pairs={{46,0},{47,1},{0,2},{1,3},{2,4},{3,5},{4,6},{5,7},{6,8},{7,9},{8,1... | collective-permute-start | bytes 368648 | tf_op jit(solution)/shard_map/ppermute | solution.py:42
  85.3 11.9 %collective-permute-start.14 = (bf16[2,12,1536]{2,1,0:T(8,128)(2,1)S(1)}, bf16[2,12,1536]{2,1,0:T(8,128)(2,1)S(1)}, u32[]{:S(2)}, u32[]{:S(2)}) collective-permute-start(bf16[2,12,1536]{2,1,0:T(8,128)(2,1)S(1)} %pad_maximum_fusion.11), channel_id=1, source_target_pairs={{49,0},{51,2},{53,4},{55,6},{57,8},{59,10},{61,12},{63,14},{65,16}... | collective-permute-start | bytes 221192 | tf_op jit(solution)/shard_map/ppermute | solution.py:42
  93.0 4.2 %collective-permute-start.13 = (bf16[2,12,1536]{2,1,0:T(8,128)(2,1)S(1)}, bf16[2,12,1536]{2,1,0:T(8,128)(2,1)S(1)}, u32[]{:S(2)}, u32[]{:S(2)}) collective-permute-start(bf16[2,12,1536]{2,1,0:T(8,128)(2,1)S(1)} %pad_maximum_fusion.10), channel_id=1, source_target_pairs={{1,48},{3,50},{5,52},{7,54},{9,56},{11,58},{13,60},{15,62},{17,64}... | collective-permute-start | bytes 221192 | tf_op jit(solution)/shard_map/ppermute | solution.py:42
  95.7 4.5 %collective-permute-start.12 = (bf16[2,16,2,1536]{3,2,1,0:T(2,128)(2,1)S(1)}, bf16[2,16,2,1536]{3,2,1,0:T(2,128)(2,1)S(1)}, u32[]{:S(2)}, u32[]{:S(2)}) collective-permute-start(bf16[2,16,2,1536]{3,2,1,0:T(2,128)(2,1)S(1)} %pad_maximum_fusion.5), channel_id=1, source_target_pairs={{1,0},{3,2},{5,4},{7,6},{9,8},{11,10},{13,12},{15,14},{17,16},{19,... | collective-permute-start | bytes 589832 | tf_op jit(solution)/shard_map/ppermute | solution.py:42
  100.3 6.4 %copy-start.1 = (f32[256,1536]{1,0:T(8,128)S(1)}, f32[256,1536]{1,0:T(8,128)}, u32[]{:S(2)}) copy-start(f32[256,1536]{1,0:T(8,128)} %copy-done) | copy-start | bytes 4718596
  100.3 6.4 %copy-start.7 = (f32[256,1536]{1,0:T(8,128)S(1)}, f32[256,1536]{1,0:T(8,128)}, u32[]{:S(2)}) copy-start(f32[256,1536]{1,0:T(8,128)} %get-tuple-element.15) | copy-start | bytes 4718596
  109.0 1.0 copy-start.4
  109.2 3.7 %collective-permute-start.15 = (bf16[20,2,2,1536]{3,1,0,2:T(2,128)(2,1)S(1)}, bf16[20,2,2,1536]{3,1,0,2:T(2,128)(2,1)S(1)}, u32[]{:S(2)}, u32[]{:S(2)}) collective-permute-start(bf16[20,2,2,1536]{3,1,0,2:T(2,128)(2,1)S(1)} %reshape.149), channel_id=1, source_target_pairs={{2,0},{3,1},{4,2},{5,3},{6,4},{7,5},{8,6},{9,7},{10,8},{11,9},{12,... | collective-permute-start | bytes 737288 | tf_op jit(solution)/shard_map/ppermute | solution.py:42
  109.3 6.8 %collective-permute-start.16 = (bf16[20,2,2,1536]{3,1,0,2:T(2,128)(2,1)S(1)}, bf16[20,2,2,1536]{3,1,0,2:T(2,128)(2,1)S(1)}, u32[]{:S(2)}, u32[]{:S(2)}) collective-permute-start(bf16[20,2,2,1536]{3,1,0,2:T(2,128)(2,1)S(1)} %reshape.150), channel_id=1, source_target_pairs={{46,0},{47,1},{0,2},{1,3},{2,4},{3,5},{4,6},{5,7},{6,8},{7,9},{8,1... | collective-permute-start | bytes 737288 | tf_op jit(solution)/shard_map/ppermute | solution.py:42
  110.0 22.0 %copy-start.5 = (f32[256,2,1536]{2,0,1:T(8,128)S(1)}, f32[256,2,1536]{2,0,1:T(8,128)}, u32[]{:S(2)}) copy-start(f32[256,2,1536]{2,0,1:T(8,128)} %get-tuple-element.22) | copy-start | bytes 9437188
  116.2 7.7 %collective-permute-start.18 = (bf16[2,12,2,1536]{3,1,0,2:T(8,128)(2,1)S(1)}, bf16[2,12,2,1536]{3,1,0,2:T(8,128)(2,1)S(1)}, u32[]{:S(2)}, u32[]{:S(2)}) collective-permute-start(bf16[2,12,2,1536]{3,1,0,2:T(8,128)(2,1)S(1)} %pad_maximum_fusion.7), channel_id=1, source_target_pairs={{48,0},{49,1},{50,2},{51,3},{52,4},{53,5},{54,6},{55,7},{56,8},{57... | collective-permute-start | bytes 442376 | tf_op jit(solution)/shard_map/ppermute | solution.py:42
  120.8 11.2 %collective-permute-start.17 = (bf16[2,12,2,1536]{3,1,0,2:T(8,128)(2,1)S(1)}, bf16[2,12,2,1536]{3,1,0,2:T(8,128)(2,1)S(1)}, u32[]{:S(2)}, u32[]{:S(2)}) collective-permute-start(bf16[2,12,2,1536]{3,1,0,2:T(8,128)(2,1)S(1)} %pad_maximum_fusion.6), channel_id=1, source_target_pairs={{0,48},{1,49},{2,50},{3,51},{4,52},{5,53},{6,54},{7,55},{8,56},{9,... | collective-permute-start | bytes 442376 | tf_op jit(solution)/shard_map/ppermute | solution.py:42

commit v6 on v5

--- a/solution.py
+++ b/solution.py
@@ -69,24 +69,22 @@
 
 
 def place(piece, rows, cols, r0, c0):
-    pad = [(r0, rows - r0 - piece.shape[0]), (c0, cols - c0 - piece.shape[1])]
-    return jnp.pad(piece.astype(jnp.float32), pad + [(0, 0)] * (piece.ndim - 2))
-
-
-def return_terms(terms, rows, cols, sizes, src_pipe=None, dst_pipe=None, centre=None):
-    tail = terms.shape[1:]
-    (c0, c1), (t0, t1), (b0, b1), (l0, l1), (r0, r1) = piece_bounds(rows, cols)
+    pad = [(0, 0), (r0, rows - r0 - piece.shape[1]), (c0, cols - c0 - piece.shape[2]), (0, 0)]
+    return jnp.pad(piece.astype(jnp.float32), pad)
+
+
+def return_terms(pieces, rows, cols, sizes, src_pipe=None, dst_pipe=None, centre=None):
+    own, top, bottom, left, right = pieces
+    lead, features = own.shape[0], own.shape[-1]
     if centre is None:
-        centre = terms[c0:c1].reshape((rows, cols) + tail)
-    top = terms[t0:t1].astype(jnp.bfloat16)
-    bottom = terms[b0:b1].astype(jnp.bfloat16)
-    strip = (rows + 2 * MARGIN, MARGIN) + tail
-    left = terms[l0:l1].astype(jnp.bfloat16).reshape(strip)
-    right = terms[r0:r1].astype(jnp.bfloat16).reshape(strip)
+        centre = own.reshape(lead, rows, cols, features)
     from_right = shifted(left, (0, 1), sizes)
     from_left = shifted(right, (0, -1), sizes)
+    strip = (lead, rows + 2 * MARGIN, MARGIN, features)
+    from_right = from_right.reshape(strip)
+    from_left = from_left.reshape(strip)
     inner = slice(MARGIN, MARGIN + rows)
-    sides = jnp.stack([from_right[inner], from_left[inner]], axis=0)
+    sides = jnp.stack([from_right[:, inner], from_left[:, inner]], axis=0)
     if src_pipe is not None:
         sides = shifted(sides, (0, 0), sizes, src_pipe, dst_pipe)
     partial = (
@@ -94,39 +92,47 @@
         + place(sides[0], rows, cols, 0, cols - MARGIN)
         + place(sides[1], rows, cols, 0, 0)
     )
-    band_shape = (MARGIN, cols) + tail
+    band = (lead, MARGIN, cols, features)
     up = jnp.concatenate(
-        [top.reshape(band_shape), from_left[:MARGIN], from_right[:MARGIN]], axis=1
+        [top.reshape(band), from_left[:, :MARGIN], from_right[:, :MARGIN]], axis=2
     )
     down = jnp.concatenate(
-        [bottom.reshape(band_shape), from_left[rows + MARGIN :], from_right[rows + MARGIN :]],
-        axis=1,
+        [bottom.reshape(band), from_left[:, rows + MARGIN :], from_right[:, rows + MARGIN :]],
+        axis=2,
     )
     from_below = shifted(up, (1, 0), sizes, src_pipe, dst_pipe)
     from_above = shifted(down, (-1, 0), sizes, src_pipe, dst_pipe)
     total = partial
     for got, r in ((from_above, 0), (from_below, rows - MARGIN)):
-        total = total + place(got[:, :cols], rows, cols, r, 0)
-        total = total + place(got[:, cols : cols + MARGIN], rows, cols, r, 0)
-        total = total + place(got[:, cols + MARGIN :], rows, cols, r, cols - MARGIN)
+        total = total + place(got[:, :, :cols], rows, cols, r, 0)
+        total = total + place(got[:, :, cols : cols + MARGIN], rows, cols, r, 0)
+        total = total + place(got[:, :, cols + MARGIN :], rows, cols, r, cols - MARGIN)
     return total
 
 
-def attention_kernel(scaling, with_context, with_backward, with_vterm, *refs):
+def attention_kernel(scaling, bounds, with_context, with_grads, with_vterm, centre_only, *refs):
     mask_ref, q_ref, k_ref = refs[:3]
     refs = refs[3:]
-    if with_context or with_backward:
+    if with_context or with_grads:
         u_ref, refs = refs[0], refs[1:]
-    if with_backward or with_vterm:
+    if with_grads or with_vterm:
         d_ref, refs = refs[0], refs[1:]
     if with_context:
         c_ref, refs = refs[0], refs[1:]
-    if with_backward:
-        gq_ref, kt_ref, refs = refs[0], refs[1], refs[2:]
-    if with_backward or with_vterm:
-        (vt_ref,) = refs
+    if with_grads:
+        gq_ref, refs = refs[0], refs[1:]
+    term_refs = refs
     head_dim = q_ref.shape[1] // HEADS
     nt = (((1,), (1,)), ((), ()))
+
+    def store_terms(res, which, lanes):
+        if centre_only:
+            (c0, c1) = bounds[0]
+            term_refs[0][which, :, lanes] = res[c0:c1]
+            return
+        for index, ((s0, s1), ref) in enumerate(zip(bounds, term_refs)):
+            part = res[s0:s1]
+            ref[which, :, lanes] = part if index == 0 else part.astype(ref.dtype)
 
     def head(h, carry):
         lanes = pl.ds(pl.multiple_of(h * head_dim, head_dim), head_dim)
@@ -142,7 +148,7 @@
             c_ref[:, lanes] = jnp.dot(
                 probs.astype(jnp.bfloat16), uh, preferred_element_type=jnp.float32
             ).astype(c_ref.dtype)
-        if with_backward:
+        if with_grads:
             uh = u_ref[:, lanes]
             dh = d_ref[:, lanes]
             dprob = lax.dot_general(dh, uh, nt, preferred_element_type=jnp.float32)
@@ -151,43 +157,47 @@
             gq_ref[:, lanes] = jnp.dot(
                 dscore.astype(jnp.bfloat16), kh, preferred_element_type=jnp.float32
             ).astype(gq_ref.dtype)
-            kt_ref[:, lanes] = jnp.dot(
-                dscore.T.astype(jnp.bfloat16), qh, preferred_element_type=jnp.float32
-            )
-        if with_backward or with_vterm:
+            kterm = jnp.dot(dscore.T.astype(jnp.bfloat16), qh, preferred_element_type=jnp.float32)
+            store_terms(kterm, 0, lanes)
+        if with_grads or with_vterm:
             dh = d_ref[:, lanes]
-            vt_ref[:, lanes] = jnp.dot(
-                probs.T.astype(jnp.bfloat16), dh, preferred_element_type=jnp.float32
-            )
+            vterm = jnp.dot(probs.T.astype(jnp.bfloat16), dh, preferred_element_type=jnp.float32)
+            store_terms(vterm, 1 if with_grads else 0, lanes)
         return carry
 
     lax.fori_loop(0, HEADS, head, 0, unroll=True)
 
 
-def attention(mask, q, k, u=None, d=None, with_context=True, scaling=1.0):
+def attention(
+    mask, q, k, bounds, u=None, d=None, with_context=True, grads=True, centre_only=False,
+    scaling=1.0,
+):
     tokens, features = q.shape
     keys = k.shape[0]
-    with_backward = d is not None and u is not None
-    with_vterm = d is not None and u is None
+    with_grads = grads and d is not None and u is not None
+    with_vterm = d is not None and not with_grads
     outs = []
     if with_context:
         outs.append(jax.ShapeDtypeStruct((tokens, features), jnp.bfloat16))
-    if with_backward:
-        outs += [
-            jax.ShapeDtypeStruct((tokens, features), jnp.bfloat16),
-            jax.ShapeDtypeStruct((keys, features), jnp.float32),
-        ]
-    if with_backward or with_vterm:
-        outs.append(jax.ShapeDtypeStruct((keys, features), jnp.float32))
+    if with_grads:
+        outs.append(jax.ShapeDtypeStruct((tokens, features), jnp.bfloat16))
+    lead = 2 if with_grads else 1
+    if with_grads or with_vterm:
+        for index, (s0, s1) in enumerate(bounds[: 1 if centre_only else len(bounds)]):
+            dtype = jnp.float32 if index == 0 else jnp.bfloat16
+            outs.append(jax.ShapeDtypeStruct((lead, s1 - s0, features), dtype))
     args = [mask, q, k] + [a for a in (u, d) if a is not None]
-    matmuls = 1 + (1 if with_context else 0) + (4 if with_backward else 0) + (1 if with_vterm else 0)
+    matmuls = 1 + (1 if with_context else 0) + (4 if with_grads else 0) + (1 if with_vterm else 0)
     flops = 2 * tokens * keys * features * matmuls
     bytes_accessed = sum(a.size * a.dtype.itemsize for a in args) + sum(
         math.prod(o.shape) * o.dtype.itemsize for o in outs
     )
     vmem = pl.BlockSpec(memory_space=pltpu.VMEM)
     return pl.pallas_call(
-        functools.partial(attention_kernel, scaling, with_context, with_backward, with_vterm),
+        functools.partial(
+            attention_kernel, scaling, tuple(bounds), with_context, with_grads, with_vterm,
+            centre_only,
+        ),
         out_shape=outs,
         in_specs=[vmem] * len(args),
         out_specs=[vmem] * len(outs),
@@ -231,44 +241,38 @@
     mask = allowed.astype(jnp.float32)[None, :]
 
     q = queries_keys[0, 0].reshape(token_count, features)
+    cot = cotangent.reshape(token_count, features)
 
     kv = keys_of(gather_keys(jnp.stack([queries_keys[0, 1], values[0]], axis=2), sizes))
     k = kv[:, 0]
     v = kv[:, 1]
 
     qk_other = shifted(jnp.concatenate([q, k], axis=0), (0, 0), sizes, 1, 0)
-    d_b = cotangent.reshape(token_count, features)
-
-    (context_a,) = attention(mask, q, k, v, scaling=scaling)
+
+    (context_a,) = attention(mask, q, k, bounds, v, scaling=scaling)
 
     c = keys_of(gather_keys(context_a.reshape(tile_rows, tile_cols, features), sizes, 0, 1))
     u = (v.astype(jnp.float32) + c.astype(jnp.float32)).astype(jnp.bfloat16)
 
-    context_b, gq_b, kterm_b, vterm_b = attention(mask, q, k, u, d_b, scaling=scaling)
+    context_b, *vterm_b = attention(mask, q, k, bounds, u, cot, grads=False, scaling=scaling)
 
     qk_other, vterm_b = lax.optimization_barrier((qk_other, vterm_b))
-    (vterm_other,) = attention(
-        mask, qk_other[:token_count], qk_other[token_count:], d=d_b, with_context=False,
-        scaling=scaling,
-    )
-    centre_other = vterm_other[:token_count].reshape(tile_rows, tile_cols, features)
+    (centre_other,) = attention(
+        mask, qk_other[:token_count], qk_other[token_count:], bounds, d=cot,
+        with_context=False, centre_only=True, scaling=scaling,
+    )
+    centre_other = centre_other.reshape(1, tile_rows, tile_cols, features)
 
     d_c = return_terms(vterm_b, tile_rows, tile_cols, sizes, 1, 0, centre_other)
-    d_c = d_c.astype(jnp.bfloat16)
-
-    gq_c, kterm_c, vterm_c = attention(
-        mask, q, k, u, d_c.reshape(token_count, features), with_context=False, scaling=scaling
-    )
-
-    terms = jnp.where(
-        is_first, jnp.stack([kterm_c, vterm_c], axis=1), jnp.stack([kterm_b, vterm_b], axis=1)
-    )
+    d_c = jnp.where(is_first, d_c[0].astype(jnp.bfloat16).reshape(token_count, features), cot)
+
+    grad_q, *terms = attention(mask, q, k, bounds, u, d_c, with_context=False, scaling=scaling)
+
     owned = return_terms(terms, tile_rows, tile_cols, sizes).astype(jnp.bfloat16)
 
     activations = jnp.where(is_first, context_a, context_b).reshape(tile_rows, tile_cols, features)
-    grad_q = jnp.where(is_first, gq_c, gq_b).reshape(tile_rows, tile_cols, features)
-    grad_qk = jnp.stack([grad_q, owned[:, :, 0]], axis=0)
-    return activations[None], grad_qk[None], owned[:, :, 1][None]
+    grad_qk = jnp.stack([grad_q.reshape(tile_rows, tile_cols, features), owned[0]], axis=0)
+    return activations[None], grad_qk[None], owned[1][None]
 
 
 def solution(mesh):

time: 136 us -> 139 us (1.022)
  local copies, waits for them, and re-layouts: 13.3 us -> 17.2 us
  starting transfers between devices: 51.3 us -> 54.5 us
  Pallas kernels: 16.4 us -> 13.9 us
    ppermute x19, starting transfers between devices: 51.3 us -> 54.5 us  [shifted(): return lax.ppermute(x, AXES, pairs_from(offset, sizes, src_pipe, dst_pipe))]
    another operation x5 -> x2, other arithmetic: 5.01 us -> 1.98 us  [the longest x1 1.19 us: return_terms(): sides = jnp.stack([from_right[:, inner], from_left[:, inner]], axis=0)]
    pallas_call x4, Pallas kernels: 16.4 us -> 13.9 us  [attention(): pl.pallas_call(functools.partial(attention_kernel, scaling, tuple(bounds)...]
    unnamed x33 -> x29, local copies, waits for them, and re-layouts: 1.46 us -> 3.62 us
    concatenate x4, other arithmetic: 0.18 us -> 1.79 us  [the longest x2 0.9 us: return_terms(): jnp.concatenate([top.reshape(band), from_left[:, :MARGIN], from_right[:,...]
    slice x16 -> x15, local copies, waits for them, and re-layouts: 1.95 us -> 3.37 us  [the longest x2 1.38 us: return_terms(): from_right[:, rows + MARGIN:]]
    reshape x6 -> x4, local copies, waits for them, and re-layouts: 3.14 us -> 3.38 us  [the longest x2 1.69 us: return_terms(): from_right = from_right.reshape(strip)]
  transfers between devices with their start and end apart: 19 -> 19, of which waited for: 10 -> 11; matrix products, arithmetic and copies ran while one was open for 9% -> 9% of each run, Pallas kernels for 7% -> 5%
where the time goes in v6:
time: 139 us; the launch traced here: 138 us
  starting transfers between devices  54.5 us (39%)
  waiting for transfers between devices  42.3 us (30%)
  local copies, waits for them, and re-layouts  17.2 us (12%)
  Pallas kernels  13.9 us (10%)
  other arithmetic  8.52 us (6%)
    ppermute x19, starting transfers between devices, shifted(): return lax.ppermute(x, AXES, pairs_from(offset, sizes, src_pipe, dst_pipe))  54.5 us
    ppermute x19, waiting for transfers between devices, shifted(): return lax.ppermute(x, AXES, pairs_from(offset, sizes, src_pipe, dst_pipe))  42.3 us
    pallas_call x4, Pallas kernels, attention(): pl.pallas_call(functools.partial(attention_kernel, scaling, tuple(bounds)...  13.9 us
    unnamed x29, local copies, waits for them, and re-layouts  3.62 us
  transfers between devices with their start and end apart: 19, of which 11 were waited for; matrix products, arithmetic and copies ran while one was open for 9% of the time, Pallas kernels for 5%

profile of v6, /device:TPU:6, one launch (start us, length us, event | category | flops | bytes accessed | tf_op | source)
XLA Modules:
  0.0 137.6 jit_solution(9165177353370064785)
XLA Ops:
  1.9 6.2 %collective-permute-start.1 = (bf16[2,8,2,1536]{3,1,0,2:T(8,128)(2,1)S(1)}, bf16[2,8,2,1536]{3,1,0,2:T(8,128)(2,1)S(1)}, u32[]{:S(2)}, u32[]{:S(2)}) collective-permute-start(bf16[2,8,2,1536]{3,1,0,2:T(8,128)(2,1)S(1)} %get-tuple-element.41), channel_id=1, source_target_pairs={{48,0},{49,1},{50,2},{51,3},{52,4},{53,5},{54,6},{55,7},{56,8},{57... | collective-permute-start | bytes 294920 | tf_op jit(solution)/shard_map/ppermute | solution.py:42
  8.2 1.9 %collective-permute-start = (bf16[2,8,2,1536]{3,1,0,2:T(8,128)(2,1)S(1)}, bf16[2,8,2,1536]{3,1,0,2:T(8,128)(2,1)S(1)}, u32[]{:S(2)}, u32[]{:S(2)}) collective-permute-start(bf16[2,8,2,1536]{3,1,0,2:T(8,128)(2,1)S(1)} %get-tuple-element.42), channel_id=1, source_target_pairs={{0,48},{1,49},{2,50},{3,51},{4,52},{5,53},{6,54},{7,55},{8,56},{9,... | collective-permute-start | bytes 294920 | tf_op jit(solution)/shard_map/ppermute | solution.py:42
  10.3 7.9 %collective-permute-done = bf16[2,8,2,1536]{3,1,0,2:T(8,128)(2,1)S(1)} collective-permute-done((bf16[2,8,2,1536]{3,1,0,2:T(8,128)(2,1)S(1)}, bf16[2,8,2,1536]{3,1,0,2:T(8,128)(2,1)S(1)}, u32[]{:S(2)}, u32[]{:S(2)}) %collective-permute-start) | collective-permute-done | bytes 98336 | tf_op jit(solution)/shard_map/ppermute | solution.py:42
  18.6 10.7 %collective-permute-start.3 = (bf16[20,2,2,1536]{3,1,0,2:T(2,128)(2,1)S(1)}, bf16[20,2,2,1536]{3,1,0,2:T(2,128)(2,1)S(1)}, u32[]{:S(2)}, u32[]{:S(2)}) collective-permute-start(bf16[20,2,2,1536]{3,1,0,2:T(2,128)(2,1)S(1)} %get-tuple-element.37), channel_id=1, source_target_pairs={{2,0},{3,1},{4,2},{5,3},{6,4},{7,5},{8,6},{9,7},{10,8},{11,9},{12,... | collective-permute-start | bytes 737288 | tf_op jit(solution)/shard_map/ppermute | solution.py:42
  29.3 6.8 %collective-permute-done.2 = bf16[20,2,2,1536]{3,1,0,2:T(2,128)(2,1)S(1)} collective-permute-done((bf16[20,2,2,1536]{3,1,0,2:T(2,128)(2,1)S(1)}, bf16[20,2,2,1536]{3,1,0,2:T(2,128)(2,1)S(1)}, u32[]{:S(2)}, u32[]{:S(2)}) %collective-permute-start.2) | collective-permute-done | bytes 245792 | tf_op jit(solution)/shard_map/ppermute | solution.py:42
  37.6 1.3 shard_map.58
  38.9 1.3 collective-permute-start.5
  43.9 5.6 %collective-permute-start.9 = (bf16[384,1536]{1,0:T(8,128)(2,1)}, bf16[384,1536]{1,0:T(8,128)(2,1)}, u32[]{:S(2)}, u32[]{:S(2)}) collective-permute-start(bf16[384,1536]{1,0:T(8,128)(2,1)} %pad_maximum_fusion), channel_id=1, source_target_pairs={{1,0},{3,2},{5,4},{7,6},{9,8},{11,10},{13,12},{15,14},{17,16},{19,... | collective-permute-start | bytes 3538952 | tf_op jit(solution)/shard_map/ppermute | solution.py:42
  50.7 2.2 %collective-permute-start.8 = (bf16[20,2,1536]{2,1,0:T(2,128)(2,1)S(1)}, bf16[20,2,1536]{2,1,0:T(2,128)(2,1)S(1)}, u32[]{:S(2)}, u32[]{:S(2)}) collective-permute-start(bf16[20,2,1536]{2,1,0:T(2,128)(2,1)S(1)} %get-tuple-element.46), channel_id=1, source_target_pairs={{2,0},{3,1},{4,2},{5,3},{6,4},{7,5},{8,6},{9,7},{10,8},{11,9},{12,... | collective-permute-start | bytes 368648 | tf_op jit(solution)/shard_map/ppermute | solution.py:42
  53.0 2.4 %collective-permute-done.8 = bf16[20,2,1536]{2,1,0:T(2,128)(2,1)S(1)} collective-permute-done((bf16[20,2,1536]{2,1,0:T(2,128)(2,1)S(1)}, bf16[20,2,1536]{2,1,0:T(2,128)(2,1)S(1)}, u32[]{:S(2)}, u32[]{:S(2)}) %collective-permute-start.8) | collective-permute-done | bytes 122912 | tf_op jit(solution)/shard_map/ppermute | solution.py:42
  55.4 3.0 %collective-permute-done.7 = bf16[20,2,1536]{2,1,0:T(2,128)(2,1)S(1)} collective-permute-done((bf16[20,2,1536]{2,1,0:T(2,128)(2,1)S(1)}, bf16[20,2,1536]{2,1,0:T(2,128)(2,1)S(1)}, u32[]{:S(2)}, u32[]{:S(2)}) %collective-permute-start.7) | collective-permute-done | bytes 122912 | tf_op jit(solution)/shard_map/ppermute | solution.py:42
  58.5 1.3 add_convert_fusion.refs_3_
  59.9 4.9 %shard_map.59 = (bf16[128,1536]{1,0:T(8,128)(2,1)S(1)}, f32[1,128,1536]{2,1,0:T(8,128)}, bf16[1,16,1536]{2,1,0:T(8,128)(2,1)S(1)}, bf16[1,16,1536]{2,1,0:T(8,128...) custom-call(f32[1,256]{1,0:T(1,128)S(1)} %convert_element_type.99.refs_0_, ...), custom_call_target="tpu_custom_call" | custom-call | flops 301989888 | bytes 3884032 | tf_op jit(solution)/shard_map/pallas_call | solution.py:196
  66.0 2.6 %collective-permute-done.9 = bf16[384,1536]{1,0:T(8,128)(2,1)} collective-permute-done((bf16[384,1536]{1,0:T(8,128)(2,1)}, bf16[384,1536]{1,0:T(8,128)(2,1)}, u32[]{:S(2)}, u32[]{:S(2)}) %collective-permute-start.9) | collective-permute-done | bytes 1179680 | tf_op jit(solution)/shard_map/ppermute | solution.py:42
  68.6 3.5 %collective-permute-start.10 = (bf16[1,40,1536]{2,1,0:T(8,128)(2,1)}, bf16[1,40,1536]{2,1,0:T(8,128)(2,1)}, u32[]{:S(2)}, u32[]{:S(2)}) collective-permute-start(bf16[1,40,1536]{2,1,0:T(8,128)(2,1)} %get-tuple-element.25), channel_id=1, source_target_pairs={{2,0},{3,1},{4,2},{5,3},{6,4},{7,5},{8,6},{9,7},{10,8},{11,9},{12,... | collective-permute-start | bytes 368648 | tf_op jit(solution)/shard_map/ppermute | solution.py:42
  74.3 1.6 %shard_map.60 = f32[1,128,1536]{2,1,0:T(8,128)S(1)} custom-call(f32[1,256]{1,0:T(1,128)S(1)} %convert_element_type.99.refs_0_, bf16[128,1536]{1,0:T(8,128)(2,1)S(1)} %slice.146.refs_1_, bf16[256,1536]{1,0:T(8,128)(2,1)S(1)} %slice.147.refs_2_, bf16[128,1536]{1,0:T(8,128)(2,1)S(1)} %bitcast.99), custom_call_target="tpu_custom_call" | custom-call | flops 201326592 | bytes 2360320 | tf_op jit(solution)/shard_map/pallas_call | solution.py:196
  76.0 1.6 %reshape.167 = bf16[1,20,2,1536]{3,2,1,0:T(2,128)(2,1)} reshape(bf16[1,40,1536]{2,1,0:T(8,128)(2,1)} %collective-permute-done.10) | data formatting | bytes 245760 | tf_op jit(solution)/shard_map/reshape | solution.py:84
  77.6 1.6 %slice_bitcast_fusion.8 = bf16[1,1,16,2,1536]{4,3,2,1,0:T(2,128)(2,1)} fusion(bf16[1,20,2,1536]{3,2,1,0:T(2,128)(2,1)} %reshape.167), kind=kLoop, calls=%fused_computation.41 | loop fusion | bytes 196608 | tf_op jit(solution)/shard_map/stack | solution.py:87
  79.2 1.3 fusion.25
  80.5 1.6 %reshape.168 = bf16[1,20,2,1536]{3,2,1,0:T(2,128)(2,1)} reshape(bf16[1,40,1536]{2,1,0:T(8,128)(2,1)} %collective-permute-done.11) | data formatting | bytes 245760 | tf_op jit(solution)/shard_map/reshape | solution.py:85
  84.7 7.7 %collective-permute-start.14 = (bf16[1,2,12,1536]{3,2,1,0:T(8,128)(2,1)S(1)}, bf16[1,2,12,1536]{3,2,1,0:T(8,128)(2,1)S(1)}, u32[]{:S(2)}, u32[]{:S(2)}) collective-permute-start(bf16[1,2,12,1536]{3,2,1,0:T(8,128)(2,1)S(1)} %pad_maximum_fusion.11), channel_id=1, source_target_pairs={{49,0},{51,2},{53,4},{55,6},{57,8},{59,10},{61,12},{63,14},{65,16}... | collective-permute-start | bytes 221192 | tf_op jit(solution)/shard_map/ppermute | solution.py:42
  93.2 1.3 collective-permute-start.13
  95.7 1.5 %collective-permute-start.12 = (bf16[2,1,16,2,1536]{4,3,2,1,0:T(2,128)(2,1)S(1)}, bf16[2,1,16,2,1536]{4,3,2,1,0:T(2,128)(2,1)S(1)}, u32[]{:S(2)}, u32[]{:S(2)}) collective-permute-start(bf16[2,1,16,2,1536]{4,3,2,1,0:T(2,128)(2,1)S(1)} %pad_maximum_fusion.5), channel_id=1, source_target_pairs={{1,0},{3,2},{5,4},{7,6},{9,8},{11,10},{13,12},{15,14},{17,16},{19,... | collective-permute-start | bytes 589832 | tf_op jit(solution)/shard_map/ppermute | solution.py:42
  97.3 2.9 %collective-permute-done.12 = bf16[2,1,16,2,1536]{4,3,2,1,0:T(2,128)(2,1)S(1)} collective-permute-done((bf16[2,1,16,2,1536]{4,3,2,1,0:T(2,128)(2,1)S(1)}, bf16[2,1,16,2,1536]{4,3,2,1,0:T(2,128)(2,1)S(1)}, u32[]{:S(2)}, u32[]{:S(2)}) %collective-permute-start.12) | collective-permute-done | bytes 196640 | tf_op jit(solution)/shard_map/ppermute | solution.py:42
  100.7 6.0 %shard_map.61 = (bf16[128,1536]{1,0:T(8,128)(2,1)S(1)}, f32[2,128,1536]{2,1,0:T(8,128)S(1)}, bf16[2,16,1536]{2,1,0:T(8,128)(2,1)S(1)}, bf16[2,16,1536]{2,1,0:T(8...) custom-call(f32[1,256]{1,0:T(1,128)S(1)} %convert_element_type.99.refs_0_, ...), custom_call_target="tpu_custom_call" | custom-call | flops 503316480 | bytes 5014528 | tf_op jit(solution)/shard_map/pallas_call | solution.py:196
  107.9 4.0 %collective-permute-start.15 = (bf16[2,40,1536]{2,1,0:T(8,128)(2,1)S(1)}, bf16[2,40,1536]{2,1,0:T(8,128)(2,1)S(1)}, u32[]{:S(2)}, u32[]{:S(2)}) collective-permute-start(bf16[2,40,1536]{2,1,0:T(8,128)(2,1)S(1)} %get-tuple-element.31), channel_id=1, source_target_pairs={{2,0},{3,1},{4,2},{5,3},{6,4},{7,5},{8,6},{9,7},{10,8},{11,9},{12,... | collective-permute-start | bytes 737288 | tf_op jit(solution)/shard_map/ppermute | solution.py:42
  112.7 2.9 %collective-permute-done.15 = bf16[2,40,1536]{2,1,0:T(8,128)(2,1)S(1)} collective-permute-done((bf16[2,40,1536]{2,1,0:T(8,128)(2,1)S(1)}, bf16[2,40,1536]{2,1,0:T(8,128)(2,1)S(1)}, u32[]{:S(2)}, u32[]{:S(2)}) %collective-permute-start.15) | collective-permute-done | bytes 245792 | tf_op jit(solution)/shard_map/ppermute | solution.py:42
  115.9 3.6 %collective-permute-done.16 = bf16[2,40,1536]{2,1,0:T(8,128)(2,1)S(1)} collective-permute-done((bf16[2,40,1536]{2,1,0:T(8,128)(2,1)S(1)}, bf16[2,40,1536]{2,1,0:T(8,128)(2,1)S(1)}, u32[]{:S(2)}, u32[]{:S(2)}) %collective-permute-start.16) | collective-permute-done | bytes 245792 | tf_op jit(solution)/shard_map/ppermute | solution.py:42
  119.9 4.1 %collective-permute-start.18 = (bf16[2,2,12,1536]{3,2,1,0:T(8,128)(2,1)S(1)}, bf16[2,2,12,1536]{3,2,1,0:T(8,128)(2,1)S(1)}, u32[]{:S(2)}, u32[]{:S(2)}) collective-permute-start(bf16[2,2,12,1536]{3,2,1,0:T(8,128)(2,1)S(1)} %pad_maximum_fusion.7), channel_id=1, source_target_pairs={{48,0},{49,1},{50,2},{51,3},{52,4},{53,5},{54,6},{55,7},{56,8},{57... | collective-permute-start | bytes 442376 | tf_op jit(solution)/shard_map/ppermute | solution.py:42
  124.0 1.9 %collective-permute-start.17 = (bf16[2,2,12,1536]{3,2,1,0:T(8,128)(2,1)S(1)}, bf16[2,2,12,1536]{3,2,1,0:T(8,128)(2,1)S(1)}, u32[]{:S(2)}, u32[]{:S(2)}) collective-permute-start(bf16[2,2,12,1536]{3,2,1,0:T(8,128)(2,1)S(1)} %pad_maximum_fusion.6), channel_id=1, source_target_pairs={{0,48},{1,49},{2,50},{3,51},{4,52},{5,53},{6,54},{7,55},{8,56},{9,... | collective-permute-start | bytes 442376 | tf_op jit(solution)/shard_map/ppermute | solution.py:42
  126.0 1.5 %collective-permute-done.18 = bf16[2,2,12,1536]{3,2,1,0:T(8,128)(2,1)S(1)} collective-permute-done((bf16[2,2,12,1536]{3,2,1,0:T(8,128)(2,1)S(1)}, bf16[2,2,12,1536]{3,2,1,0:T(8,128)(2,1)S(1)}, u32[]{:S(2)}, u32[]{:S(2)}) %collective-permute-start.18) | collective-permute-done | bytes 147488 | tf_op jit(solution)/shard_map/ppermute | solution.py:42
  127.5 7.7 %collective-permute-done.17 = bf16[2,2,12,1536]{3,2,1,0:T(8,128)(2,1)S(1)} collective-permute-done((bf16[2,2,12,1536]{3,2,1,0:T(8,128)(2,1)S(1)}, bf16[2,2,12,1536]{3,2,1,0:T(8,128)(2,1)S(1)}, u32[]{:S(2)}, u32[]{:S(2)}) %collective-permute-start.17) | collective-permute-done | bytes 147488 | tf_op jit(solution)/shard_map/ppermute | solution.py:42
  (95 shorter events, 21.8 us)
Async XLA Ops:
  0.6 1.3 copy-start.8
  1.9 8.4 %collective-permute-start.1 = (bf16[2,8,2,1536]{3,1,0,2:T(8,128)(2,1)S(1)}, bf16[2,8,2,1536]{3,1,0,2:T(8,128)(2,1)S(1)}, u32[]{:S(2)}, u32[]{:S(2)}) collective-permute-start(bf16[2,8,2,1536]{3,1,0,2:T(8,128)(2,1)S(1)} %get-tuple-element.41), channel_id=1, source_target_pairs={{48,0},{49,1},{50,2},{51,3},{52,4},{53,5},{54,6},{55,7},{56,8},{57... | collective-permute-start | bytes 294920 | tf_op jit(solution)/shard_map/ppermute | solution.py:42
  8.2 10.1 %collective-permute-start = (bf16[2,8,2,1536]{3,1,0,2:T(8,128)(2,1)S(1)}, bf16[2,8,2,1536]{3,1,0,2:T(8,128)(2,1)S(1)}, u32[]{:S(2)}, u32[]{:S(2)}) collective-permute-start(bf16[2,8,2,1536]{3,1,0,2:T(8,128)(2,1)S(1)} %get-tuple-element.42), channel_id=1, source_target_pairs={{0,48},{1,49},{2,50},{3,51},{4,52},{5,53},{6,54},{7,55},{8,56},{9,... | collective-permute-start | bytes 294920 | tf_op jit(solution)/shard_map/ppermute | solution.py:42
  18.6 17.7 %collective-permute-start.3 = (bf16[20,2,2,1536]{3,1,0,2:T(2,128)(2,1)S(1)}, bf16[20,2,2,1536]{3,1,0,2:T(2,128)(2,1)S(1)}, u32[]{:S(2)}, u32[]{:S(2)}) collective-permute-start(bf16[20,2,2,1536]{3,1,0,2:T(2,128)(2,1)S(1)} %get-tuple-element.37), channel_id=1, source_target_pairs={{2,0},{3,1},{4,2},{5,3},{6,4},{7,5},{8,6},{9,7},{10,8},{11,9},{12,... | collective-permute-start | bytes 737288 | tf_op jit(solution)/shard_map/ppermute | solution.py:42
  29.3 6.8 %collective-permute-start.2 = (bf16[20,2,2,1536]{3,1,0,2:T(2,128)(2,1)S(1)}, bf16[20,2,2,1536]{3,1,0,2:T(2,128)(2,1)S(1)}, u32[]{:S(2)}, u32[]{:S(2)}) collective-permute-start(bf16[20,2,2,1536]{3,1,0,2:T(2,128)(2,1)S(1)} %get-tuple-element.38), channel_id=1, source_target_pairs={{46,0},{47,1},{0,2},{1,3},{2,4},{3,5},{4,6},{5,7},{6,8},{7,9},{8,1... | collective-permute-start | bytes 737288 | tf_op jit(solution)/shard_map/ppermute | solution.py:42
  36.4 1.2 copy-start.7
  38.9 10.6 %collective-permute-start.5 = (bf16[2,8,1536]{2,1,0:T(8,128)(2,1)S(1)}, bf16[2,8,1536]{2,1,0:T(8,128)(2,1)S(1)}, u32[]{:S(2)}, u32[]{:S(2)}) collective-permute-start(bf16[2,8,1536]{2,1,0:T(8,128)(2,1)S(1)} %get-tuple-element.49), channel_id=1, source_target_pairs={{0,49},{2,51},{4,53},{6,55},{8,57},{10,59},{12,61},{14,63},{16,65}... | collective-permute-start | bytes 147464 | tf_op jit(solution)/shard_map/ppermute | solution.py:42
  40.2 10.2 %collective-permute-start.4 = (bf16[16,8,1536]{2,1,0:T(8,128)(2,1)S(1)}, bf16[16,8,1536]{2,1,0:T(8,128)(2,1)S(1)}, u32[]{:S(2)}, u32[]{:S(2)}) collective-permute-start(bf16[16,8,1536]{2,1,0:T(8,128)(2,1)S(1)} %bitcast.100), channel_id=1, source_target_pairs={{0,1},{2,3},{4,5},{6,7},{8,9},{10,11},{12,13},{14,15},{16,17},{18,... | collective-permute-start | bytes 1179656 | tf_op jit(solution)/shard_map/ppermute | solution.py:42
  42.6 7.8 %collective-permute-start.6 = (bf16[2,8,1536]{2,1,0:T(8,128)(2,1)S(1)}, bf16[2,8,1536]{2,1,0:T(8,128)(2,1)S(1)}, u32[]{:S(2)}, u32[]{:S(2)}) collective-permute-start(bf16[2,8,1536]{2,1,0:T(8,128)(2,1)S(1)} %get-tuple-element.48), channel_id=1, source_target_pairs={{48,1},{50,3},{52,5},{54,7},{56,9},{58,11},{60,13},{62,15},{64,17}... | collective-permute-start | bytes 147464 | tf_op jit(solution)/shard_map/ppermute | solution.py:42
  43.9 24.7 %collective-permute-start.9 = (bf16[384,1536]{1,0:T(8,128)(2,1)}, bf16[384,1536]{1,0:T(8,128)(2,1)}, u32[]{:S(2)}, u32[]{:S(2)}) collective-permute-start(bf16[384,1536]{1,0:T(8,128)(2,1)} %pad_maximum_fusion), channel_id=1, source_target_pairs={{1,0},{3,2},{5,4},{7,6},{9,8},{11,10},{13,12},{15,14},{17,16},{19,... | collective-permute-start | bytes 3538952 | tf_op jit(solution)/shard_map/ppermute | solution.py:42
  50.7 4.7 %collective-permute-start.8 = (bf16[20,2,1536]{2,1,0:T(2,128)(2,1)S(1)}, bf16[20,2,1536]{2,1,0:T(2,128)(2,1)S(1)}, u32[]{:S(2)}, u32[]{:S(2)}) collective-permute-start(bf16[20,2,1536]{2,1,0:T(2,128)(2,1)S(1)} %get-tuple-element.46), channel_id=1, source_target_pairs={{2,0},{3,1},{4,2},{5,3},{6,4},{7,5},{8,6},{9,7},{10,8},{11,9},{12,... | collective-permute-start | bytes 368648 | tf_op jit(solution)/shard_map/ppermute | solution.py:42
  52.9 5.5 %collective-permute-start.7 = (bf16[20,2,1536]{2,1,0:T(2,128)(2,1)S(1)}, bf16[20,2,1536]{2,1,0:T(2,128)(2,1)S(1)}, u32[]{:S(2)}, u32[]{:S(2)}) collective-permute-start(bf16[20,2,1536]{2,1,0:T(2,128)(2,1)S(1)} %get-tuple-element.47), channel_id=1, source_target_pairs={{46,0},{47,1},{0,2},{1,3},{2,4},{3,5},{4,6},{5,7},{6,8},{7,9},{8,1... | collective-permute-start | bytes 368648 | tf_op jit(solution)/shard_map/ppermute | solution.py:42
  55.4 4.4 %copy-start = (bf16[16,8,1536]{2,1,0:T(8,128)(2,1)S(1)}, bf16[16,8,1536]{2,1,0:T(8,128)(2,1)}, u32[]{:S(2)}) copy-start(bf16[16,8,1536]{2,1,0:T(8,128)(2,1)} %param.5) | copy-start | bytes 1179652
  64.8 0.6 copy-start.5
  65.4 0.6 copy-start.6
  66.0 8.3 %copy-start.3 = (bf16[128,1536]{1,0:T(8,128)(2,1)}, bf16[128,1536]{1,0:T(8,128)(2,1)S(1)}, u32[]{:S(2)}) copy-start(bf16[128,1536]{1,0:T(8,128)(2,1)S(1)} %get-tuple-element.19) | copy-start | bytes 1179652
  68.6 7.4 %collective-permute-start.10 = (bf16[1,40,1536]{2,1,0:T(8,128)(2,1)}, bf16[1,40,1536]{2,1,0:T(8,128)(2,1)}, u32[]{:S(2)}, u32[]{:S(2)}) collective-permute-start(bf16[1,40,1536]{2,1,0:T(8,128)(2,1)} %get-tuple-element.25), channel_id=1, source_target_pairs={{2,0},{3,1},{4,2},{5,3},{6,4},{7,5},{8,6},{9,7},{10,8},{11,9},{12,... | collective-permute-start | bytes 368648 | tf_op jit(solution)/shard_map/ppermute | solution.py:42
  74.3 6.2 %collective-permute-start.11 = (bf16[1,40,1536]{2,1,0:T(8,128)(2,1)}, bf16[1,40,1536]{2,1,0:T(8,128)(2,1)}, u32[]{:S(2)}, u32[]{:S(2)}) collective-permute-start(bf16[1,40,1536]{2,1,0:T(8,128)(2,1)} %get-tuple-element.26), channel_id=1, source_target_pairs={{46,0},{47,1},{0,2},{1,3},{2,4},{3,5},{4,6},{5,7},{6,8},{7,9},{8,1... | collective-permute-start | bytes 368648 | tf_op jit(solution)/shard_map/ppermute | solution.py:42
  84.7 12.5 %collective-permute-start.14 = (bf16[1,2,12,1536]{3,2,1,0:T(8,128)(2,1)S(1)}, bf16[1,2,12,1536]{3,2,1,0:T(8,128)(2,1)S(1)}, u32[]{:S(2)}, u32[]{:S(2)}) collective-permute-start(bf16[1,2,12,1536]{3,2,1,0:T(8,128)(2,1)S(1)} %pad_maximum_fusion.11), channel_id=1, source_target_pairs={{49,0},{51,2},{53,4},{55,6},{57,8},{59,10},{61,12},{63,14},{65,16}... | collective-permute-start | bytes 221192 | tf_op jit(solution)/shard_map/ppermute | solution.py:42
  93.2 4.0 %collective-permute-start.13 = (bf16[1,2,12,1536]{3,2,1,0:T(8,128)(2,1)S(1)}, bf16[1,2,12,1536]{3,2,1,0:T(8,128)(2,1)S(1)}, u32[]{:S(2)}, u32[]{:S(2)}) collective-permute-start(bf16[1,2,12,1536]{3,2,1,0:T(8,128)(2,1)S(1)} %pad_maximum_fusion.10), channel_id=1, source_target_pairs={{1,48},{3,50},{5,52},{7,54},{9,56},{11,58},{13,60},{15,62},{17,64}... | collective-permute-start | bytes 221192 | tf_op jit(solution)/shard_map/ppermute | solution.py:42
  95.7 4.5 %collective-permute-start.12 = (bf16[2,1,16,2,1536]{4,3,2,1,0:T(2,128)(2,1)S(1)}, bf16[2,1,16,2,1536]{4,3,2,1,0:T(2,128)(2,1)S(1)}, u32[]{:S(2)}, u32[]{:S(2)}) collective-permute-start(bf16[2,1,16,2,1536]{4,3,2,1,0:T(2,128)(2,1)S(1)} %pad_maximum_fusion.5), channel_id=1, source_target_pairs={{1,0},{3,2},{5,4},{7,6},{9,8},{11,10},{13,12},{15,14},{17,16},{19,... | collective-permute-start | bytes 589832 | tf_op jit(solution)/shard_map/ppermute | solution.py:42
  100.7 11.2 %copy-start.4 = (bf16[128,1536]{1,0:T(8,128)(2,1)S(1)}, bf16[128,1536]{1,0:T(8,128)(2,1)}, u32[]{:S(2)}) copy-start(bf16[128,1536]{1,0:T(8,128)(2,1)} %copy-done.3) | copy-start | bytes 1179652
  106.7 1.2 copy-start.1
  107.9 7.7 %collective-permute-start.15 = (bf16[2,40,1536]{2,1,0:T(8,128)(2,1)S(1)}, bf16[2,40,1536]{2,1,0:T(8,128)(2,1)S(1)}, u32[]{:S(2)}, u32[]{:S(2)}) collective-permute-start(bf16[2,40,1536]{2,1,0:T(8,128)(2,1)S(1)} %get-tuple-element.31), channel_id=1, source_target_pairs={{2,0},{3,1},{4,2},{5,3},{6,4},{7,5},{8,6},{9,7},{10,8},{11,9},{12,... | collective-permute-start | bytes 737288 | tf_op jit(solution)/shard_map/ppermute | solution.py:42
  112.7 22.6 %copy-start.2 = (f32[2,128,1536]{2,1,0:T(8,128)S(1)}, f32[2,128,1536]{2,1,0:T(8,128)}, u32[]{:S(2)}) copy-start(f32[2,128,1536]{2,1,0:T(8,128)} %copy-done.1) | copy-start | bytes 4718596
  112.7 6.8 %collective-permute-start.16 = (bf16[2,40,1536]{2,1,0:T(8,128)(2,1)S(1)}, bf16[2,40,1536]{2,1,0:T(8,128)(2,1)S(1)}, u32[]{:S(2)}, u32[]{:S(2)}) collective-permute-start(bf16[2,40,1536]{2,1,0:T(8,128)(2,1)S(1)} %get-tuple-element.32), channel_id=1, source_target_pairs={{46,0},{47,1},{0,2},{1,3},{2,4},{3,5},{4,6},{5,7},{6,8},{7,9},{8,1... | collective-permute-start | bytes 737288 | tf_op jit(solution)/shard_map/ppermute | solution.py:42
  119.9 7.6 %collective-permute-start.18 = (bf16[2,2,12,1536]{3,2,1,0:T(8,128)(2,1)S(1)}, bf16[2,2,12,1536]{3,2,1,0:T(8,128)(2,1)S(1)}, u32[]{:S(2)}, u32[]{:S(2)}) collective-permute-start(bf16[2,2,12,1536]{3,2,1,0:T(8,128)(2,1)S(1)} %pad_maximum_fusion.7), channel_id=1, source_target_pairs={{48,0},{49,1},{50,2},{51,3},{52,4},{53,5},{54,6},{55,7},{56,8},{57... | collective-permute-start | bytes 442376 | tf_op jit(solution)/shard_map/ppermute | solution.py:42
  124.0 11.2 %collective-permute-start.17 = (bf16[2,2,12,1536]{3,2,1,0:T(8,128)(2,1)S(1)}, bf16[2,2,12,1536]{3,2,1,0:T(8,128)(2,1)S(1)}, u32[]{:S(2)}, u32[]{:S(2)}) collective-permute-start(bf16[2,2,12,1536]{3,2,1,0:T(8,128)(2,1)S(1)} %pad_maximum_fusion.6), channel_id=1, source_target_pairs={{0,48},{1,49},{2,50},{3,51},{4,52},{5,53},{6,54},{7,55},{8,56},{9,... | collective-permute-start | bytes 442376 | tf_op jit(solution)/shard_map/ppermute | solution.py:42

commit v7 on v6

--- a/solution.py
+++ b/solution.py
@@ -111,8 +111,15 @@
 
 
 def attention_kernel(scaling, bounds, with_context, with_grads, with_vterm, centre_only, *refs):
-    mask_ref, q_ref, k_ref = refs[:3]
-    refs = refs[3:]
+    if centre_only:
+        mask_ref, qk_ref = refs[:2]
+        tokens = qk_ref.shape[0] - mask_ref.shape[1]
+        q_ref = qk_ref.at[:tokens]
+        k_ref = qk_ref.at[tokens:]
+        refs = refs[2:]
+    else:
+        mask_ref, q_ref, k_ref = refs[:3]
+        refs = refs[3:]
     if with_context or with_grads:
         u_ref, refs = refs[0], refs[1:]
     if with_grads or with_vterm:
@@ -172,8 +179,12 @@
     mask, q, k, bounds, u=None, d=None, with_context=True, grads=True, centre_only=False,
     scaling=1.0,
 ):
-    tokens, features = q.shape
-    keys = k.shape[0]
+    if centre_only:
+        keys = mask.shape[1]
+        tokens, features = q.shape[0] - keys, q.shape[1]
+    else:
+        tokens, features = q.shape
+        keys = k.shape[0]
     with_grads = grads and d is not None and u is not None
     with_vterm = d is not None and not with_grads
     outs = []
@@ -186,7 +197,7 @@
         for index, (s0, s1) in enumerate(bounds[: 1 if centre_only else len(bounds)]):
             dtype = jnp.float32 if index == 0 else jnp.bfloat16
             outs.append(jax.ShapeDtypeStruct((lead, s1 - s0, features), dtype))
-    args = [mask, q, k] + [a for a in (u, d) if a is not None]
+    args = [mask, q] + ([] if centre_only else [k]) + [a for a in (u, d) if a is not None]
     matmuls = 1 + (1 if with_context else 0) + (4 if with_grads else 0) + (1 if with_vterm else 0)
     flops = 2 * tokens * keys * features * matmuls
     bytes_accessed = sum(a.size * a.dtype.itemsize for a in args) + sum(
@@ -258,8 +269,7 @@
 
     qk_other, vterm_b = lax.optimization_barrier((qk_other, vterm_b))
     (centre_other,) = attention(
-        mask, qk_other[:token_count], qk_other[token_count:], bounds, d=cot,
-        with_context=False, centre_only=True, scaling=scaling,
+        mask, qk_other, None, bounds, d=cot, with_context=False, centre_only=True, scaling=scaling
     )
     centre_other = centre_other.reshape(1, tile_rows, tile_cols, features)
 

time: 139 us -> 138 us (level)
  local copies, waits for them, and re-layouts: 17.2 us -> 15.8 us
    slice x2 -> x0, local copies, waits for them, and re-layouts: 2.21 us -> none  [the longest x1 1.19 us: body(): qk_other[token_count:]]
  transfers between devices with their start and end apart: 19 -> 19, of which waited for: 11 -> 11; matrix products, arithmetic and copies ran while one was open for 9% -> 8% of each run, Pallas kernels for 5% -> 6%
where the time goes in v7:
time: 138 us; the launch traced here: 137 us
  starting transfers between devices  54.5 us (39%)
  waiting for transfers between devices  41.5 us (30%)
  local copies, waits for them, and re-layouts  15.8 us (11%)
  Pallas kernels  15.1 us (11%)
  other arithmetic  8.52 us (6%)
    ppermute x19, starting transfers between devices, shifted(): return lax.ppermute(x, AXES, pairs_from(offset, sizes, src_pipe, dst_pipe))  54.5 us
    ppermute x19, waiting for transfers between devices, shifted(): return lax.ppermute(x, AXES, pairs_from(offset, sizes, src_pipe, dst_pipe))  41.5 us
    pallas_call x4, Pallas kernels, attention(): pl.pallas_call(functools.partial(attention_kernel, scaling, tuple(bounds)...  15.1 us
    unnamed x29, local copies, waits for them, and re-layouts  4.36 us
  transfers between devices with their start and end apart: 19, of which 11 were waited for; matrix products, arithmetic and copies ran while one was open for 8% of the time, Pallas kernels for 6%

profile of v7, /device:TPU:6, one launch (start us, length us, event | category | flops | bytes accessed | tf_op | source)
XLA Modules:
  0.0 136.7 jit_solution(9094591469913407515)
XLA Ops:
  1.9 6.2 %collective-permute-start.1 = (bf16[2,8,2,1536]{3,1,0,2:T(8,128)(2,1)S(1)}, bf16[2,8,2,1536]{3,1,0,2:T(8,128)(2,1)S(1)}, u32[]{:S(2)}, u32[]{:S(2)}) collective-permute-start(bf16[2,8,2,1536]{3,1,0,2:T(8,128)(2,1)S(1)} %get-tuple-element.41), channel_id=1, source_target_pairs={{48,0},{49,1},{50,2},{51,3},{52,4},{53,5},{54,6},{55,7},{56,8},{57... | collective-permute-start | bytes 294920 | tf_op jit(solution)/shard_map/ppermute | solution.py:42
  8.2 1.9 %collective-permute-start = (bf16[2,8,2,1536]{3,1,0,2:T(8,128)(2,1)S(1)}, bf16[2,8,2,1536]{3,1,0,2:T(8,128)(2,1)S(1)}, u32[]{:S(2)}, u32[]{:S(2)}) collective-permute-start(bf16[2,8,2,1536]{3,1,0,2:T(8,128)(2,1)S(1)} %get-tuple-element.42), channel_id=1, source_target_pairs={{0,48},{1,49},{2,50},{3,51},{4,52},{5,53},{6,54},{7,55},{8,56},{9,... | collective-permute-start | bytes 294920 | tf_op jit(solution)/shard_map/ppermute | solution.py:42
  10.3 7.9 %collective-permute-done = bf16[2,8,2,1536]{3,1,0,2:T(8,128)(2,1)S(1)} collective-permute-done((bf16[2,8,2,1536]{3,1,0,2:T(8,128)(2,1)S(1)}, bf16[2,8,2,1536]{3,1,0,2:T(8,128)(2,1)S(1)}, u32[]{:S(2)}, u32[]{:S(2)}) %collective-permute-start) | collective-permute-done | bytes 98336 | tf_op jit(solution)/shard_map/ppermute | solution.py:42
  18.6 10.7 %collective-permute-start.3 = (bf16[20,2,2,1536]{3,1,0,2:T(2,128)(2,1)S(1)}, bf16[20,2,2,1536]{3,1,0,2:T(2,128)(2,1)S(1)}, u32[]{:S(2)}, u32[]{:S(2)}) collective-permute-start(bf16[20,2,2,1536]{3,1,0,2:T(2,128)(2,1)S(1)} %get-tuple-element.37), channel_id=1, source_target_pairs={{2,0},{3,1},{4,2},{5,3},{6,4},{7,5},{8,6},{9,7},{10,8},{11,9},{12,... | collective-permute-start | bytes 737288 | tf_op jit(solution)/shard_map/ppermute | solution.py:42
  29.3 6.8 %collective-permute-done.2 = bf16[20,2,2,1536]{3,1,0,2:T(2,128)(2,1)S(1)} collective-permute-done((bf16[20,2,2,1536]{3,1,0,2:T(2,128)(2,1)S(1)}, bf16[20,2,2,1536]{3,1,0,2:T(2,128)(2,1)S(1)}, u32[]{:S(2)}, u32[]{:S(2)}) %collective-permute-start.2) | collective-permute-done | bytes 245792 | tf_op jit(solution)/shard_map/ppermute | solution.py:42
  37.6 1.3 shard_map.58
  38.9 1.3 collective-permute-start.5
  43.9 5.6 %collective-permute-start.9 = (bf16[384,1536]{1,0:T(8,128)(2,1)}, bf16[384,1536]{1,0:T(8,128)(2,1)}, u32[]{:S(2)}, u32[]{:S(2)}) collective-permute-start(bf16[384,1536]{1,0:T(8,128)(2,1)} %pad_maximum_fusion), channel_id=1, source_target_pairs={{1,0},{3,2},{5,4},{7,6},{9,8},{11,10},{13,12},{15,14},{17,16},{19,... | collective-permute-start | bytes 3538952 | tf_op jit(solution)/shard_map/ppermute | solution.py:42
  50.7 2.2 %collective-permute-start.8 = (bf16[20,2,1536]{2,1,0:T(2,128)(2,1)S(1)}, bf16[20,2,1536]{2,1,0:T(2,128)(2,1)S(1)}, u32[]{:S(2)}, u32[]{:S(2)}) collective-permute-start(bf16[20,2,1536]{2,1,0:T(2,128)(2,1)S(1)} %get-tuple-element.46), channel_id=1, source_target_pairs={{2,0},{3,1},{4,2},{5,3},{6,4},{7,5},{8,6},{9,7},{10,8},{11,9},{12,... | collective-permute-start | bytes 368648 | tf_op jit(solution)/shard_map/ppermute | solution.py:42
  53.0 2.4 %collective-permute-done.8 = bf16[20,2,1536]{2,1,0:T(2,128)(2,1)S(1)} collective-permute-done((bf16[20,2,1536]{2,1,0:T(2,128)(2,1)S(1)}, bf16[20,2,1536]{2,1,0:T(2,128)(2,1)S(1)}, u32[]{:S(2)}, u32[]{:S(2)}) %collective-permute-start.8) | collective-permute-done | bytes 122912 | tf_op jit(solution)/shard_map/ppermute | solution.py:42
  55.4 3.0 %collective-permute-done.7 = bf16[20,2,1536]{2,1,0:T(2,128)(2,1)S(1)} collective-permute-done((bf16[20,2,1536]{2,1,0:T(2,128)(2,1)S(1)}, bf16[20,2,1536]{2,1,0:T(2,128)(2,1)S(1)}, u32[]{:S(2)}, u32[]{:S(2)}) %collective-permute-start.7) | collective-permute-done | bytes 122912 | tf_op jit(solution)/shard_map/ppermute | solution.py:42
  58.5 1.3 add_convert_fusion.refs_3_
  59.9 4.9 %shard_map.59 = (bf16[128,1536]{1,0:T(8,128)(2,1)S(1)}, f32[1,128,1536]{2,1,0:T(8,128)}, bf16[1,16,1536]{2,1,0:T(8,128)(2,1)S(1)}, bf16[1,16,1536]{2,1,0:T(8,128...) custom-call(f32[1,256]{1,0:T(1,128)S(1)} %convert_element_type.99.refs_0_, ...), custom_call_target="tpu_custom_call" | custom-call | flops 301989888 | bytes 3884032 | tf_op jit(solution)/shard_map/pallas_call | solution.py:207
  66.7 1.9 %collective-permute-done.9.refs_1_ = bf16[384,1536]{1,0:T(8,128)(2,1)} collective-permute-done((bf16[384,1536]{1,0:T(8,128)(2,1)}, bf16[384,1536]{1,0:T(8,128)(2,1)}, u32[]{:S(2)}, u32[]{:S(2)}) %collective-permute-start.9) | collective-permute-done | bytes 1179680 | tf_op jit(solution)/shard_map/ppermute | solution.py:42
  68.6 3.5 %collective-permute-start.10 = (bf16[1,40,1536]{2,1,0:T(8,128)(2,1)}, bf16[1,40,1536]{2,1,0:T(8,128)(2,1)}, u32[]{:S(2)}, u32[]{:S(2)}) collective-permute-start(bf16[1,40,1536]{2,1,0:T(8,128)(2,1)} %get-tuple-element.25), channel_id=1, source_target_pairs={{2,0},{3,1},{4,2},{5,3},{6,4},{7,5},{8,6},{9,7},{10,8},{11,9},{12,... | collective-permute-start | bytes 368648 | tf_op jit(solution)/shard_map/ppermute | solution.py:42
  72.1 2.9 %shard_map.60 = f32[1,128,1536]{2,1,0:T(8,128)S(1)} custom-call(f32[1,256]{1,0:T(1,128)S(1)} %convert_element_type.99.refs_0_, bf16[384,1536]{1,0:T(8,128)(2,1)} %collective-permute-done.9.refs_1_, bf16[128,1536]{1,0:T(8,128)(2,1)S(1)} %bitcast.99), custom_call_target="tpu_custom_call" | custom-call | flops 201326592 | bytes 2360320 | tf_op jit(solution)/shard_map/pallas_call | solution.py:207
  75.0 1.6 %reshape.167 = bf16[1,20,2,1536]{3,2,1,0:T(2,128)(2,1)} reshape(bf16[1,40,1536]{2,1,0:T(8,128)(2,1)} %collective-permute-done.10) | data formatting | bytes 245760 | tf_op jit(solution)/shard_map/reshape | solution.py:84
  76.6 1.6 %slice_bitcast_fusion.8 = bf16[1,1,16,2,1536]{4,3,2,1,0:T(2,128)(2,1)} fusion(bf16[1,20,2,1536]{3,2,1,0:T(2,128)(2,1)} %reshape.167), kind=kLoop, calls=%fused_computation.41 | loop fusion | bytes 196608 | tf_op jit(solution)/shard_map/stack | solution.py:87
  78.2 1.3 fusion.25
  79.5 1.6 %reshape.168 = bf16[1,20,2,1536]{3,2,1,0:T(2,128)(2,1)} reshape(bf16[1,40,1536]{2,1,0:T(8,128)(2,1)} %collective-permute-done.11) | data formatting | bytes 245760 | tf_op jit(solution)/shard_map/reshape | solution.py:85
  83.7 7.7 %collective-permute-start.14 = (bf16[1,2,12,1536]{3,2,1,0:T(8,128)(2,1)S(1)}, bf16[1,2,12,1536]{3,2,1,0:T(8,128)(2,1)S(1)}, u32[]{:S(2)}, u32[]{:S(2)}) collective-permute-start(bf16[1,2,12,1536]{3,2,1,0:T(8,128)(2,1)S(1)} %pad_maximum_fusion.11), channel_id=1, source_target_pairs={{49,0},{51,2},{53,4},{55,6},{57,8},{59,10},{61,12},{63,14},{65,16}... | collective-permute-start | bytes 221192 | tf_op jit(solution)/shard_map/ppermute | solution.py:42
  92.2 1.3 collective-permute-start.13
  94.7 1.5 %collective-permute-start.12 = (bf16[2,1,16,2,1536]{4,3,2,1,0:T(2,128)(2,1)S(1)}, bf16[2,1,16,2,1536]{4,3,2,1,0:T(2,128)(2,1)S(1)}, u32[]{:S(2)}, u32[]{:S(2)}) collective-permute-start(bf16[2,1,16,2,1536]{4,3,2,1,0:T(2,128)(2,1)S(1)} %pad_maximum_fusion.5), channel_id=1, source_target_pairs={{1,0},{3,2},{5,4},{7,6},{9,8},{11,10},{13,12},{15,14},{17,16},{19,... | collective-permute-start | bytes 589832 | tf_op jit(solution)/shard_map/ppermute | solution.py:42
  96.3 2.9 %collective-permute-done.12 = bf16[2,1,16,2,1536]{4,3,2,1,0:T(2,128)(2,1)S(1)} collective-permute-done((bf16[2,1,16,2,1536]{4,3,2,1,0:T(2,128)(2,1)S(1)}, bf16[2,1,16,2,1536]{4,3,2,1,0:T(2,128)(2,1)S(1)}, u32[]{:S(2)}, u32[]{:S(2)}) %collective-permute-start.12) | collective-permute-done | bytes 196640 | tf_op jit(solution)/shard_map/ppermute | solution.py:42
  99.7 6.0 %shard_map.61 = (bf16[128,1536]{1,0:T(8,128)(2,1)S(1)}, f32[2,128,1536]{2,1,0:T(8,128)S(1)}, bf16[2,16,1536]{2,1,0:T(8,128)(2,1)S(1)}, bf16[2,16,1536]{2,1,0:T(8...) custom-call(f32[1,256]{1,0:T(1,128)S(1)} %convert_element_type.99.refs_0_, ...), custom_call_target="tpu_custom_call" | custom-call | flops 503316480 | bytes 5014528 | tf_op jit(solution)/shard_map/pallas_call | solution.py:207
  106.9 4.0 %collective-permute-start.15 = (bf16[2,40,1536]{2,1,0:T(8,128)(2,1)S(1)}, bf16[2,40,1536]{2,1,0:T(8,128)(2,1)S(1)}, u32[]{:S(2)}, u32[]{:S(2)}) collective-permute-start(bf16[2,40,1536]{2,1,0:T(8,128)(2,1)S(1)} %get-tuple-element.31), channel_id=1, source_target_pairs={{2,0},{3,1},{4,2},{5,3},{6,4},{7,5},{8,6},{9,7},{10,8},{11,9},{12,... | collective-permute-start | bytes 737288 | tf_op jit(solution)/shard_map/ppermute | solution.py:42
  111.7 2.9 %collective-permute-done.15 = bf16[2,40,1536]{2,1,0:T(8,128)(2,1)S(1)} collective-permute-done((bf16[2,40,1536]{2,1,0:T(8,128)(2,1)S(1)}, bf16[2,40,1536]{2,1,0:T(8,128)(2,1)S(1)}, u32[]{:S(2)}, u32[]{:S(2)}) %collective-permute-start.15) | collective-permute-done | bytes 245792 | tf_op jit(solution)/shard_map/ppermute | solution.py:42
  114.9 3.6 %collective-permute-done.16 = bf16[2,40,1536]{2,1,0:T(8,128)(2,1)S(1)} collective-permute-done((bf16[2,40,1536]{2,1,0:T(8,128)(2,1)S(1)}, bf16[2,40,1536]{2,1,0:T(8,128)(2,1)S(1)}, u32[]{:S(2)}, u32[]{:S(2)}) %collective-permute-start.16) | collective-permute-done | bytes 245792 | tf_op jit(solution)/shard_map/ppermute | solution.py:42
  118.9 4.1 %collective-permute-start.18 = (bf16[2,2,12,1536]{3,2,1,0:T(8,128)(2,1)S(1)}, bf16[2,2,12,1536]{3,2,1,0:T(8,128)(2,1)S(1)}, u32[]{:S(2)}, u32[]{:S(2)}) collective-permute-start(bf16[2,2,12,1536]{3,2,1,0:T(8,128)(2,1)S(1)} %pad_maximum_fusion.7), channel_id=1, source_target_pairs={{48,0},{49,1},{50,2},{51,3},{52,4},{53,5},{54,6},{55,7},{56,8},{57... | collective-permute-start | bytes 442376 | tf_op jit(solution)/shard_map/ppermute | solution.py:42
  123.1 1.9 %collective-permute-start.17 = (bf16[2,2,12,1536]{3,2,1,0:T(8,128)(2,1)S(1)}, bf16[2,2,12,1536]{3,2,1,0:T(8,128)(2,1)S(1)}, u32[]{:S(2)}, u32[]{:S(2)}) collective-permute-start(bf16[2,2,12,1536]{3,2,1,0:T(8,128)(2,1)S(1)} %pad_maximum_fusion.6), channel_id=1, source_target_pairs={{0,48},{1,49},{2,50},{3,51},{4,52},{5,53},{6,54},{7,55},{8,56},{9,... | collective-permute-start | bytes 442376 | tf_op jit(solution)/shard_map/ppermute | solution.py:42
  125.0 1.5 %collective-permute-done.18 = bf16[2,2,12,1536]{3,2,1,0:T(8,128)(2,1)S(1)} collective-permute-done((bf16[2,2,12,1536]{3,2,1,0:T(8,128)(2,1)S(1)}, bf16[2,2,12,1536]{3,2,1,0:T(8,128)(2,1)S(1)}, u32[]{:S(2)}, u32[]{:S(2)}) %collective-permute-start.18) | collective-permute-done | bytes 147488 | tf_op jit(solution)/shard_map/ppermute | solution.py:42
  126.5 7.7 %collective-permute-done.17 = bf16[2,2,12,1536]{3,2,1,0:T(8,128)(2,1)S(1)} collective-permute-done((bf16[2,2,12,1536]{3,2,1,0:T(8,128)(2,1)S(1)}, bf16[2,2,12,1536]{3,2,1,0:T(8,128)(2,1)S(1)}, u32[]{:S(2)}, u32[]{:S(2)}) %collective-permute-start.17) | collective-permute-done | bytes 147488 | tf_op jit(solution)/shard_map/ppermute | solution.py:42
  (93 shorter events, 20.4 us)
Async XLA Ops:
  0.6 1.3 copy-start.8
  1.9 8.4 %collective-permute-start.1 = (bf16[2,8,2,1536]{3,1,0,2:T(8,128)(2,1)S(1)}, bf16[2,8,2,1536]{3,1,0,2:T(8,128)(2,1)S(1)}, u32[]{:S(2)}, u32[]{:S(2)}) collective-permute-start(bf16[2,8,2,1536]{3,1,0,2:T(8,128)(2,1)S(1)} %get-tuple-element.41), channel_id=1, source_target_pairs={{48,0},{49,1},{50,2},{51,3},{52,4},{53,5},{54,6},{55,7},{56,8},{57... | collective-permute-start | bytes 294920 | tf_op jit(solution)/shard_map/ppermute | solution.py:42
  8.2 10.1 %collective-permute-start = (bf16[2,8,2,1536]{3,1,0,2:T(8,128)(2,1)S(1)}, bf16[2,8,2,1536]{3,1,0,2:T(8,128)(2,1)S(1)}, u32[]{:S(2)}, u32[]{:S(2)}) collective-permute-start(bf16[2,8,2,1536]{3,1,0,2:T(8,128)(2,1)S(1)} %get-tuple-element.42), channel_id=1, source_target_pairs={{0,48},{1,49},{2,50},{3,51},{4,52},{5,53},{6,54},{7,55},{8,56},{9,... | collective-permute-start | bytes 294920 | tf_op jit(solution)/shard_map/ppermute | solution.py:42
  18.6 17.7 %collective-permute-start.3 = (bf16[20,2,2,1536]{3,1,0,2:T(2,128)(2,1)S(1)}, bf16[20,2,2,1536]{3,1,0,2:T(2,128)(2,1)S(1)}, u32[]{:S(2)}, u32[]{:S(2)}) collective-permute-start(bf16[20,2,2,1536]{3,1,0,2:T(2,128)(2,1)S(1)} %get-tuple-element.37), channel_id=1, source_target_pairs={{2,0},{3,1},{4,2},{5,3},{6,4},{7,5},{8,6},{9,7},{10,8},{11,9},{12,... | collective-permute-start | bytes 737288 | tf_op jit(solution)/shard_map/ppermute | solution.py:42
  29.3 6.8 %collective-permute-start.2 = (bf16[20,2,2,1536]{3,1,0,2:T(2,128)(2,1)S(1)}, bf16[20,2,2,1536]{3,1,0,2:T(2,128)(2,1)S(1)}, u32[]{:S(2)}, u32[]{:S(2)}) collective-permute-start(bf16[20,2,2,1536]{3,1,0,2:T(2,128)(2,1)S(1)} %get-tuple-element.38), channel_id=1, source_target_pairs={{46,0},{47,1},{0,2},{1,3},{2,4},{3,5},{4,6},{5,7},{6,8},{7,9},{8,1... | collective-permute-start | bytes 737288 | tf_op jit(solution)/shard_map/ppermute | solution.py:42
  36.4 1.2 copy-start.7
  38.9 10.6 %collective-permute-start.5 = (bf16[2,8,1536]{2,1,0:T(8,128)(2,1)S(1)}, bf16[2,8,1536]{2,1,0:T(8,128)(2,1)S(1)}, u32[]{:S(2)}, u32[]{:S(2)}) collective-permute-start(bf16[2,8,1536]{2,1,0:T(8,128)(2,1)S(1)} %get-tuple-element.49), channel_id=1, source_target_pairs={{0,49},{2,51},{4,53},{6,55},{8,57},{10,59},{12,61},{14,63},{16,65}... | collective-permute-start | bytes 147464 | tf_op jit(solution)/shard_map/ppermute | solution.py:42
  40.2 10.2 %collective-permute-start.4 = (bf16[16,8,1536]{2,1,0:T(8,128)(2,1)S(1)}, bf16[16,8,1536]{2,1,0:T(8,128)(2,1)S(1)}, u32[]{:S(2)}, u32[]{:S(2)}) collective-permute-start(bf16[16,8,1536]{2,1,0:T(8,128)(2,1)S(1)} %bitcast.100), channel_id=1, source_target_pairs={{0,1},{2,3},{4,5},{6,7},{8,9},{10,11},{12,13},{14,15},{16,17},{18,... | collective-permute-start | bytes 1179656 | tf_op jit(solution)/shard_map/ppermute | solution.py:42
  42.6 7.8 %collective-permute-start.6 = (bf16[2,8,1536]{2,1,0:T(8,128)(2,1)S(1)}, bf16[2,8,1536]{2,1,0:T(8,128)(2,1)S(1)}, u32[]{:S(2)}, u32[]{:S(2)}) collective-permute-start(bf16[2,8,1536]{2,1,0:T(8,128)(2,1)S(1)} %get-tuple-element.48), channel_id=1, source_target_pairs={{48,1},{50,3},{52,5},{54,7},{56,9},{58,11},{60,13},{62,15},{64,17}... | collective-permute-start | bytes 147464 | tf_op jit(solution)/shard_map/ppermute | solution.py:42
  43.9 24.7 %collective-permute-start.9 = (bf16[384,1536]{1,0:T(8,128)(2,1)}, bf16[384,1536]{1,0:T(8,128)(2,1)}, u32[]{:S(2)}, u32[]{:S(2)}) collective-permute-start(bf16[384,1536]{1,0:T(8,128)(2,1)} %pad_maximum_fusion), channel_id=1, source_target_pairs={{1,0},{3,2},{5,4},{7,6},{9,8},{11,10},{13,12},{15,14},{17,16},{19,... | collective-permute-start | bytes 3538952 | tf_op jit(solution)/shard_map/ppermute | solution.py:42
  50.7 4.7 %collective-permute-start.8 = (bf16[20,2,1536]{2,1,0:T(2,128)(2,1)S(1)}, bf16[20,2,1536]{2,1,0:T(2,128)(2,1)S(1)}, u32[]{:S(2)}, u32[]{:S(2)}) collective-permute-start(bf16[20,2,1536]{2,1,0:T(2,128)(2,1)S(1)} %get-tuple-element.46), channel_id=1, source_target_pairs={{2,0},{3,1},{4,2},{5,3},{6,4},{7,5},{8,6},{9,7},{10,8},{11,9},{12,... | collective-permute-start | bytes 368648 | tf_op jit(solution)/shard_map/ppermute | solution.py:42
  52.9 5.5 %collective-permute-start.7 = (bf16[20,2,1536]{2,1,0:T(2,128)(2,1)S(1)}, bf16[20,2,1536]{2,1,0:T(2,128)(2,1)S(1)}, u32[]{:S(2)}, u32[]{:S(2)}) collective-permute-start(bf16[20,2,1536]{2,1,0:T(2,128)(2,1)S(1)} %get-tuple-element.47), channel_id=1, source_target_pairs={{46,0},{47,1},{0,2},{1,3},{2,4},{3,5},{4,6},{5,7},{6,8},{7,9},{8,1... | collective-permute-start | bytes 368648 | tf_op jit(solution)/shard_map/ppermute | solution.py:42
  55.4 4.4 %copy-start = (bf16[16,8,1536]{2,1,0:T(8,128)(2,1)S(1)}, bf16[16,8,1536]{2,1,0:T(8,128)(2,1)}, u32[]{:S(2)}) copy-start(bf16[16,8,1536]{2,1,0:T(8,128)(2,1)} %param.5) | copy-start | bytes 1179652
  64.8 0.7 copy-start.3
  65.5 0.6 copy-start.5
  66.1 0.6 copy-start.6
  68.6 6.4 %collective-permute-start.10 = (bf16[1,40,1536]{2,1,0:T(8,128)(2,1)}, bf16[1,40,1536]{2,1,0:T(8,128)(2,1)}, u32[]{:S(2)}, u32[]{:S(2)}) collective-permute-start(bf16[1,40,1536]{2,1,0:T(8,128)(2,1)} %get-tuple-element.25), channel_id=1, source_target_pairs={{2,0},{3,1},{4,2},{5,3},{6,4},{7,5},{8,6},{9,7},{10,8},{11,9},{12,... | collective-permute-start | bytes 368648 | tf_op jit(solution)/shard_map/ppermute | solution.py:42
  72.1 7.5 %collective-permute-start.11 = (bf16[1,40,1536]{2,1,0:T(8,128)(2,1)}, bf16[1,40,1536]{2,1,0:T(8,128)(2,1)}, u32[]{:S(2)}, u32[]{:S(2)}) collective-permute-start(bf16[1,40,1536]{2,1,0:T(8,128)(2,1)} %get-tuple-element.26), channel_id=1, source_target_pairs={{46,0},{47,1},{0,2},{1,3},{2,4},{3,5},{4,6},{5,7},{6,8},{7,9},{8,1... | collective-permute-start | bytes 368648 | tf_op jit(solution)/shard_map/ppermute | solution.py:42
  83.7 12.5 %collective-permute-start.14 = (bf16[1,2,12,1536]{3,2,1,0:T(8,128)(2,1)S(1)}, bf16[1,2,12,1536]{3,2,1,0:T(8,128)(2,1)S(1)}, u32[]{:S(2)}, u32[]{:S(2)}) collective-permute-start(bf16[1,2,12,1536]{3,2,1,0:T(8,128)(2,1)S(1)} %pad_maximum_fusion.11), channel_id=1, source_target_pairs={{49,0},{51,2},{53,4},{55,6},{57,8},{59,10},{61,12},{63,14},{65,16}... | collective-permute-start | bytes 221192 | tf_op jit(solution)/shard_map/ppermute | solution.py:42
  92.2 4.0 %collective-permute-start.13 = (bf16[1,2,12,1536]{3,2,1,0:T(8,128)(2,1)S(1)}, bf16[1,2,12,1536]{3,2,1,0:T(8,128)(2,1)S(1)}, u32[]{:S(2)}, u32[]{:S(2)}) collective-permute-start(bf16[1,2,12,1536]{3,2,1,0:T(8,128)(2,1)S(1)} %pad_maximum_fusion.10), channel_id=1, source_target_pairs={{1,48},{3,50},{5,52},{7,54},{9,56},{11,58},{13,60},{15,62},{17,64}... | collective-permute-start | bytes 221192 | tf_op jit(solution)/shard_map/ppermute | solution.py:42
  94.7 4.5 %collective-permute-start.12 = (bf16[2,1,16,2,1536]{4,3,2,1,0:T(2,128)(2,1)S(1)}, bf16[2,1,16,2,1536]{4,3,2,1,0:T(2,128)(2,1)S(1)}, u32[]{:S(2)}, u32[]{:S(2)}) collective-permute-start(bf16[2,1,16,2,1536]{4,3,2,1,0:T(2,128)(2,1)S(1)} %pad_maximum_fusion.5), channel_id=1, source_target_pairs={{1,0},{3,2},{5,4},{7,6},{9,8},{11,10},{13,12},{15,14},{17,16},{19,... | collective-permute-start | bytes 589832 | tf_op jit(solution)/shard_map/ppermute | solution.py:42
  99.7 11.2 %copy-start.4 = (bf16[128,1536]{1,0:T(8,128)(2,1)S(1)}, bf16[128,1536]{1,0:T(8,128)(2,1)}, u32[]{:S(2)}) copy-start(bf16[128,1536]{1,0:T(8,128)(2,1)} %copy-done.3) | copy-start | bytes 1179652
  105.8 1.2 copy-start.1
  106.9 7.7 %collective-permute-start.15 = (bf16[2,40,1536]{2,1,0:T(8,128)(2,1)S(1)}, bf16[2,40,1536]{2,1,0:T(8,128)(2,1)S(1)}, u32[]{:S(2)}, u32[]{:S(2)}) collective-permute-start(bf16[2,40,1536]{2,1,0:T(8,128)(2,1)S(1)} %get-tuple-element.31), channel_id=1, source_target_pairs={{2,0},{3,1},{4,2},{5,3},{6,4},{7,5},{8,6},{9,7},{10,8},{11,9},{12,... | collective-permute-start | bytes 737288 | tf_op jit(solution)/shard_map/ppermute | solution.py:42
  111.7 22.6 %copy-start.2 = (f32[2,128,1536]{2,1,0:T(8,128)S(1)}, f32[2,128,1536]{2,1,0:T(8,128)}, u32[]{:S(2)}) copy-start(f32[2,128,1536]{2,1,0:T(8,128)} %copy-done.1) | copy-start | bytes 4718596
  111.7 6.8 %collective-permute-start.16 = (bf16[2,40,1536]{2,1,0:T(8,128)(2,1)S(1)}, bf16[2,40,1536]{2,1,0:T(8,128)(2,1)S(1)}, u32[]{:S(2)}, u32[]{:S(2)}) collective-permute-start(bf16[2,40,1536]{2,1,0:T(8,128)(2,1)S(1)} %get-tuple-element.32), channel_id=1, source_target_pairs={{46,0},{47,1},{0,2},{1,3},{2,4},{3,5},{4,6},{5,7},{6,8},{7,9},{8,1... | collective-permute-start | bytes 737288 | tf_op jit(solution)/shard_map/ppermute | solution.py:42
  118.9 7.6 %collective-permute-start.18 = (bf16[2,2,12,1536]{3,2,1,0:T(8,128)(2,1)S(1)}, bf16[2,2,12,1536]{3,2,1,0:T(8,128)(2,1)S(1)}, u32[]{:S(2)}, u32[]{:S(2)}) collective-permute-start(bf16[2,2,12,1536]{3,2,1,0:T(8,128)(2,1)S(1)} %pad_maximum_fusion.7), channel_id=1, source_target_pairs={{48,0},{49,1},{50,2},{51,3},{52,4},{53,5},{54,6},{55,7},{56,8},{57... | collective-permute-start | bytes 442376 | tf_op jit(solution)/shard_map/ppermute | solution.py:42
  123.1 11.2 %collective-permute-start.17 = (bf16[2,2,12,1536]{3,2,1,0:T(8,128)(2,1)S(1)}, bf16[2,2,12,1536]{3,2,1,0:T(8,128)(2,1)S(1)}, u32[]{:S(2)}, u32[]{:S(2)}) collective-permute-start(bf16[2,2,12,1536]{3,2,1,0:T(8,128)(2,1)S(1)} %pad_maximum_fusion.6), channel_id=1, source_target_pairs={{0,48},{1,49},{2,50},{3,51},{4,52},{5,53},{6,54},{7,55},{8,56},{9,... | collective-permute-start | bytes 442376 | tf_op jit(solution)/shard_map/ppermute | solution.py:42

commit v8 on v7

--- a/solution.py
+++ b/solution.py
@@ -131,6 +131,7 @@
     term_refs = refs
     head_dim = q_ref.shape[1] // HEADS
     nt = (((1,), (1,)), ((), ()))
+    tn = (((0,), (0,)), ((), ()))
 
     def store_terms(res, which, lanes):
         if centre_only:
@@ -164,11 +165,15 @@
             gq_ref[:, lanes] = jnp.dot(
                 dscore.astype(jnp.bfloat16), kh, preferred_element_type=jnp.float32
             ).astype(gq_ref.dtype)
-            kterm = jnp.dot(dscore.T.astype(jnp.bfloat16), qh, preferred_element_type=jnp.float32)
+            kterm = lax.dot_general(
+                dscore.astype(jnp.bfloat16), qh, tn, preferred_element_type=jnp.float32
+            )
             store_terms(kterm, 0, lanes)
         if with_grads or with_vterm:
             dh = d_ref[:, lanes]
-            vterm = jnp.dot(probs.T.astype(jnp.bfloat16), dh, preferred_element_type=jnp.float32)
+            vterm = lax.dot_general(
+                probs.astype(jnp.bfloat16), dh, tn, preferred_element_type=jnp.float32
+            )
             store_terms(vterm, 1 if with_grads else 0, lanes)
         return carry
 

time: 138 us -> 138 us (level)
  no operation moved by 1% of the time
where the time goes in v8:
time: 138 us; the launch traced here: 136 us
  starting transfers between devices  54.5 us (39%)
  waiting for transfers between devices  41.2 us (30%)
  local copies, waits for them, and re-layouts  15.8 us (11%)
  Pallas kernels  15.3 us (11%)
  other arithmetic  8.52 us (6%)
    ppermute x19, starting transfers between devices, shifted(): return lax.ppermute(x, AXES, pairs_from(offset, sizes, src_pipe, dst_pipe))  54.5 us
    ppermute x19, waiting for transfers between devices, shifted(): return lax.ppermute(x, AXES, pairs_from(offset, sizes, src_pipe, dst_pipe))  41.2 us
    pallas_call x4, Pallas kernels, attention(): pl.pallas_call(functools.partial(attention_kernel, scaling, tuple(bounds)...  15.3 us
    unnamed x29, local copies, waits for them, and re-layouts  4.35 us
  transfers between devices with their start and end apart: 19, of which 11 were waited for; matrix products, arithmetic and copies ran while one was open for 8% of the time, Pallas kernels for 6%

profile of v8, /device:TPU:6, one launch (start us, length us, event | category | flops | bytes accessed | tf_op | source)
XLA Modules:
  0.0 136.5 jit_solution(7406634022800925262)
XLA Ops:
  1.9 6.2 %collective-permute-start.1 = (bf16[2,8,2,1536]{3,1,0,2:T(8,128)(2,1)S(1)}, bf16[2,8,2,1536]{3,1,0,2:T(8,128)(2,1)S(1)}, u32[]{:S(2)}, u32[]{:S(2)}) collective-permute-start(bf16[2,8,2,1536]{3,1,0,2:T(8,128)(2,1)S(1)} %get-tuple-element.41), channel_id=1, source_target_pairs={{48,0},{49,1},{50,2},{51,3},{52,4},{53,5},{54,6},{55,7},{56,8},{57... | collective-permute-start | bytes 294920 | tf_op jit(solution)/shard_map/ppermute | solution.py:42
  8.2 1.9 %collective-permute-start = (bf16[2,8,2,1536]{3,1,0,2:T(8,128)(2,1)S(1)}, bf16[2,8,2,1536]{3,1,0,2:T(8,128)(2,1)S(1)}, u32[]{:S(2)}, u32[]{:S(2)}) collective-permute-start(bf16[2,8,2,1536]{3,1,0,2:T(8,128)(2,1)S(1)} %get-tuple-element.42), channel_id=1, source_target_pairs={{0,48},{1,49},{2,50},{3,51},{4,52},{5,53},{6,54},{7,55},{8,56},{9,... | collective-permute-start | bytes 294920 | tf_op jit(solution)/shard_map/ppermute | solution.py:42
  10.3 7.9 %collective-permute-done = bf16[2,8,2,1536]{3,1,0,2:T(8,128)(2,1)S(1)} collective-permute-done((bf16[2,8,2,1536]{3,1,0,2:T(8,128)(2,1)S(1)}, bf16[2,8,2,1536]{3,1,0,2:T(8,128)(2,1)S(1)}, u32[]{:S(2)}, u32[]{:S(2)}) %collective-permute-start) | collective-permute-done | bytes 98336 | tf_op jit(solution)/shard_map/ppermute | solution.py:42
  18.6 10.7 %collective-permute-start.3 = (bf16[20,2,2,1536]{3,1,0,2:T(2,128)(2,1)S(1)}, bf16[20,2,2,1536]{3,1,0,2:T(2,128)(2,1)S(1)}, u32[]{:S(2)}, u32[]{:S(2)}) collective-permute-start(bf16[20,2,2,1536]{3,1,0,2:T(2,128)(2,1)S(1)} %get-tuple-element.37), channel_id=1, source_target_pairs={{2,0},{3,1},{4,2},{5,3},{6,4},{7,5},{8,6},{9,7},{10,8},{11,9},{12,... | collective-permute-start | bytes 737288 | tf_op jit(solution)/shard_map/ppermute | solution.py:42
  29.3 6.8 %collective-permute-done.2 = bf16[20,2,2,1536]{3,1,0,2:T(2,128)(2,1)S(1)} collective-permute-done((bf16[20,2,2,1536]{3,1,0,2:T(2,128)(2,1)S(1)}, bf16[20,2,2,1536]{3,1,0,2:T(2,128)(2,1)S(1)}, u32[]{:S(2)}, u32[]{:S(2)}) %collective-permute-start.2) | collective-permute-done | bytes 245792 | tf_op jit(solution)/shard_map/ppermute | solution.py:42
  37.6 1.3 shard_map.58
  38.9 1.3 collective-permute-start.5
  43.9 5.6 %collective-permute-start.9 = (bf16[384,1536]{1,0:T(8,128)(2,1)}, bf16[384,1536]{1,0:T(8,128)(2,1)}, u32[]{:S(2)}, u32[]{:S(2)}) collective-permute-start(bf16[384,1536]{1,0:T(8,128)(2,1)} %pad_maximum_fusion), channel_id=1, source_target_pairs={{1,0},{3,2},{5,4},{7,6},{9,8},{11,10},{13,12},{15,14},{17,16},{19,... | collective-permute-start | bytes 3538952 | tf_op jit(solution)/shard_map/ppermute | solution.py:42
  50.7 2.2 %collective-permute-start.8 = (bf16[20,2,1536]{2,1,0:T(2,128)(2,1)S(1)}, bf16[20,2,1536]{2,1,0:T(2,128)(2,1)S(1)}, u32[]{:S(2)}, u32[]{:S(2)}) collective-permute-start(bf16[20,2,1536]{2,1,0:T(2,128)(2,1)S(1)} %get-tuple-element.46), channel_id=1, source_target_pairs={{2,0},{3,1},{4,2},{5,3},{6,4},{7,5},{8,6},{9,7},{10,8},{11,9},{12,... | collective-permute-start | bytes 368648 | tf_op jit(solution)/shard_map/ppermute | solution.py:42
  53.0 2.4 %collective-permute-done.8 = bf16[20,2,1536]{2,1,0:T(2,128)(2,1)S(1)} collective-permute-done((bf16[20,2,1536]{2,1,0:T(2,128)(2,1)S(1)}, bf16[20,2,1536]{2,1,0:T(2,128)(2,1)S(1)}, u32[]{:S(2)}, u32[]{:S(2)}) %collective-permute-start.8) | collective-permute-done | bytes 122912 | tf_op jit(solution)/shard_map/ppermute | solution.py:42
  55.4 3.0 %collective-permute-done.7 = bf16[20,2,1536]{2,1,0:T(2,128)(2,1)S(1)} collective-permute-done((bf16[20,2,1536]{2,1,0:T(2,128)(2,1)S(1)}, bf16[20,2,1536]{2,1,0:T(2,128)(2,1)S(1)}, u32[]{:S(2)}, u32[]{:S(2)}) %collective-permute-start.7) | collective-permute-done | bytes 122912 | tf_op jit(solution)/shard_map/ppermute | solution.py:42
  58.5 1.3 add_convert_fusion.refs_3_
  59.9 5.2 %shard_map.59 = (bf16[128,1536]{1,0:T(8,128)(2,1)S(1)}, f32[1,128,1536]{2,1,0:T(8,128)}, bf16[1,16,1536]{2,1,0:T(8,128)(2,1)S(1)}, bf16[1,16,1536]{2,1,0:T(8,128...) custom-call(f32[1,256]{1,0:T(1,128)S(1)} %convert_element_type.99.refs_0_, ...), custom_call_target="tpu_custom_call" | custom-call | flops 301989888 | bytes 3884032 | tf_op jit(solution)/shard_map/pallas_call | solution.py:212
  67.0 1.5 %collective-permute-done.9.refs_1_ = bf16[384,1536]{1,0:T(8,128)(2,1)} collective-permute-done((bf16[384,1536]{1,0:T(8,128)(2,1)}, bf16[384,1536]{1,0:T(8,128)(2,1)}, u32[]{:S(2)}, u32[]{:S(2)}) %collective-permute-start.9) | collective-permute-done | bytes 1179680 | tf_op jit(solution)/shard_map/ppermute | solution.py:42
  68.6 3.5 %collective-permute-start.10 = (bf16[1,40,1536]{2,1,0:T(8,128)(2,1)}, bf16[1,40,1536]{2,1,0:T(8,128)(2,1)}, u32[]{:S(2)}, u32[]{:S(2)}) collective-permute-start(bf16[1,40,1536]{2,1,0:T(8,128)(2,1)} %get-tuple-element.25), channel_id=1, source_target_pairs={{2,0},{3,1},{4,2},{5,3},{6,4},{7,5},{8,6},{9,7},{10,8},{11,9},{12,... | collective-permute-start | bytes 368648 | tf_op jit(solution)/shard_map/ppermute | solution.py:42
  72.1 2.9 %shard_map.60 = f32[1,128,1536]{2,1,0:T(8,128)S(1)} custom-call(f32[1,256]{1,0:T(1,128)S(1)} %convert_element_type.99.refs_0_, bf16[384,1536]{1,0:T(8,128)(2,1)} %collective-permute-done.9.refs_1_, bf16[128,1536]{1,0:T(8,128)(2,1)S(1)} %bitcast.99), custom_call_target="tpu_custom_call" | custom-call | flops 201326592 | bytes 2360320 | tf_op jit(solution)/shard_map/pallas_call | solution.py:212
  75.0 1.6 %reshape.167 = bf16[1,20,2,1536]{3,2,1,0:T(2,128)(2,1)} reshape(bf16[1,40,1536]{2,1,0:T(8,128)(2,1)} %collective-permute-done.10) | data formatting | bytes 245760 | tf_op jit(solution)/shard_map/reshape | solution.py:84
  76.6 1.6 %slice_bitcast_fusion.8 = bf16[1,1,16,2,1536]{4,3,2,1,0:T(2,128)(2,1)} fusion(bf16[1,20,2,1536]{3,2,1,0:T(2,128)(2,1)} %reshape.167), kind=kLoop, calls=%fused_computation.41 | loop fusion | bytes 196608 | tf_op jit(solution)/shard_map/stack | solution.py:87
  78.2 1.3 fusion.25
  79.5 1.6 %reshape.168 = bf16[1,20,2,1536]{3,2,1,0:T(2,128)(2,1)} reshape(bf16[1,40,1536]{2,1,0:T(8,128)(2,1)} %collective-permute-done.11) | data formatting | bytes 245760 | tf_op jit(solution)/shard_map/reshape | solution.py:85
  83.7 7.7 %collective-permute-start.14 = (bf16[1,2,12,1536]{3,2,1,0:T(8,128)(2,1)S(1)}, bf16[1,2,12,1536]{3,2,1,0:T(8,128)(2,1)S(1)}, u32[]{:S(2)}, u32[]{:S(2)}) collective-permute-start(bf16[1,2,12,1536]{3,2,1,0:T(8,128)(2,1)S(1)} %pad_maximum_fusion.11), channel_id=1, source_target_pairs={{49,0},{51,2},{53,4},{55,6},{57,8},{59,10},{61,12},{63,14},{65,16}... | collective-permute-start | bytes 221192 | tf_op jit(solution)/shard_map/ppermute | solution.py:42
  92.3 1.3 collective-permute-start.13
  94.7 1.5 %collective-permute-start.12 = (bf16[2,1,16,2,1536]{4,3,2,1,0:T(2,128)(2,1)S(1)}, bf16[2,1,16,2,1536]{4,3,2,1,0:T(2,128)(2,1)S(1)}, u32[]{:S(2)}, u32[]{:S(2)}) collective-permute-start(bf16[2,1,16,2,1536]{4,3,2,1,0:T(2,128)(2,1)S(1)} %pad_maximum_fusion.5), channel_id=1, source_target_pairs={{1,0},{3,2},{5,4},{7,6},{9,8},{11,10},{13,12},{15,14},{17,16},{19,... | collective-permute-start | bytes 589832 | tf_op jit(solution)/shard_map/ppermute | solution.py:42
  96.3 2.9 %collective-permute-done.12 = bf16[2,1,16,2,1536]{4,3,2,1,0:T(2,128)(2,1)S(1)} collective-permute-done((bf16[2,1,16,2,1536]{4,3,2,1,0:T(2,128)(2,1)S(1)}, bf16[2,1,16,2,1536]{4,3,2,1,0:T(2,128)(2,1)S(1)}, u32[]{:S(2)}, u32[]{:S(2)}) %collective-permute-start.12) | collective-permute-done | bytes 196640 | tf_op jit(solution)/shard_map/ppermute | solution.py:42
  99.7 5.9 %shard_map.61 = (bf16[128,1536]{1,0:T(8,128)(2,1)S(1)}, f32[2,128,1536]{2,1,0:T(8,128)S(1)}, bf16[2,16,1536]{2,1,0:T(8,128)(2,1)S(1)}, bf16[2,16,1536]{2,1,0:T(8...) custom-call(f32[1,256]{1,0:T(1,128)S(1)} %convert_element_type.99.refs_0_, ...), custom_call_target="tpu_custom_call" | custom-call | flops 503316480 | bytes 5014528 | tf_op jit(solution)/shard_map/pallas_call | solution.py:212
  106.8 4.0 %collective-permute-start.15 = (bf16[2,40,1536]{2,1,0:T(8,128)(2,1)S(1)}, bf16[2,40,1536]{2,1,0:T(8,128)(2,1)S(1)}, u32[]{:S(2)}, u32[]{:S(2)}) collective-permute-start(bf16[2,40,1536]{2,1,0:T(8,128)(2,1)S(1)} %get-tuple-element.31), channel_id=1, source_target_pairs={{2,0},{3,1},{4,2},{5,3},{6,4},{7,5},{8,6},{9,7},{10,8},{11,9},{12,... | collective-permute-start | bytes 737288 | tf_op jit(solution)/shard_map/ppermute | solution.py:42
  111.6 2.9 %collective-permute-done.15 = bf16[2,40,1536]{2,1,0:T(8,128)(2,1)S(1)} collective-permute-done((bf16[2,40,1536]{2,1,0:T(8,128)(2,1)S(1)}, bf16[2,40,1536]{2,1,0:T(8,128)(2,1)S(1)}, u32[]{:S(2)}, u32[]{:S(2)}) %collective-permute-start.15) | collective-permute-done | bytes 245792 | tf_op jit(solution)/shard_map/ppermute | solution.py:42
  114.8 3.6 %collective-permute-done.16 = bf16[2,40,1536]{2,1,0:T(8,128)(2,1)S(1)} collective-permute-done((bf16[2,40,1536]{2,1,0:T(8,128)(2,1)S(1)}, bf16[2,40,1536]{2,1,0:T(8,128)(2,1)S(1)}, u32[]{:S(2)}, u32[]{:S(2)}) %collective-permute-start.16) | collective-permute-done | bytes 245792 | tf_op jit(solution)/shard_map/ppermute | solution.py:42
  118.7 4.1 %collective-permute-start.18 = (bf16[2,2,12,1536]{3,2,1,0:T(8,128)(2,1)S(1)}, bf16[2,2,12,1536]{3,2,1,0:T(8,128)(2,1)S(1)}, u32[]{:S(2)}, u32[]{:S(2)}) collective-permute-start(bf16[2,2,12,1536]{3,2,1,0:T(8,128)(2,1)S(1)} %pad_maximum_fusion.7), channel_id=1, source_target_pairs={{48,0},{49,1},{50,2},{51,3},{52,4},{53,5},{54,6},{55,7},{56,8},{57... | collective-permute-start | bytes 442376 | tf_op jit(solution)/shard_map/ppermute | solution.py:42
  122.9 1.9 %collective-permute-start.17 = (bf16[2,2,12,1536]{3,2,1,0:T(8,128)(2,1)S(1)}, bf16[2,2,12,1536]{3,2,1,0:T(8,128)(2,1)S(1)}, u32[]{:S(2)}, u32[]{:S(2)}) collective-permute-start(bf16[2,2,12,1536]{3,2,1,0:T(8,128)(2,1)S(1)} %pad_maximum_fusion.6), channel_id=1, source_target_pairs={{0,48},{1,49},{2,50},{3,51},{4,52},{5,53},{6,54},{7,55},{8,56},{9,... | collective-permute-start | bytes 442376 | tf_op jit(solution)/shard_map/ppermute | solution.py:42
  124.8 1.5 %collective-permute-done.18 = bf16[2,2,12,1536]{3,2,1,0:T(8,128)(2,1)S(1)} collective-permute-done((bf16[2,2,12,1536]{3,2,1,0:T(8,128)(2,1)S(1)}, bf16[2,2,12,1536]{3,2,1,0:T(8,128)(2,1)S(1)}, u32[]{:S(2)}, u32[]{:S(2)}) %collective-permute-start.18) | collective-permute-done | bytes 147488 | tf_op jit(solution)/shard_map/ppermute | solution.py:42
  126.4 7.7 %collective-permute-done.17 = bf16[2,2,12,1536]{3,2,1,0:T(8,128)(2,1)S(1)} collective-permute-done((bf16[2,2,12,1536]{3,2,1,0:T(8,128)(2,1)S(1)}, bf16[2,2,12,1536]{3,2,1,0:T(8,128)(2,1)S(1)}, u32[]{:S(2)}, u32[]{:S(2)}) %collective-permute-start.17) | collective-permute-done | bytes 147488 | tf_op jit(solution)/shard_map/ppermute | solution.py:42
  (93 shorter events, 20.4 us)
Async XLA Ops:
  0.6 1.3 copy-start.8
  1.9 8.4 %collective-permute-start.1 = (bf16[2,8,2,1536]{3,1,0,2:T(8,128)(2,1)S(1)}, bf16[2,8,2,1536]{3,1,0,2:T(8,128)(2,1)S(1)}, u32[]{:S(2)}, u32[]{:S(2)}) collective-permute-start(bf16[2,8,2,1536]{3,1,0,2:T(8,128)(2,1)S(1)} %get-tuple-element.41), channel_id=1, source_target_pairs={{48,0},{49,1},{50,2},{51,3},{52,4},{53,5},{54,6},{55,7},{56,8},{57... | collective-permute-start | bytes 294920 | tf_op jit(solution)/shard_map/ppermute | solution.py:42
  8.2 10.1 %collective-permute-start = (bf16[2,8,2,1536]{3,1,0,2:T(8,128)(2,1)S(1)}, bf16[2,8,2,1536]{3,1,0,2:T(8,128)(2,1)S(1)}, u32[]{:S(2)}, u32[]{:S(2)}) collective-permute-start(bf16[2,8,2,1536]{3,1,0,2:T(8,128)(2,1)S(1)} %get-tuple-element.42), channel_id=1, source_target_pairs={{0,48},{1,49},{2,50},{3,51},{4,52},{5,53},{6,54},{7,55},{8,56},{9,... | collective-permute-start | bytes 294920 | tf_op jit(solution)/shard_map/ppermute | solution.py:42
  18.6 17.7 %collective-permute-start.3 = (bf16[20,2,2,1536]{3,1,0,2:T(2,128)(2,1)S(1)}, bf16[20,2,2,1536]{3,1,0,2:T(2,128)(2,1)S(1)}, u32[]{:S(2)}, u32[]{:S(2)}) collective-permute-start(bf16[20,2,2,1536]{3,1,0,2:T(2,128)(2,1)S(1)} %get-tuple-element.37), channel_id=1, source_target_pairs={{2,0},{3,1},{4,2},{5,3},{6,4},{7,5},{8,6},{9,7},{10,8},{11,9},{12,... | collective-permute-start | bytes 737288 | tf_op jit(solution)/shard_map/ppermute | solution.py:42
  29.3 6.8 %collective-permute-start.2 = (bf16[20,2,2,1536]{3,1,0,2:T(2,128)(2,1)S(1)}, bf16[20,2,2,1536]{3,1,0,2:T(2,128)(2,1)S(1)}, u32[]{:S(2)}, u32[]{:S(2)}) collective-permute-start(bf16[20,2,2,1536]{3,1,0,2:T(2,128)(2,1)S(1)} %get-tuple-element.38), channel_id=1, source_target_pairs={{46,0},{47,1},{0,2},{1,3},{2,4},{3,5},{4,6},{5,7},{6,8},{7,9},{8,1... | collective-permute-start | bytes 737288 | tf_op jit(solution)/shard_map/ppermute | solution.py:42
  36.4 1.2 copy-start.7
  38.9 10.6 %collective-permute-start.5 = (bf16[2,8,1536]{2,1,0:T(8,128)(2,1)S(1)}, bf16[2,8,1536]{2,1,0:T(8,128)(2,1)S(1)}, u32[]{:S(2)}, u32[]{:S(2)}) collective-permute-start(bf16[2,8,1536]{2,1,0:T(8,128)(2,1)S(1)} %get-tuple-element.49), channel_id=1, source_target_pairs={{0,49},{2,51},{4,53},{6,55},{8,57},{10,59},{12,61},{14,63},{16,65}... | collective-permute-start | bytes 147464 | tf_op jit(solution)/shard_map/ppermute | solution.py:42
  40.2 10.2 %collective-permute-start.4 = (bf16[16,8,1536]{2,1,0:T(8,128)(2,1)S(1)}, bf16[16,8,1536]{2,1,0:T(8,128)(2,1)S(1)}, u32[]{:S(2)}, u32[]{:S(2)}) collective-permute-start(bf16[16,8,1536]{2,1,0:T(8,128)(2,1)S(1)} %bitcast.100), channel_id=1, source_target_pairs={{0,1},{2,3},{4,5},{6,7},{8,9},{10,11},{12,13},{14,15},{16,17},{18,... | collective-permute-start | bytes 1179656 | tf_op jit(solution)/shard_map/ppermute | solution.py:42
  42.6 7.8 %collective-permute-start.6 = (bf16[2,8,1536]{2,1,0:T(8,128)(2,1)S(1)}, bf16[2,8,1536]{2,1,0:T(8,128)(2,1)S(1)}, u32[]{:S(2)}, u32[]{:S(2)}) collective-permute-start(bf16[2,8,1536]{2,1,0:T(8,128)(2,1)S(1)} %get-tuple-element.48), channel_id=1, source_target_pairs={{48,1},{50,3},{52,5},{54,7},{56,9},{58,11},{60,13},{62,15},{64,17}... | collective-permute-start | bytes 147464 | tf_op jit(solution)/shard_map/ppermute | solution.py:42
  43.9 24.7 %collective-permute-start.9 = (bf16[384,1536]{1,0:T(8,128)(2,1)}, bf16[384,1536]{1,0:T(8,128)(2,1)}, u32[]{:S(2)}, u32[]{:S(2)}) collective-permute-start(bf16[384,1536]{1,0:T(8,128)(2,1)} %pad_maximum_fusion), channel_id=1, source_target_pairs={{1,0},{3,2},{5,4},{7,6},{9,8},{11,10},{13,12},{15,14},{17,16},{19,... | collective-permute-start | bytes 3538952 | tf_op jit(solution)/shard_map/ppermute | solution.py:42
  50.7 4.7 %collective-permute-start.8 = (bf16[20,2,1536]{2,1,0:T(2,128)(2,1)S(1)}, bf16[20,2,1536]{2,1,0:T(2,128)(2,1)S(1)}, u32[]{:S(2)}, u32[]{:S(2)}) collective-permute-start(bf16[20,2,1536]{2,1,0:T(2,128)(2,1)S(1)} %get-tuple-element.46), channel_id=1, source_target_pairs={{2,0},{3,1},{4,2},{5,3},{6,4},{7,5},{8,6},{9,7},{10,8},{11,9},{12,... | collective-permute-start | bytes 368648 | tf_op jit(solution)/shard_map/ppermute | solution.py:42
  52.9 5.5 %collective-permute-start.7 = (bf16[20,2,1536]{2,1,0:T(2,128)(2,1)S(1)}, bf16[20,2,1536]{2,1,0:T(2,128)(2,1)S(1)}, u32[]{:S(2)}, u32[]{:S(2)}) collective-permute-start(bf16[20,2,1536]{2,1,0:T(2,128)(2,1)S(1)} %get-tuple-element.47), channel_id=1, source_target_pairs={{46,0},{47,1},{0,2},{1,3},{2,4},{3,5},{4,6},{5,7},{6,8},{7,9},{8,1... | collective-permute-start | bytes 368648 | tf_op jit(solution)/shard_map/ppermute | solution.py:42
  55.4 4.4 %copy-start = (bf16[16,8,1536]{2,1,0:T(8,128)(2,1)S(1)}, bf16[16,8,1536]{2,1,0:T(8,128)(2,1)}, u32[]{:S(2)}) copy-start(bf16[16,8,1536]{2,1,0:T(8,128)(2,1)} %param.5) | copy-start | bytes 1179652
  65.1 0.7 copy-start.3
  65.8 0.6 copy-start.5
  66.4 0.6 copy-start.6
  68.6 6.4 %collective-permute-start.10 = (bf16[1,40,1536]{2,1,0:T(8,128)(2,1)}, bf16[1,40,1536]{2,1,0:T(8,128)(2,1)}, u32[]{:S(2)}, u32[]{:S(2)}) collective-permute-start(bf16[1,40,1536]{2,1,0:T(8,128)(2,1)} %get-tuple-element.25), channel_id=1, source_target_pairs={{2,0},{3,1},{4,2},{5,3},{6,4},{7,5},{8,6},{9,7},{10,8},{11,9},{12,... | collective-permute-start | bytes 368648 | tf_op jit(solution)/shard_map/ppermute | solution.py:42
  72.1 7.5 %collective-permute-start.11 = (bf16[1,40,1536]{2,1,0:T(8,128)(2,1)}, bf16[1,40,1536]{2,1,0:T(8,128)(2,1)}, u32[]{:S(2)}, u32[]{:S(2)}) collective-permute-start(bf16[1,40,1536]{2,1,0:T(8,128)(2,1)} %get-tuple-element.26), channel_id=1, source_target_pairs={{46,0},{47,1},{0,2},{1,3},{2,4},{3,5},{4,6},{5,7},{6,8},{7,9},{8,1... | collective-permute-start | bytes 368648 | tf_op jit(solution)/shard_map/ppermute | solution.py:42
  83.7 12.5 %collective-permute-start.14 = (bf16[1,2,12,1536]{3,2,1,0:T(8,128)(2,1)S(1)}, bf16[1,2,12,1536]{3,2,1,0:T(8,128)(2,1)S(1)}, u32[]{:S(2)}, u32[]{:S(2)}) collective-permute-start(bf16[1,2,12,1536]{3,2,1,0:T(8,128)(2,1)S(1)} %pad_maximum_fusion.11), channel_id=1, source_target_pairs={{49,0},{51,2},{53,4},{55,6},{57,8},{59,10},{61,12},{63,14},{65,16}... | collective-permute-start | bytes 221192 | tf_op jit(solution)/shard_map/ppermute | solution.py:42
  92.3 4.0 %collective-permute-start.13 = (bf16[1,2,12,1536]{3,2,1,0:T(8,128)(2,1)S(1)}, bf16[1,2,12,1536]{3,2,1,0:T(8,128)(2,1)S(1)}, u32[]{:S(2)}, u32[]{:S(2)}) collective-permute-start(bf16[1,2,12,1536]{3,2,1,0:T(8,128)(2,1)S(1)} %pad_maximum_fusion.10), channel_id=1, source_target_pairs={{1,48},{3,50},{5,52},{7,54},{9,56},{11,58},{13,60},{15,62},{17,64}... | collective-permute-start | bytes 221192 | tf_op jit(solution)/shard_map/ppermute | solution.py:42
  94.7 4.5 %collective-permute-start.12 = (bf16[2,1,16,2,1536]{4,3,2,1,0:T(2,128)(2,1)S(1)}, bf16[2,1,16,2,1536]{4,3,2,1,0:T(2,128)(2,1)S(1)}, u32[]{:S(2)}, u32[]{:S(2)}) collective-permute-start(bf16[2,1,16,2,1536]{4,3,2,1,0:T(2,128)(2,1)S(1)} %pad_maximum_fusion.5), channel_id=1, source_target_pairs={{1,0},{3,2},{5,4},{7,6},{9,8},{11,10},{13,12},{15,14},{17,16},{19,... | collective-permute-start | bytes 589832 | tf_op jit(solution)/shard_map/ppermute | solution.py:42
  99.7 11.0 %copy-start.4 = (bf16[128,1536]{1,0:T(8,128)(2,1)S(1)}, bf16[128,1536]{1,0:T(8,128)(2,1)}, u32[]{:S(2)}) copy-start(bf16[128,1536]{1,0:T(8,128)(2,1)} %copy-done.3) | copy-start | bytes 1179652
  105.6 1.2 copy-start.1
  106.8 7.7 %collective-permute-start.15 = (bf16[2,40,1536]{2,1,0:T(8,128)(2,1)S(1)}, bf16[2,40,1536]{2,1,0:T(8,128)(2,1)S(1)}, u32[]{:S(2)}, u32[]{:S(2)}) collective-permute-start(bf16[2,40,1536]{2,1,0:T(8,128)(2,1)S(1)} %get-tuple-element.31), channel_id=1, source_target_pairs={{2,0},{3,1},{4,2},{5,3},{6,4},{7,5},{8,6},{9,7},{10,8},{11,9},{12,... | collective-permute-start | bytes 737288 | tf_op jit(solution)/shard_map/ppermute | solution.py:42
  111.6 22.6 %copy-start.2 = (f32[2,128,1536]{2,1,0:T(8,128)S(1)}, f32[2,128,1536]{2,1,0:T(8,128)}, u32[]{:S(2)}) copy-start(f32[2,128,1536]{2,1,0:T(8,128)} %copy-done.1) | copy-start | bytes 4718596
  111.6 6.8 %collective-permute-start.16 = (bf16[2,40,1536]{2,1,0:T(8,128)(2,1)S(1)}, bf16[2,40,1536]{2,1,0:T(8,128)(2,1)S(1)}, u32[]{:S(2)}, u32[]{:S(2)}) collective-permute-start(bf16[2,40,1536]{2,1,0:T(8,128)(2,1)S(1)} %get-tuple-element.32), channel_id=1, source_target_pairs={{46,0},{47,1},{0,2},{1,3},{2,4},{3,5},{4,6},{5,7},{6,8},{7,9},{8,1... | collective-permute-start | bytes 737288 | tf_op jit(solution)/shard_map/ppermute | solution.py:42
  118.7 7.6 %collective-permute-start.18 = (bf16[2,2,12,1536]{3,2,1,0:T(8,128)(2,1)S(1)}, bf16[2,2,12,1536]{3,2,1,0:T(8,128)(2,1)S(1)}, u32[]{:S(2)}, u32[]{:S(2)}) collective-permute-start(bf16[2,2,12,1536]{3,2,1,0:T(8,128)(2,1)S(1)} %pad_maximum_fusion.7), channel_id=1, source_target_pairs={{48,0},{49,1},{50,2},{51,3},{52,4},{53,5},{54,6},{55,7},{56,8},{57... | collective-permute-start | bytes 442376 | tf_op jit(solution)/shard_map/ppermute | solution.py:42
  122.9 11.2 %collective-permute-start.17 = (bf16[2,2,12,1536]{3,2,1,0:T(8,128)(2,1)S(1)}, bf16[2,2,12,1536]{3,2,1,0:T(8,128)(2,1)S(1)}, u32[]{:S(2)}, u32[]{:S(2)}) collective-permute-start(bf16[2,2,12,1536]{3,2,1,0:T(8,128)(2,1)S(1)} %pad_maximum_fusion.6), channel_id=1, source_target_pairs={{0,48},{1,49},{2,50},{3,51},{4,52},{5,53},{6,54},{7,55},{8,56},{9,... | collective-permute-start | bytes 442376 | tf_op jit(solution)/shard_map/ppermute | solution.py:42
